TPU v7x, 128 devices: a whole 4x4x4 slice. The times are simulated.
128 devices in a mesh: leaf: 16 (over x, y), col: 8 (over z, core).
Axes of the slice: x: 4, y: 4, z: 4, core: 2. Of those that a mesh axis runs over, the one named last changes fastest.
Arguments:
- right_side: float32 [31, 2560, 256], P(None, 'leaf'), may hold values from -6 to 6
- reciprocal_pivot_matrix: bfloat16 [31, 2560, 2560], P(None, 'col', 'leaf'), as said below
- panels: bfloat16 [98, 2560, 2560], P(None, 'leaf', 'col'), may hold values from -0.03125 to 0.03125
- parent: int32 [31], replicated, may hold values from 16 to 30, as said below
Outputs:
- solution: float32 [31, 2560, 256], P(None, 'leaf')
Inputs may be any that keep to these rules, and one draw needn't show every extreme that they name: Supernodes 0 to 15 have parents among 16 to 23, 16 to 23 among 24 to 27, 24 to 27 among 28 and 29, 28 and 29 have parent 30, and entry 30 is 30 itself; each supernode of levels 1 to 4 is the parent of exactly two supernodes of the level below. `reciprocal_pivot_matrix`: each block is lower triangular with a positive diagonal.
All inputs are finite; a program needn't handle non-finite values.
Results may differ from a plain program's by a relative error of at most 0.03.
Values may be sent and summed in bfloat16 or wider, within the bound.
No kernel may reach another device: no remote copies, remote signals or barrier semaphores. Data moves between devices by JAX's collectives and lax.ppermute only.
A program may use at most 192 MiB of HBM per device.

v0:
```python
import jax
import jax.numpy as jnp
import numpy as np
from jax import lax
from jax.sharding import PartitionSpec as P

level_starts = (0, 16, 24, 28, 30)
level_counts = (16, 8, 4, 2, 1)


def pair_table():
    sources = []
    distances = []
    for tree_level in range(5):
        for tree_vertex in range(
            level_starts[tree_level], level_starts[tree_level] + level_counts[tree_level]
        ):
            for distance in range(1, 5 - tree_level):
                sources.append(tree_vertex)
                distances.append(distance)
    return (sources, distances)


def node_level(tree_vertex):
    deepest = 0
    for tree_level in range(5):
        if level_starts[tree_level] <= tree_vertex:
            deepest = tree_level
    return deepest


def pair_offset(tree_level):
    initial_position = 0
    for lower in range(tree_level):
        initial_position = initial_position + level_counts[lower] * (4 - lower)
    return initial_position


def pair_ancestors(parent):
    sources, distances = pair_table()
    climbed = [jnp.arange(parent.shape[0], dtype=jnp.int32)]
    for distance in range(4):
        climbed.append(parent[climbed[-1]])
    return jnp.stack(
        [climbed[distance][source_node] for source_node, distance in zip(sources, distances)]
    )


def forward_products(panel_local, forward_stack, ancestor, pair_list, start_node, node_count):
    sources, distances = pair_table()
    chosen = np.array(pair_list, dtype=np.int32)
    feeders = np.array([sources[node_pairing] for node_pairing in pair_list], dtype=np.int32)
    products = jnp.einsum(
        "sjv,svk->sjk",
        panel_local[chosen],
        forward_stack[feeders],
        preferred_element_type=jnp.float32,
    )
    slots = jnp.arange(node_count, dtype=jnp.int32) + start_node
    onehot = (slots[:, None] == ancestor[chosen][None, :]).astype(jnp.float32)
    return jnp.einsum("kp,par->kar", onehot, products, precision=lax.Precision.HIGHEST)


def solve(right_side, diag_local, panel_local, ancestor):
    sources, distances = pair_table()
    node_total = right_side.shape[0]
    load_vector_count = right_side.shape[2]
    col_rows = diag_local.shape[1]
    leaf_rows = diag_local.shape[2]
    forward_stack = jnp.zeros((node_total, col_rows, load_vector_count), jnp.bfloat16)
    forward_levels = [None] * 5
    for tree_level in range(5):
        start_node = level_starts[tree_level]
        node_count = level_counts[tree_level]
        reduced = right_side[start_node : start_node + node_count]
        if tree_level > 0:
            arriving = [
                node_pairing
                for node_pairing in range(len(sources))
                if node_level(sources[node_pairing]) + distances[node_pairing] == tree_level
            ]
            partial_value = forward_products(
                panel_local, forward_stack, ancestor, arriving, start_node, node_count
            )
            reduced = reduced - lax.psum(partial_value.astype(jnp.bfloat16), "col").astype(
                jnp.float32
            )
        division_count = jnp.einsum(
            "kcl,klr->kcr",
            diag_local[start_node : start_node + node_count],
            reduced.astype(jnp.bfloat16),
            preferred_element_type=jnp.float32,
        )
        forward_value = lax.psum(division_count.astype(jnp.bfloat16), "leaf").astype(jnp.float32)
        forward_levels[tree_level] = forward_value
        forward_stack = forward_stack.at[start_node : start_node + node_count].set(
            forward_value.astype(jnp.bfloat16)
        )
    solution_stack = jnp.zeros((node_total, leaf_rows, load_vector_count), jnp.bfloat16)
    results = [None] * 5
    for tree_level in (4, 3, 2, 1, 0):
        start_node = level_starts[tree_level]
        node_count = level_counts[tree_level]
        corrected = forward_levels[tree_level]
        if tree_level < 4:
            initial_position = pair_offset(tree_level)
            span_pairs = node_count * (4 - tree_level)
            upper_node = solution_stack[ancestor[initial_position : initial_position + span_pairs]]
            products = jnp.einsum(
                "boj,boh->bjh",
                panel_local[initial_position : initial_position + span_pairs],
                upper_node,
                preferred_element_type=jnp.float32,
            )
            partial_value = jnp.sum(
                products.reshape(node_count, 4 - tree_level, col_rows, load_vector_count), axis=1
            )
            corrected = corrected - lax.psum(partial_value.astype(jnp.bfloat16), "leaf").astype(
                jnp.float32
            )
        division_count = jnp.einsum(
            "kcl,kcr->klr",
            diag_local[start_node : start_node + node_count],
            corrected.astype(jnp.bfloat16),
            preferred_element_type=jnp.float32,
        )
        solution = lax.psum(division_count.astype(jnp.bfloat16), "col").astype(jnp.float32)
        results[tree_level] = solution
        solution_stack = solution_stack.at[start_node : start_node + node_count].set(
            solution.astype(jnp.bfloat16)
        )
    return jnp.concatenate(results, axis=0)


def shards(right_side, reciprocal_pivot_matrix, panels, parent):
    ancestor = pair_ancestors(parent)
    return solve(right_side, reciprocal_pivot_matrix, panels, ancestor)


def solution(mesh):
    return jax.shard_map(
        shards,
        mesh=mesh,
        in_specs=(P(None, "leaf", None), P(None, "col", "leaf"), P(None, "leaf", "col"), P()),
        out_specs=P(None, "leaf", None),
        check_vma=False,
    )
```

profile of v0, /device:TPU:1, one launch (start us, length us, event | category | flops | bytes accessed | tf_op | source)
XLA Modules:
  0.0 1463.8 jit_solution(12247454413178244909)
XLA Ops:
  18.7 62.5 %stack.204 = s32[98]{0:T(128)S(1)} concatenate(s32[1]{0:T(128)} %get-tuple-element.201, s32[1]{0:T(128)} %get-tuple-element.184, s32[1]{0:T(128)} %get-tuple-element.198, s32[1]{0:T(128)} %get-tuple-element.175, s32[1]{0:T(128)} %get-tuple-element.202, s32[1]{0:T(128)} %get-tuple-element.183, s32[1]{0:T(128)} %get-tuple-element.197, s32[1]{0:T(128)} %get-tuple-element.174, ...), dimensions={0} | concatenate | bytes 784 | tf_op jit(solution)/shard_map/stack | solution.py:44
  81.9 5.4 gather_fusion.7
  87.3 19.6 %all-reduce.21.cloned.1.call-done = bf16[16,320,256]{2,1,0:T(8,128)(2,1)} async-done(((bf16[16,320,256]{2,1,0:T(8,128)(2,1)}), bf16[16,320,256]{2,1,0:T(8,128)(2,1)}) %all-reduce.21.cloned.1.call-update) | async-done | bytes 2621456 | tf_op jit(solution)/shard_map/psum | solution.py:94
  122.3 59.4 %all-reduce.23.cloned.1.call-done = bf16[8,160,256]{2,1,0:T(8,128)(2,1)} async-done(((bf16[8,160,256]{2,1,0:T(8,128)(2,1)}), bf16[8,160,256]{2,1,0:T(8,128)(2,1)}) %all-reduce.23.cloned.1.call-update) | async-done | bytes 655376 | tf_op jit(solution)/shard_map/psum | solution.py:85
  185.6 7.2 gather_fusion.10
  193.5 79.2 %all-reduce.25.cloned.1.call-done = bf16[8,320,256]{2,1,0:T(8,128)(2,1)} async-done(((bf16[8,320,256]{2,1,0:T(8,128)(2,1)}), bf16[8,320,256]{2,1,0:T(8,128)(2,1)}) %all-reduce.25.cloned.1.call-update) | async-done | bytes 1310736 | tf_op jit(solution)/shard_map/psum | solution.py:94
  275.1 5.2 gather_fusion.11
  289.0 59.2 %all-reduce.27.cloned.1.call-done = bf16[4,160,256]{2,1,0:T(8,128)(2,1)} async-done(((bf16[4,160,256]{2,1,0:T(8,128)(2,1)}), bf16[4,160,256]{2,1,0:T(8,128)(2,1)}) %all-reduce.27.cloned.1.call-update) | async-done | bytes 327696 | tf_op jit(solution)/shard_map/psum | solution.py:85
  351.5 7.3 gather_fusion.13
  359.5 76.6 %all-reduce.29.cloned.1.call-done = bf16[4,320,256]{2,1,0:T(8,128)(2,1)} async-done(((bf16[4,320,256]{2,1,0:T(8,128)(2,1)}), bf16[4,320,256]{2,1,0:T(8,128)(2,1)}) %all-reduce.29.cloned.1.call-update) | async-done | bytes 655376 | tf_op jit(solution)/shard_map/psum | solution.py:94
  438.1 5.4 gather_fusion.14
  453.3 58.3 %all-reduce.31.cloned.1.call-done = bf16[2,160,256]{2,1,0:T(8,128)(2,1)} async-done(((bf16[2,160,256]{2,1,0:T(8,128)(2,1)}), bf16[2,160,256]{2,1,0:T(8,128)(2,1)}) %all-reduce.31.cloned.1.call-update) | async-done | bytes 163856 | tf_op jit(solution)/shard_map/psum | solution.py:85
  514.1 7.4 gather_fusion.5
  522.3 75.3 %all-reduce.33.cloned.1.call-done = bf16[2,320,256]{2,1,0:T(8,128)(2,1)} async-done(((bf16[2,320,256]{2,1,0:T(8,128)(2,1)}), bf16[2,320,256]{2,1,0:T(8,128)(2,1)}) %all-reduce.33.cloned.1.call-update) | async-done | bytes 327696 | tf_op jit(solution)/shard_map/psum | solution.py:94
  599.3 5.5 gather_fusion.15
  615.1 56.2 %all-reduce.35.cloned.1.call-done = bf16[1,160,256]{2,1,0:T(8,128)(2,1)} async-done(((bf16[1,160,256]{2,1,0:T(8,128)(2,1)}), bf16[1,160,256]{2,1,0:T(8,128)(2,1)}) %all-reduce.35.cloned.1.call-update) | async-done | bytes 81936 | tf_op jit(solution)/shard_map/psum | solution.py:85
  673.4 82.9 %all-reduce.37.cloned.1.call-done = bf16[320,256]{0,1:T(8,128)(2,1)} async-done(((bf16[320,256]{0,1:T(8,128)(2,1)}), bf16[320,256]{0,1:T(8,128)(2,1)}) %all-reduce.37.cloned.1.call-update) | async-done | bytes 163856 | tf_op jit(solution)/shard_map/psum | solution.py:94
  758.2 56.3 %all-reduce.39.cloned.1.call-done = bf16[1,160,256]{2,1,0:T(8,128)(2,1)} async-done(((bf16[1,160,256]{2,1,0:T(8,128)(2,1)}), bf16[1,160,256]{2,1,0:T(8,128)(2,1)}) %all-reduce.39.cloned.1.call-update) | async-done | bytes 81936 | tf_op jit(solution)/shard_map/psum | solution.py:127
  819.0 5.2 stack.213
  824.3 76.6 %all-reduce.41.cloned.1.call-done = bf16[2,320,256]{2,1,0:T(8,128)(2,1)} async-done(((bf16[2,320,256]{2,1,0:T(8,128)(2,1)}), bf16[2,320,256]{2,1,0:T(8,128)(2,1)}) %all-reduce.41.cloned.1.call-update) | async-done | bytes 327696 | tf_op jit(solution)/shard_map/psum | solution.py:118
  903.0 58.4 %all-reduce.43.cloned.1.call-done = bf16[2,160,256]{2,1,0:T(8,128)(2,1)} async-done(((bf16[2,160,256]{2,1,0:T(8,128)(2,1)}), bf16[2,160,256]{2,1,0:T(8,128)(2,1)}) %all-reduce.43.cloned.1.call-update) | async-done | bytes 163856 | tf_op jit(solution)/shard_map/psum | solution.py:127
  967.0 15.4 %stack.238 = s32[24,1]{0,1:T(1,128)S(1)} concatenate(s32[1,1]{0,1:T(1,128)} %bitcast.34, s32[1,1]{0,1:T(1,128)} %bitcast.35, s32[1,1]{0,1:T(1,128)} %bitcast.36, s32[1,1]{0,1:T(1,128)} %bitcast.37, s32[1,1]{0,1:T(1,128)} %bitcast.38, s32[1,1]{0,1:T(1,128)} %bitcast.39, s32[1,1]{0,1:T(1,128)} %bitcast.40, s32[1,1]{0,1:T(1,128)} %bitcast.41, s32[1,1]{0,1:T(1,128)} %bitcast.42, ...), dimensions={0} | concatenate | bytes 192 | tf_op jit(solution)/shard_map/stack | solution.py:44
  982.4 68.7 %all-reduce.45.cloned.1.call-done = bf16[4,320,256]{2,1,0:T(8,128)(2,1)} async-done(((bf16[4,320,256]{2,1,0:T(8,128)(2,1)}), bf16[4,320,256]{2,1,0:T(8,128)(2,1)}) %all-reduce.45.cloned.1.call-update) | async-done | bytes 655376 | tf_op jit(solution)/shard_map/psum | solution.py:118
  1053.7 58.9 %all-reduce.47.cloned.1.call-done = bf16[4,160,256]{2,1,0:T(8,128)(2,1)} async-done(((bf16[4,160,256]{2,1,0:T(8,128)(2,1)}), bf16[4,160,256]{2,1,0:T(8,128)(2,1)}) %all-reduce.47.cloned.1.call-update) | async-done | bytes 327696 | tf_op jit(solution)/shard_map/psum | solution.py:127
  1115.6 6.9 fusion.10
  1122.5 5.3 reduce_sum.32
  1129.0 86.2 %all-reduce.49.cloned.1.call-done = bf16[8,320,256]{2,1,0:T(8,128)(2,1)} async-done(((bf16[8,320,256]{2,1,0:T(8,128)(2,1)}), bf16[8,320,256]{2,1,0:T(8,128)(2,1)}) %all-reduce.49.cloned.1.call-update) | async-done | bytes 1310736 | tf_op jit(solution)/shard_map/psum | solution.py:118
  1218.7 60.3 %all-reduce.51.cloned.1.call-done = bf16[8,160,256]{2,1,0:T(8,128)(2,1)} async-done(((bf16[8,160,256]{2,1,0:T(8,128)(2,1)}), bf16[8,160,256]{2,1,0:T(8,128)(2,1)}) %all-reduce.51.cloned.1.call-update) | async-done | bytes 655376 | tf_op jit(solution)/shard_map/psum | solution.py:127
  1283.3 8.7 bitcast_reduce_fusion
  1292.2 93.4 %all-reduce.53.cloned.1.call-done = bf16[16,320,256]{2,1,0:T(8,128)(2,1)} async-done(((bf16[16,320,256]{2,1,0:T(8,128)(2,1)}), bf16[16,320,256]{2,1,0:T(8,128)(2,1)}) %all-reduce.53.cloned.1.call-update) | async-done | bytes 2621456 | tf_op jit(solution)/shard_map/psum | solution.py:118
  1385.6 5.1 fusion.20
  1390.7 61.5 %all-reduce.55.cloned.1.call-done = bf16[16,160,256]{2,1,0:T(8,128)(2,1)} async-done(((bf16[16,160,256]{2,1,0:T(8,128)(2,1)}), bf16[16,160,256]{2,1,0:T(8,128)(2,1)}) %all-reduce.55.cloned.1.call-update) | async-done | bytes 1310736 | tf_op jit(solution)/shard_map/psum | solution.py:127
  (146 shorter events, 109.6 us)
Async XLA Ops:
  6.5 4.9 copy-start
  6.5 100.4 %all-reduce.21.cloned.1.call-start = ((), (), s32[]{:S(2)}) async-start(), calls=%async_computation | async-start | bytes 5242880 | tf_op jit(solution)/shard_map/psum | solution.py:94
  11.4 170.3 %all-reduce.23.cloned.1.call-start = ((), (), s32[]{:S(2)}) async-start(), calls=%async_computation.1 | async-start | bytes 1310720 | tf_op jit(solution)/shard_map/psum | solution.py:85
  121.2 64.4 %copy-start.10 = (s32[24]{0:T(128)S(1)}, s32[24]{0:T(128)}, u32[]{:S(2)}) copy-start(s32[24]{0:T(128)} %constant.265) | copy-start | bytes 292
  122.2 150.4 %all-reduce.25.cloned.1.call-start = ((), (), s32[]{:S(2)}) async-start(), calls=%async_computation.2 | async-start | bytes 2621440 | tf_op jit(solution)/shard_map/psum | solution.py:94
  185.3 163.0 %all-reduce.27.cloned.1.call-start = ((), (), s32[]{:S(2)}) async-start(), calls=%async_computation.3 | async-start | bytes 655360 | tf_op jit(solution)/shard_map/psum | solution.py:85
  284.6 66.9 %copy-start.9 = (s32[28]{0:T(128)S(1)}, s32[28]{0:T(128)}, u32[]{:S(2)}) copy-start(s32[28]{0:T(128)} %constant.267) | copy-start | bytes 340
  289.0 147.1 %all-reduce.29.cloned.1.call-start = ((), (), s32[]{:S(2)}) async-start(), calls=%async_computation.4 | async-start | bytes 1310720 | tf_op jit(solution)/shard_map/psum | solution.py:94
  350.9 160.8 %all-reduce.31.cloned.1.call-start = ((), (), s32[]{:S(2)}) async-start(), calls=%async_computation.5 | async-start | bytes 327680 | tf_op jit(solution)/shard_map/psum | solution.py:85
  448.2 65.9 %copy-start.8 = (s32[30]{0:T(128)S(1)}, s32[30]{0:T(128)}, u32[]{:S(2)}) copy-start(s32[30]{0:T(128)} %constant.263) | copy-start | bytes 364
  453.3 144.3 %all-reduce.33.cloned.1.call-start = ((), (), s32[]{:S(2)}) async-start(), calls=%async_computation.6 | async-start | bytes 655360 | tf_op jit(solution)/shard_map/psum | solution.py:94
  513.9 157.5 %all-reduce.35.cloned.1.call-start = ((), (), s32[]{:S(2)}) async-start(), calls=%async_computation.7 | async-start | bytes 163840 | tf_op jit(solution)/shard_map/psum | solution.py:85
  614.4 286.5 %copy-start.5 = (bf16[2,320,256]{2,1,0:T(8,128)(2,1)S(1)}, bf16[2,320,256]{2,1,0:T(8,128)(2,1)}, u32[]{:S(2)}) copy-start(bf16[2,320,256]{2,1,0:T(8,128)(2,1)} %all-reduce.33.cloned.1.call-done) | copy-start | bytes 983044
  615.1 141.2 %all-reduce.37.cloned.1.call-start = ((), (), s32[]{:S(2)}) async-start(), calls=%async_computation.8 | async-start | bytes 393216 | tf_op jit(solution)/shard_map/psum | solution.py:94
  673.3 141.1 %all-reduce.39.cloned.1.call-start = ((), (), s32[]{:S(2)}) async-start(), calls=%async_computation.9 | async-start | bytes 163840 | tf_op jit(solution)/shard_map/psum | solution.py:127
  758.1 142.8 %all-reduce.41.cloned.1.call-start = ((), (), s32[]{:S(2)}) async-start(), calls=%async_computation.10 | async-start | bytes 655360 | tf_op jit(solution)/shard_map/psum | solution.py:118
  816.9 234.2 %copy-start.2 = (bf16[4,320,256]{2,1,0:T(8,128)(2,1)S(1)}, bf16[4,320,256]{2,1,0:T(8,128)(2,1)}, u32[]{:S(2)}) copy-start(bf16[4,320,256]{2,1,0:T(8,128)(2,1)} %all-reduce.29.cloned.1.call-done) | copy-start | bytes 1966084
  819.0 142.5 %all-reduce.43.cloned.1.call-start = ((), (), s32[]{:S(2)}) async-start(), calls=%async_computation.11 | async-start | bytes 327680 | tf_op jit(solution)/shard_map/psum | solution.py:127
  903.0 148.1 %all-reduce.45.cloned.1.call-start = ((), (), s32[]{:S(2)}) async-start(), calls=%async_computation.12 | async-start | bytes 1310720 | tf_op jit(solution)/shard_map/psum | solution.py:118
  966.9 145.7 %all-reduce.47.cloned.1.call-start = ((), (), s32[]{:S(2)}) async-start(), calls=%async_computation.13 | async-start | bytes 655360 | tf_op jit(solution)/shard_map/psum | solution.py:127
  1053.4 161.8 %all-reduce.49.cloned.1.call-start = ((), (), s32[]{:S(2)}) async-start(), calls=%async_computation.14 | async-start | bytes 2621440 | tf_op jit(solution)/shard_map/psum | solution.py:118
  1127.8 151.2 %all-reduce.51.cloned.1.call-start = ((), (), s32[]{:S(2)}) async-start(), calls=%async_computation.15 | async-start | bytes 1310720 | tf_op jit(solution)/shard_map/psum | solution.py:127
  1218.6 167.0 %all-reduce.53.cloned.1.call-start = ((), (), s32[]{:S(2)}) async-start(), calls=%async_computation.16 | async-start | bytes 5242880 | tf_op jit(solution)/shard_map/psum | solution.py:118
  1292.1 160.1 %all-reduce.55.cloned.1.call-start = ((), (), s32[]{:S(2)}) async-start(), calls=%async_computation.17 | async-start | bytes 2621440 | tf_op jit(solution)/shard_map/psum | solution.py:127
  1390.7 63.0 %copy-start.3 = (bf16[8,160,256]{2,1,0:T(8,128)(2,1)S(1)}, bf16[8,160,256]{2,1,0:T(8,128)(2,1)}, u32[]{:S(2)}) copy-start(bf16[8,160,256]{2,1,0:T(8,128)(2,1)} %all-reduce.51.cloned.1.call-done) | copy-start | bytes 1966084
  1390.7 63.0 %copy-start.4 = (bf16[4,160,256]{2,1,0:T(8,128)(2,1)S(1)}, bf16[4,160,256]{2,1,0:T(8,128)(2,1)}, u32[]{:S(2)}) copy-start(bf16[4,160,256]{2,1,0:T(8,128)(2,1)} %all-reduce.47.cloned.1.call-done) | copy-start | bytes 983044
  1390.7 63.1 %copy-start.6 = (bf16[2,160,256]{2,1,0:T(8,128)(2,1)S(1)}, bf16[2,160,256]{2,1,0:T(8,128)(2,1)}, u32[]{:S(2)}) copy-start(bf16[2,160,256]{2,1,0:T(8,128)(2,1)} %all-reduce.43.cloned.1.call-done) | copy-start | bytes 491524
  1390.7 63.1 %copy-start.7 = (bf16[1,160,256]{2,1,0:T(8,128)(2,1)S(1)}, bf16[1,160,256]{2,1,0:T(8,128)(2,1)}, u32[]{:S(2)}) copy-start(bf16[1,160,256]{2,1,0:T(8,128)(2,1)} %all-reduce.39.cloned.1.call-done) | copy-start | bytes 245764
  1453.8 3.0 copy-start.1
Sparse Core Ops, SparseCore 0:
  11.5 95.3 all-reduce.20
  122.4 59.3 all-reduce.22
  185.4 87.2 all-reduce.24
  289.1 59.1 all-reduce.26
  351.4 84.6 all-reduce.28
  453.4 58.2 all-reduce.30
  515.2 82.2 all-reduce.32
  615.2 56.1 all-reduce.34
  674.6 81.6 all-reduce.36
  758.4 56.0 all-reduce.38
  819.1 81.7 all-reduce.40
  903.2 58.2 all-reduce.42
  967.0 83.9 all-reduce.44
  1053.5 59.0 all-reduce.46
  1127.9 87.2 all-reduce.48
  1218.7 60.2 all-reduce.50
  1292.2 93.3 all-reduce.52
  1390.8 61.3 all-reduce.54
where the time goes:
time: 1470 us; the launch traced here: 1460 us
  waiting for transfers between devices  1190 us (81%)
  local copies, waits for them, and re-layouts  170 us (12%)
  matrix products  82 us (6%)
    psum x5, waiting for transfers between devices, solve(): lax.psum(division_count.astype(jnp.bfloat16), 'leaf').astype(jnp.float32)  334 us
    psum x4, waiting for transfers between devices, solve(): lax.psum(partial_value.astype(jnp.bfloat16), 'leaf').astype(jnp.float32)  325 us
    psum x5, waiting for transfers between devices, solve(): lax.psum(division_count.astype(jnp.bfloat16), 'col').astype(jnp.float32)  296 us
    psum x4, waiting for transfers between devices, solve(): lax.psum(partial_value.astype(jnp.bfloat16), 'col').astype(jnp.float32)  233 us
    another operation x4, local copies, waits for them, and re-layouts, pair_ancestors(): jnp.stack([climbed[distance][source_node] for source_node, distance in zi...  84.2 us
  transfers between devices with their start and end apart: 18, of which 18 were waited for; matrix products, arithmetic and copies ran while one was open for 8% of the time, Pallas kernels for 0%

commit v1 on v0

v1 whole, which is shorter than its diff:
```python
import jax
import jax.numpy as jnp
import numpy as np
from jax import lax
from jax.sharding import PartitionSpec as P

level_starts = (0, 16, 24, 28, 30)
level_counts = (16, 8, 4, 2, 1)

LEAF_FACTORS = ((1, 4), (4, 4))
COL_FACTORS = ((1, 2), (2, 4))


def pair_offset(tree_level):
    initial_position = 0
    for lower in range(tree_level):
        initial_position = initial_position + level_counts[lower] * (4 - lower)
    return initial_position


def climb_table(parent):
    climbed = [jnp.arange(parent.shape[0], dtype=jnp.int32)]
    for distance in range(4):
        climbed.append(jnp.take(parent, climbed[-1]))
    return climbed


def level_onehot(climbed, source_level, distance):
    start, count = level_starts[source_level], level_counts[source_level]
    target = source_level + distance
    anc = climbed[distance][start : start + count]
    slots = jnp.arange(level_counts[target], dtype=jnp.int32) + level_starts[target]
    return (slots[:, None] == anc[None, :]).astype(jnp.float32)


def pair_slice(panel_local, source_level, distance):
    start = pair_offset(source_level) + distance - 1
    stride = 4 - source_level
    stop = pair_offset(source_level) + level_counts[source_level] * stride
    return panel_local[start:stop:stride]


def ring_perm(n, stride, size, shift):
    perm = []
    for i in range(n):
        g = (i // stride) % size
        perm.append((i, i + (((g + shift) % size) - g) * stride))
    return perm


def group_allreduce(x, axis, n, factors):
    shape = x.shape
    idx = lax.axis_index(axis)
    cur = x.reshape(-1)
    for stride, size in factors:
        g = (idx // stride) % size
        pieces = cur.reshape(size, -1)
        acc = lax.dynamic_index_in_dim(pieces, g, keepdims=False).astype(jnp.float32)
        for shift in range(1, size):
            send = lax.dynamic_index_in_dim(pieces, (g + shift) % size, keepdims=False)
            acc = acc + lax.ppermute(send, axis, ring_perm(n, stride, size, shift)).astype(jnp.float32)
        cur = acc.astype(jnp.bfloat16)
    for stride, size in reversed(factors):
        g = (idx // stride) % size
        got = [cur] + [lax.ppermute(cur, axis, ring_perm(n, stride, size, shift)) for shift in range(1, size)]
        ordered = jnp.stack([got[0]] + [got[size - t] for t in range(1, size)])
        cur = jnp.roll(ordered, g, axis=0).reshape(-1)
    return cur.reshape(shape)


def solve(right_side, diag_local, panel_local, parent):
    climbed = climb_table(parent)
    n_leaf = 16
    n_col = 8
    forward_levels = [None] * 5
    forward_half = [None] * 5
    for tree_level in range(5):
        start_node = level_starts[tree_level]
        node_count = level_counts[tree_level]
        reduced = right_side[start_node : start_node + node_count]
        if tree_level > 0:
            partial_value = None
            for source_level in range(tree_level):
                distance = tree_level - source_level
                products = jnp.einsum(
                    "sjv,svk->sjk",
                    pair_slice(panel_local, source_level, distance),
                    forward_half[source_level],
                    preferred_element_type=jnp.float32,
                )
                onehot = level_onehot(climbed, source_level, distance)
                term = jnp.einsum("ks,sjr->kjr", onehot, products, precision=lax.Precision.HIGHEST)
                partial_value = term if partial_value is None else partial_value + term
            reduced = reduced - group_allreduce(
                partial_value.astype(jnp.bfloat16), "col", n_col, COL_FACTORS
            ).astype(jnp.float32)
        division_count = jnp.einsum(
            "kcl,klr->kcr",
            diag_local[start_node : start_node + node_count],
            reduced.astype(jnp.bfloat16),
            preferred_element_type=jnp.float32,
        )
        forward_value = group_allreduce(
            division_count.astype(jnp.bfloat16), "leaf", n_leaf, LEAF_FACTORS
        )
        forward_levels[tree_level] = forward_value.astype(jnp.float32)
        forward_half[tree_level] = forward_value
    solution_half = [None] * 5
    results = [None] * 5
    for tree_level in (4, 3, 2, 1, 0):
        start_node = level_starts[tree_level]
        node_count = level_counts[tree_level]
        corrected = forward_levels[tree_level]
        if tree_level < 4:
            partial_value = None
            for distance in range(1, 5 - tree_level):
                onehot = level_onehot(climbed, tree_level, distance)
                upper_node = jnp.einsum(
                    "ks,kjr->sjr",
                    onehot,
                    solution_half[tree_level + distance].astype(jnp.float32),
                    precision=lax.Precision.HIGHEST,
                ).astype(jnp.bfloat16)
                term = jnp.einsum(
                    "boj,boh->bjh",
                    pair_slice(panel_local, tree_level, distance),
                    upper_node,
                    preferred_element_type=jnp.float32,
                )
                partial_value = term if partial_value is None else partial_value + term
            corrected = corrected - group_allreduce(
                partial_value.astype(jnp.bfloat16), "leaf", n_leaf, LEAF_FACTORS
            ).astype(jnp.float32)
        division_count = jnp.einsum(
            "kcl,kcr->klr",
            diag_local[start_node : start_node + node_count],
            corrected.astype(jnp.bfloat16),
            preferred_element_type=jnp.float32,
        )
        solution = group_allreduce(division_count.astype(jnp.bfloat16), "col", n_col, COL_FACTORS)
        results[tree_level] = solution.astype(jnp.float32)
        solution_half[tree_level] = solution
    return jnp.concatenate(results, axis=0)


def solution(mesh):
    return jax.shard_map(
        solve,
        mesh=mesh,
        in_specs=(P(None, "leaf", None), P(None, "col", "leaf"), P(None, "leaf", "col"), P()),
        out_specs=P(None, "leaf", None),
        check_vma=False,
    )
```

time: 1470 us -> 1210 us (0.82)
  waiting for transfers between devices: 1190 us -> 246 us
  other arithmetic: 8.48 us -> 409 us
  starting transfers between devices: 1.91 us -> 278 us
  matrix products: 82 us -> 109 us
    psum x18 -> x0, waiting for transfers between devices: 1190 us -> none  [the longest x5 334 us: solve(): lax.psum(division_count.astype(jnp.bfloat16), 'leaf').astype(jnp.float32)]
    ppermute x0 -> x180, starting transfers between devices: none -> 278 us  [the longest x90 161 us: group_allreduce(): lax.ppermute(send, axis, ring_perm(n, stride, size, shift))]
    ppermute x0 -> x180, waiting for transfers between devices: none -> 246 us  [the longest x90 176 us: group_allreduce(): lax.ppermute(send, axis, ring_perm(n, stride, size, shift))]
    dynamic_slice x0 -> x36, other arithmetic: none -> 124 us  [group_allreduce(): send = lax.dynamic_index_in_dim(pieces, (g + shift) % size, keepdims=False)]
    unnamed x0 -> x37, other arithmetic: none -> 108 us
    concatenate x0 -> x10, other arithmetic: none -> 87.5 us  [group_allreduce(): cur = jnp.roll(ordered, g, axis=0).reshape(-1)]
    convert_element_type x0 -> x45, other arithmetic: none -> 85.5 us  [the longest x4 62.4 us: solve(): corrected = corrected - group_allreduce(partial_value.astype(jnp.bfloat16...]
    gather x20 -> x4, local copies, waits for them, and re-layouts: 61.5 us -> 2.79 us  [climb_table(): climbed.append(jnp.take(parent, climbed[-1]))]
  transfers between devices with their start and end apart: 18 -> 180, of which waited for: 18 -> 117; matrix products, arithmetic and copies ran while one was open for 8% -> 12% of each run, Pallas kernels for 0% -> 0%
where the time goes in v1:
time: 1210 us; the launch traced here: 1200 us
  other arithmetic  409 us (34%)
  starting transfers between devices  278 us (23%)
  waiting for transfers between devices  246 us (20%)
  local copies, waits for them, and re-layouts  156 us (13%)
  matrix products  109 us (9%)
    ppermute x90, waiting for transfers between devices, group_allreduce(): lax.ppermute(send, axis, ring_perm(n, stride, size, shift))  176 us
    ppermute x90, starting transfers between devices, group_allreduce(): lax.ppermute(send, axis, ring_perm(n, stride, size, shift))  161 us
    dynamic_slice x36, other arithmetic, group_allreduce(): send = lax.dynamic_index_in_dim(pieces, (g + shift) % size, keepdims=False)  124 us
    ppermute x90, starting transfers between devices, group_allreduce(): lax.ppermute(cur, axis, ring_perm(n, stride, size, shift))  117 us
    unnamed x37, other arithmetic  108 us
    concatenate x10, other arithmetic, group_allreduce(): cur = jnp.roll(ordered, g, axis=0).reshape(-1)  87.5 us
    ppermute x90, waiting for transfers between devices, group_allreduce(): lax.ppermute(cur, axis, ring_perm(n, stride, size, shift))  70.2 us
    another operation x108, local copies, waits for them, and re-layouts, group_allreduce(): ordered = jnp.stack([got[0]] + [got[size - t] for t in range(1, size)])  63.3 us
  transfers between devices with their start and end apart: 180, of which 117 were waited for; matrix products, arithmetic and copies ran while one was open for 12% of the time, Pallas kernels for 0%

profile of v1, /device:TPU:1, one launch (start us, length us, event | category | flops | bytes accessed | tf_op | source)
XLA Modules:
  0.0 1201.3 jit_solution(11168247630704791749)
XLA Ops:
  8.6 17.0 %dynamic-slice_reduce_fusion.6 = (bf16[327680]{0:T(1024)(128)(2,1)}, bf16[327680]{0:T(1024)(128)(2,1)}, bf16[327680]{0:T(1024)(128)(2,1)S(1)}, f32[1,327680]{1,0:T(1,128)}) fusion(bf16[4,327680]{1,0:T(4,128)(2,1)S(1)} %reshape_reshape.86, s32[]{:T(128)S(6)} %select_n.697, s32[]{:T(128)S(6)} %select_n.701, s32[]{:T(128)S(6)} %select_n.699, s32[]{:T(128)S(6)} %select_n.695), kind=kLoop, calls=%fused_computation.198 | loop fusion | flops 327680 | bytes 5898256 | tf_op jit(solution)/shard_map/jit(dynamic_index_in_dim)/dynamic_slice | solution.py:60
  31.3 12.4 %collective-permute-done = bf16[327680]{0:T(1024)(128)(2,1)S(1)} collective-permute-done((bf16[327680]{0:T(1024)(128)(2,1)}, bf16[327680]{0:T(1024)(128)(2,1)S(1)}, u32[]{:S(2)}, u32[]{:S(2)}) %collective-permute-start) | collective-permute-done | bytes 655392 | tf_op jit(solution)/shard_map/ppermute | solution.py:61
  43.7 15.1 %collective-permute-done.1 = bf16[327680]{0:T(1024)(128)(2,1)S(1)} collective-permute-done((bf16[327680]{0:T(1024)(128)(2,1)S(1)}, bf16[327680]{0:T(1024)(128)(2,1)S(1)}, u32[]{:S(2)}, u32[]{:S(2)}) %collective-permute-start.1) | collective-permute-done | bytes 655392 | tf_op jit(solution)/shard_map/ppermute | solution.py:61
  82.6 8.2 fusion.516
  93.9 8.1 fusion.517
  106.5 7.5 stack.437
  117.1 7.5 stack.436
  124.6 7.7 stack.435
  132.3 32.5 %fusion.13 = bf16[4,327680]{1,0:T(4,128)(2,1)} fusion(s32[]{:T(128)S(6)} %select_n.783, bf16[1,327680]{1,0:T(2,128)(2,1)S(1)} %bitcast.330, bf16[1,327680]{1,0:T(2,128)(2,1)S(1)} %stack.435, bf16[1,327680]{1,0:T(2,128)(2,1)S(1)} %stack.436, bf16[1,327680]{1,0:T(2,128)(2,1)S(1)} %stack.437), kind=kLoop, calls=%fused_computation.35 | loop fusion | flops 20971520 | bytes 5242884 | tf_op jit(solution)/shard_map/jit(_roll_dynamic)/concatenate | solution.py:67
  182.8 13.8 %collective-permute-start.12 = (bf16[163840]{0:T(1024)(128)(2,1)}, bf16[163840]{0:T(1024)(128)(2,1)S(1)}, u32[]{:S(2)}, u32[]{:S(2)}) collective-permute-start(bf16[163840]{0:T(1024)(128)(2,1)} %get-tuple-element.114), channel_id=1, source_target_pairs={{0,1},{1,0},{2,3},{3,2},{4,5},{5,4},{6,7},{7,6},{8,9},{9,8},{10,11... | collective-permute-start | bytes 983048 | tf_op jit(solution)/shard_map/ppermute | solution.py:61
  245.8 11.2 dynamic-slice_reduce_fusion.13
  260.9 13.9 %collective-permute-done.20 = bf16[163840]{0:T(1024)(128)(2,1)} collective-permute-done((bf16[163840]{0:T(1024)(128)(2,1)}, bf16[163840]{0:T(1024)(128)(2,1)}, u32[]{:S(2)}, u32[]{:S(2)}) %collective-permute-start.20) | collective-permute-done | bytes 327712 | tf_op jit(solution)/shard_map/ppermute | solution.py:61
  313.5 16.4 %fusion.63 = bf16[4,163840]{1,0:T(4,128)(2,1)} fusion(s32[]{:T(128)S(6)} %select_n.783, bf16[1,163840]{1,0:T(2,128)(2,1)S(1)} %bitcast.339, bf16[1,163840]{1,0:T(2,128)(2,1)S(1)} %stack.451, bf16[1,163840]{1,0:T(2,128)(2,1)S(1)} %stack.452, bf16[1,163840]{1,0:T(2,128)(2,1)S(1)} %stack.453), kind=kLoop, calls=%fused_computation.120 | loop fusion | flops 10485760 | bytes 2621444 | tf_op jit(solution)/shard_map/jit(_roll_dynamic)/concatenate | solution.py:67
  409.4 8.0 fusion.141
  706.2 8.0 fusion.134
  761.6 10.5 dynamic-slice_reduce_fusion.10
  828.6 16.6 %fusion.56 = f32[4,163840]{1,0:T(4,128)} fusion(s32[]{:T(128)S(6)} %select_n.783, bf16[1,163840]{1,0:T(2,128)(2,1)S(1)} %bitcast.343, bf16[1,163840]{1,0:T(2,128)(2,1)S(1)} %stack.547, bf16[1,163840]{1,0:T(2,128)(2,1)S(1)} %stack.548, bf16[1,163840]{1,0:T(2,128)(2,1)S(1)} %stack.549), kind=kLoop, calls=%fused_computation.113 | loop fusion | flops 10485760 | bytes 3932164 | tf_op jit(solution)/shard_map/convert_element_type | solution.py:133
  923.7 18.8 %dynamic-slice_reduce_fusion.3 = (bf16[327680]{0:T(1024)(128)(2,1)S(1)}, bf16[327680]{0:T(1024)(128)(2,1)S(1)}, bf16[327680]{0:T(1024)(128)(2,1)S(1)}, f32[1,327680]{1,0:T(1,128)S(1)}) fusion(bf16[4,327680]{1,0:T(4,128)(2,1)} %reshape_reshape.109, s32[]{:T(128)S(6)} %select_n.697, s32[]{:T(128)S(6)} %select_n.701, s32[]{:T(128)S(6)} %select_n.699, ...), kind=kLoop, calls=%fused_computation.189 | loop fusion | flops 327680 | bytes 5898256 | tf_op jit(solution)/shard_map/jit(dynamic_index_in_dim)/dynamic_slice | solution.py:60
  946.0 14.1 %collective-permute-done.160 = bf16[327680]{0:T(1024)(128)(2,1)S(1)} collective-permute-done((bf16[327680]{0:T(1024)(128)(2,1)S(1)}, bf16[327680]{0:T(1024)(128)(2,1)S(1)}, u32[]{:S(2)}, u32[]{:S(2)}) %collective-permute-start.160) | collective-permute-done | bytes 655392 | tf_op jit(solution)/shard_map/ppermute | solution.py:61
  960.1 12.8 %collective-permute-done.162 = bf16[327680]{0:T(1024)(128)(2,1)S(1)} collective-permute-done((bf16[327680]{0:T(1024)(128)(2,1)S(1)}, bf16[327680]{0:T(1024)(128)(2,1)S(1)}, u32[]{:S(2)}, u32[]{:S(2)}) %collective-permute-start.162) | collective-permute-done | bytes 655392 | tf_op jit(solution)/shard_map/ppermute | solution.py:61
  1003.7 8.2 fusion.484
  1015.2 8.1 fusion.485
  1027.4 7.5 stack.565
  1048.2 7.7 stack.563
  1055.9 33.0 %fusion.6 = f32[4,327680]{1,0:T(4,128)} fusion(s32[]{:T(128)S(6)} %select_n.783, bf16[1,327680]{1,0:T(2,128)(2,1)S(1)} %bitcast.331, bf16[1,327680]{1,0:T(2,128)(2,1)S(1)} %stack.563, bf16[1,327680]{1,0:T(2,128)(2,1)S(1)} %stack.564, bf16[1,327680]{1,0:T(2,128)(2,1)S(1)} %stack.565), kind=kLoop, calls=%fused_computation.28 | loop fusion | flops 20971520 | bytes 7864324 | tf_op jit(solution)/shard_map/convert_element_type | solution.py:133
  1088.9 8.4 reshape.387
  1104.1 12.2 %dynamic-slice_reduce_fusion = (bf16[327680]{0:T(1024)(128)(2,1)S(1)}, f32[1,327680]{1,0:T(1,128)S(1)}) fusion(bf16[2,327680]{1,0:T(2,128)(2,1)S(1)} %reshape_reshape.110, s32[]{:T(128)S(6)} %select_n.714, s32[]{:T(128)S(6)} %select_n.712), kind=kLoop, calls=%fused_computation.184 | loop fusion | flops 327680 | bytes 3276808 | tf_op jit(solution)/shard_map/jit(dynamic_index_in_dim)/dynamic_slice | solution.py:60
  1116.3 11.8 collective-permute-start.172
  1151.6 8.2 fusion.483
  1163.8 8.1 fusion.482
  1173.0 7.5 stack.572
  1180.5 12.0 fusion.51
  (771 shorter events, 805.7 us)
Async XLA Ops:
  25.6 18.1 %collective-permute-start = (bf16[327680]{0:T(1024)(128)(2,1)}, bf16[327680]{0:T(1024)(128)(2,1)S(1)}, u32[]{:S(2)}, u32[]{:S(2)}) collective-permute-start(bf16[327680]{0:T(1024)(128)(2,1)} %get-tuple-element.12), channel_id=1, source_target_pairs={{0,8},{8,16},{16,24},{24,0},{32,40},{40,48},{48,56},{56,32},{64,72... | collective-permute-start | bytes 1966088 | tf_op jit(solution)/shard_map/ppermute | solution.py:61
  27.7 16.0 %collective-permute-start.2 = (bf16[327680]{0:T(1024)(128)(2,1)}, bf16[327680]{0:T(1024)(128)(2,1)S(1)}, u32[]{:S(2)}, u32[]{:S(2)}) collective-permute-start(bf16[327680]{0:T(1024)(128)(2,1)} %get-tuple-element.14), channel_id=1, source_target_pairs={{0,24},{8,0},{16,8},{24,16},{32,56},{40,32},{48,40},{56,48},{64,88... | collective-permute-start | bytes 1966088 | tf_op jit(solution)/shard_map/ppermute | solution.py:61
  29.2 29.6 %collective-permute-start.1 = (bf16[327680]{0:T(1024)(128)(2,1)S(1)}, bf16[327680]{0:T(1024)(128)(2,1)S(1)}, u32[]{:S(2)}, u32[]{:S(2)}) collective-permute-start(bf16[327680]{0:T(1024)(128)(2,1)S(1)} %get-tuple-element.16), channel_id=1, source_target_pairs={{0,16},{8,24},{16,0},{24,8},{32,48},{40,56},{48,32},{56,40},{64,80... | collective-permute-start | bytes 1966088 | tf_op jit(solution)/shard_map/ppermute | solution.py:61
  90.9 15.6 %collective-permute-start.11 = (bf16[327680]{0:T(1024)(128)(2,1)S(1)}, bf16[327680]{0:T(1024)(128)(2,1)S(1)}, u32[]{:S(2)}, u32[]{:S(2)}) collective-permute-start(bf16[327680]{0:T(1024)(128)(2,1)S(1)} %bitcast.361), channel_id=1, source_target_pairs={{0,8},{8,16},{16,24},{24,0},{32,40},{40,48},{48,56},{56,32},{64,72... | collective-permute-start | bytes 1966088 | tf_op jit(solution)/shard_map/ppermute | solution.py:65
  91.0 26.1 %collective-permute-start.10 = (bf16[327680]{0:T(1024)(128)(2,1)S(1)}, bf16[327680]{0:T(1024)(128)(2,1)S(1)}, u32[]{:S(2)}, u32[]{:S(2)}) collective-permute-start(bf16[327680]{0:T(1024)(128)(2,1)S(1)} %bitcast.362), channel_id=1, source_target_pairs={{0,16},{8,24},{16,0},{24,8},{32,48},{40,56},{48,32},{56,40},{64,80... | collective-permute-start | bytes 1966088 | tf_op jit(solution)/shard_map/ppermute | solution.py:65
  92.5 32.1 %collective-permute-start.9 = (bf16[327680]{0:T(1024)(128)(2,1)S(1)}, bf16[327680]{0:T(1024)(128)(2,1)S(1)}, u32[]{:S(2)}, u32[]{:S(2)}) collective-permute-start(bf16[327680]{0:T(1024)(128)(2,1)S(1)} %bitcast.363), channel_id=1, source_target_pairs={{0,24},{8,0},{16,8},{24,16},{32,56},{40,32},{48,40},{56,48},{64,88... | collective-permute-start | bytes 1966088 | tf_op jit(solution)/shard_map/ppermute | solution.py:65
  182.8 15.3 %collective-permute-start.12 = (bf16[163840]{0:T(1024)(128)(2,1)}, bf16[163840]{0:T(1024)(128)(2,1)S(1)}, u32[]{:S(2)}, u32[]{:S(2)}) collective-permute-start(bf16[163840]{0:T(1024)(128)(2,1)} %get-tuple-element.114), channel_id=1, source_target_pairs={{0,1},{1,0},{2,3},{3,2},{4,5},{5,4},{6,7},{7,6},{8,9},{9,8},{10,11... | collective-permute-start | bytes 983048 | tf_op jit(solution)/shard_map/ppermute | solution.py:61
  257.0 17.9 %collective-permute-start.20 = (bf16[163840]{0:T(1024)(128)(2,1)}, bf16[163840]{0:T(1024)(128)(2,1)}, u32[]{:S(2)}, u32[]{:S(2)}) collective-permute-start(bf16[163840]{0:T(1024)(128)(2,1)} %get-tuple-element.24), channel_id=1, source_target_pairs={{0,8},{8,16},{16,24},{24,0},{32,40},{40,48},{48,56},{56,32},{64,72... | collective-permute-start | bytes 983048 | tf_op jit(solution)/shard_map/ppermute | solution.py:61
  257.0 17.9 %collective-permute-start.22 = (bf16[163840]{0:T(1024)(128)(2,1)}, bf16[163840]{0:T(1024)(128)(2,1)}, u32[]{:S(2)}, u32[]{:S(2)}) collective-permute-start(bf16[163840]{0:T(1024)(128)(2,1)} %get-tuple-element.26), channel_id=1, source_target_pairs={{0,24},{8,0},{16,8},{24,16},{32,56},{40,32},{48,40},{56,48},{64,88... | collective-permute-start | bytes 983048 | tf_op jit(solution)/shard_map/ppermute | solution.py:61
  259.6 15.2 %collective-permute-start.21 = (bf16[163840]{0:T(1024)(128)(2,1)}, bf16[163840]{0:T(1024)(128)(2,1)}, u32[]{:S(2)}, u32[]{:S(2)}) collective-permute-start(bf16[163840]{0:T(1024)(128)(2,1)} %get-tuple-element.28), channel_id=1, source_target_pairs={{0,16},{8,24},{16,0},{24,8},{32,48},{40,56},{48,32},{56,40},{64,80... | collective-permute-start | bytes 983048 | tf_op jit(solution)/shard_map/ppermute | solution.py:61
  298.0 13.2 %collective-permute-start.30 = (bf16[163840]{0:T(1024)(128)(2,1)S(1)}, bf16[163840]{0:T(1024)(128)(2,1)S(1)}, u32[]{:S(2)}, u32[]{:S(2)}) collective-permute-start(bf16[163840]{0:T(1024)(128)(2,1)S(1)} %bitcast.378), channel_id=1, source_target_pairs={{0,16},{8,24},{16,0},{24,8},{32,48},{40,56},{48,32},{56,40},{64,80... | collective-permute-start | bytes 983048 | tf_op jit(solution)/shard_map/ppermute | solution.py:65
  300.9 12.2 %collective-permute-start.29 = (bf16[163840]{0:T(1024)(128)(2,1)S(1)}, bf16[163840]{0:T(1024)(128)(2,1)S(1)}, u32[]{:S(2)}, u32[]{:S(2)}) collective-permute-start(bf16[163840]{0:T(1024)(128)(2,1)S(1)} %bitcast.379), channel_id=1, source_target_pairs={{0,24},{8,0},{16,8},{24,16},{32,56},{40,32},{48,40},{56,48},{64,88... | collective-permute-start | bytes 983048 | tf_op jit(solution)/shard_map/ppermute | solution.py:65
  375.0 9.3 collective-permute-start.42
  423.3 10.1 collective-permute-start.52
  631.1 8.3 collective-permute-start.112
  671.1 8.3 collective-permute-start.121
  772.1 10.6 collective-permute-start.140
  772.4 16.1 %collective-permute-start.142 = (bf16[163840]{0:T(1024)(128)(2,1)S(1)}, bf16[163840]{0:T(1024)(128)(2,1)S(1)}, u32[]{:S(2)}, u32[]{:S(2)}) collective-permute-start(bf16[163840]{0:T(1024)(128)(2,1)S(1)} %get-tuple-element.20), channel_id=1, source_target_pairs={{0,24},{8,0},{16,8},{24,16},{32,56},{40,32},{48,40},{56,48},{64,88... | collective-permute-start | bytes 983048 | tf_op jit(solution)/shard_map/ppermute | solution.py:61
  774.9 15.6 %collective-permute-start.141 = (bf16[163840]{0:T(1024)(128)(2,1)S(1)}, bf16[163840]{0:T(1024)(128)(2,1)S(1)}, u32[]{:S(2)}, u32[]{:S(2)}) collective-permute-start(bf16[163840]{0:T(1024)(128)(2,1)S(1)} %get-tuple-element.22), channel_id=1, source_target_pairs={{0,16},{8,24},{16,0},{24,8},{32,48},{40,56},{48,32},{56,40},{64,80... | collective-permute-start | bytes 983048 | tf_op jit(solution)/shard_map/ppermute | solution.py:61
  812.5 12.6 %collective-permute-start.150 = (bf16[163840]{0:T(1024)(128)(2,1)S(1)}, bf16[163840]{0:T(1024)(128)(2,1)S(1)}, u32[]{:S(2)}, u32[]{:S(2)}) collective-permute-start(bf16[163840]{0:T(1024)(128)(2,1)S(1)} %bitcast.381), channel_id=1, source_target_pairs={{0,16},{8,24},{16,0},{24,8},{32,48},{40,56},{48,32},{56,40},{64,80... | collective-permute-start | bytes 983048 | tf_op jit(solution)/shard_map/ppermute | solution.py:65
  814.8 13.5 %collective-permute-start.149 = (bf16[163840]{0:T(1024)(128)(2,1)S(1)}, bf16[163840]{0:T(1024)(128)(2,1)S(1)}, u32[]{:S(2)}, u32[]{:S(2)}) collective-permute-start(bf16[163840]{0:T(1024)(128)(2,1)S(1)} %bitcast.382), channel_id=1, source_target_pairs={{0,24},{8,0},{16,8},{24,16},{32,56},{40,32},{48,40},{56,48},{64,88... | collective-permute-start | bytes 983048 | tf_op jit(solution)/shard_map/ppermute | solution.py:65
  860.7 8.3 collective-permute-start.152
  880.1 8.8 collective-permute-start.158
  880.2 8.8 collective-permute-start.157
  942.5 17.6 %collective-permute-start.160 = (bf16[327680]{0:T(1024)(128)(2,1)S(1)}, bf16[327680]{0:T(1024)(128)(2,1)S(1)}, u32[]{:S(2)}, u32[]{:S(2)}) collective-permute-start(bf16[327680]{0:T(1024)(128)(2,1)S(1)} %get-tuple-element.6), channel_id=1, source_target_pairs={{0,8},{8,16},{16,24},{24,0},{32,40},{40,48},{48,56},{56,32},{64,72... | collective-permute-start | bytes 1966088 | tf_op jit(solution)/shard_map/ppermute | solution.py:61
  942.7 30.3 %collective-permute-start.162 = (bf16[327680]{0:T(1024)(128)(2,1)S(1)}, bf16[327680]{0:T(1024)(128)(2,1)S(1)}, u32[]{:S(2)}, u32[]{:S(2)}) collective-permute-start(bf16[327680]{0:T(1024)(128)(2,1)S(1)} %get-tuple-element.8), channel_id=1, source_target_pairs={{0,24},{8,0},{16,8},{24,16},{32,56},{40,32},{48,40},{56,48},{64,88... | collective-permute-start | bytes 1966088 | tf_op jit(solution)/shard_map/ppermute | solution.py:61
  945.3 29.6 %collective-permute-start.161 = (bf16[327680]{0:T(1024)(128)(2,1)S(1)}, bf16[327680]{0:T(1024)(128)(2,1)S(1)}, u32[]{:S(2)}, u32[]{:S(2)}) collective-permute-start(bf16[327680]{0:T(1024)(128)(2,1)S(1)} %get-tuple-element.10), channel_id=1, source_target_pairs={{0,16},{8,24},{16,0},{24,8},{32,48},{40,56},{48,32},{56,40},{64,80... | collective-permute-start | bytes 1966088 | tf_op jit(solution)/shard_map/ppermute | solution.py:61
  1012.0 15.3 %collective-permute-start.171 = (bf16[327680]{0:T(1024)(128)(2,1)S(1)}, bf16[327680]{0:T(1024)(128)(2,1)S(1)}, u32[]{:S(2)}, u32[]{:S(2)}) collective-permute-start(bf16[327680]{0:T(1024)(128)(2,1)S(1)} %bitcast.358), channel_id=1, source_target_pairs={{0,8},{8,16},{16,24},{24,0},{32,40},{40,48},{48,56},{56,32},{64,72... | collective-permute-start | bytes 1966088 | tf_op jit(solution)/shard_map/ppermute | solution.py:65
  1012.3 28.4 %collective-permute-start.170 = (bf16[327680]{0:T(1024)(128)(2,1)S(1)}, bf16[327680]{0:T(1024)(128)(2,1)S(1)}, u32[]{:S(2)}, u32[]{:S(2)}) collective-permute-start(bf16[327680]{0:T(1024)(128)(2,1)S(1)} %bitcast.359), channel_id=1, source_target_pairs={{0,16},{8,24},{16,0},{24,8},{32,48},{40,56},{48,32},{56,40},{64,80... | collective-permute-start | bytes 1966088 | tf_op jit(solution)/shard_map/ppermute | solution.py:65
  1014.7 33.5 %collective-permute-start.169 = (bf16[327680]{0:T(1024)(128)(2,1)S(1)}, bf16[327680]{0:T(1024)(128)(2,1)S(1)}, u32[]{:S(2)}, u32[]{:S(2)}) collective-permute-start(bf16[327680]{0:T(1024)(128)(2,1)S(1)} %bitcast.360), channel_id=1, source_target_pairs={{0,24},{8,0},{16,8},{24,16},{32,56},{40,32},{48,40},{56,48},{64,88... | collective-permute-start | bytes 1966088 | tf_op jit(solution)/shard_map/ppermute | solution.py:65
  1116.3 13.5 %collective-permute-start.172 = (bf16[327680]{0:T(1024)(128)(2,1)S(1)}, bf16[327680]{0:T(1024)(128)(2,1)S(1)}, u32[]{:S(2)}, u32[]{:S(2)}) collective-permute-start(bf16[327680]{0:T(1024)(128)(2,1)S(1)} %get-tuple-element.104), channel_id=1, source_target_pairs={{0,1},{1,0},{2,3},{3,2},{4,5},{5,4},{6,7},{7,6},{8,9},{9,8},{10,11... | collective-permute-start | bytes 1966088 | tf_op jit(solution)/shard_map/ppermute | solution.py:61
  1159.9 13.1 %collective-permute-start.179 = (bf16[327680]{0:T(1024)(128)(2,1)S(1)}, bf16[327680]{0:T(1024)(128)(2,1)S(1)}, u32[]{:S(2)}, u32[]{:S(2)}) collective-permute-start(bf16[327680]{0:T(1024)(128)(2,1)S(1)} %bitcast.364), channel_id=1, source_target_pairs={{0,1},{1,0},{2,3},{3,2},{4,5},{5,4},{6,7},{7,6},{8,9},{9,8},{10,11... | collective-permute-start | bytes 1966088 | tf_op jit(solution)/shard_map/ppermute | solution.py:65
  (170 other events, 980.3 us)

commit v2 on v1

--- a/solution.py
+++ b/solution.py
@@ -6,9 +6,6 @@
 
 level_starts = (0, 16, 24, 28, 30)
 level_counts = (16, 8, 4, 2, 1)
-
-LEAF_FACTORS = ((1, 4), (4, 4))
-COL_FACTORS = ((1, 2), (2, 4))
 
 
 def pair_offset(tree_level):
@@ -40,32 +37,18 @@
     return panel_local[start:stop:stride]
 
 
-def ring_perm(n, stride, size, shift):
-    perm = []
-    for i in range(n):
-        g = (i // stride) % size
-        perm.append((i, i + (((g + shift) % size) - g) * stride))
-    return perm
+def xor_perm(n, bit):
+    return [(i, i ^ bit) for i in range(n)]
 
 
-def group_allreduce(x, axis, n, factors):
-    shape = x.shape
-    idx = lax.axis_index(axis)
-    cur = x.reshape(-1)
-    for stride, size in factors:
-        g = (idx // stride) % size
-        pieces = cur.reshape(size, -1)
-        acc = lax.dynamic_index_in_dim(pieces, g, keepdims=False).astype(jnp.float32)
-        for shift in range(1, size):
-            send = lax.dynamic_index_in_dim(pieces, (g + shift) % size, keepdims=False)
-            acc = acc + lax.ppermute(send, axis, ring_perm(n, stride, size, shift)).astype(jnp.float32)
-        cur = acc.astype(jnp.bfloat16)
-    for stride, size in reversed(factors):
-        g = (idx // stride) % size
-        got = [cur] + [lax.ppermute(cur, axis, ring_perm(n, stride, size, shift)) for shift in range(1, size)]
-        ordered = jnp.stack([got[0]] + [got[size - t] for t in range(1, size)])
-        cur = jnp.roll(ordered, g, axis=0).reshape(-1)
-    return cur.reshape(shape)
+def group_allreduce(x, axis, n):
+    if x.size * 2 >= (1 << 20):
+        return lax.psum(x, axis)
+    bit = 1
+    while bit < n:
+        x = (x.astype(jnp.float32) + lax.ppermute(x, axis, xor_perm(n, bit)).astype(jnp.float32)).astype(jnp.bfloat16)
+        bit *= 2
+    return x
 
 
 def solve(right_side, diag_local, panel_local, parent):
@@ -92,7 +75,7 @@
                 term = jnp.einsum("ks,sjr->kjr", onehot, products, precision=lax.Precision.HIGHEST)
                 partial_value = term if partial_value is None else partial_value + term
             reduced = reduced - group_allreduce(
-                partial_value.astype(jnp.bfloat16), "col", n_col, COL_FACTORS
+                partial_value.astype(jnp.bfloat16), "col", n_col
             ).astype(jnp.float32)
         division_count = jnp.einsum(
             "kcl,klr->kcr",
@@ -101,7 +84,7 @@
             preferred_element_type=jnp.float32,
         )
         forward_value = group_allreduce(
-            division_count.astype(jnp.bfloat16), "leaf", n_leaf, LEAF_FACTORS
+            division_count.astype(jnp.bfloat16), "leaf", n_leaf
         )
         forward_levels[tree_level] = forward_value.astype(jnp.float32)
         forward_half[tree_level] = forward_value
@@ -129,7 +112,7 @@
                 )
                 partial_value = term if partial_value is None else partial_value + term
             corrected = corrected - group_allreduce(
-                partial_value.astype(jnp.bfloat16), "leaf", n_leaf, LEAF_FACTORS
+                partial_value.astype(jnp.bfloat16), "leaf", n_leaf
             ).astype(jnp.float32)
         division_count = jnp.einsum(
             "kcl,kcr->klr",
@@ -137,7 +120,7 @@
             corrected.astype(jnp.bfloat16),
             preferred_element_type=jnp.float32,
         )
-        solution = group_allreduce(division_count.astype(jnp.bfloat16), "col", n_col, COL_FACTORS)
+        solution = group_allreduce(division_count.astype(jnp.bfloat16), "col", n_col)
         results[tree_level] = solution.astype(jnp.float32)
         solution_half[tree_level] = solution
     return jnp.concatenate(results, axis=0)

time: 1210 us -> 904 us (0.75)
  waiting for transfers between devices: 246 us -> 675 us
  other arithmetic: 409 us -> 11.2 us
  starting transfers between devices: 278 us -> 102 us
  local copies, waits for them, and re-layouts: 156 us -> 5.58 us
  matrix products: 109 us -> 88.3 us
    psum x0 -> x5, waiting for transfers between devices: none -> 418 us  [group_allreduce(): return lax.psum(x, axis)]
    ppermute x180 -> x44, starting transfers between devices: 278 us -> 102 us  [group_allreduce(): lax.ppermute(x, axis, xor_perm(n, bit)).astype(jnp.float32)]
    dynamic_slice x36 -> x0, other arithmetic: 124 us -> none  [group_allreduce(): send = lax.dynamic_index_in_dim(pieces, (g + shift) % size, keepdims=False)]
    unnamed x37 -> x1, other arithmetic: 108 us -> 0.01 us
    another operation x129 -> x0, local copies, waits for them, and re-layouts: 103 us -> none  [the longest x108 63.3 us: group_allreduce(): ordered = jnp.stack([got[0]] + [got[size - t] for t in range(1, size)])]
    concatenate x10 -> x0, other arithmetic: 87.5 us -> none  [group_allreduce(): cur = jnp.roll(ordered, g, axis=0).reshape(-1)]
    convert_element_type x45 -> x38, other arithmetic: 85.5 us -> 7.9 us  [the longest x34 6.03 us: group_allreduce(): (x.astype(jnp.float32) + lax.ppermute(x, axis, xor_perm(n, bit)).astype(j...]
    convert_element_type x10 -> x0, local copies, waits for them, and re-layouts: 25.8 us -> none  [the longest x3 15.8 us: solve(): corrected = corrected - group_allreduce(partial_value.astype(jnp.bfloat16...]
  transfers between devices with their start and end apart: 180 -> 49, of which waited for: 117 -> 48; matrix products, arithmetic and copies ran while one was open for 12% -> 4% of each run, Pallas kernels for 0% -> 0%
where the time goes in v2:
time: 904 us; the launch traced here: 896 us
  waiting for transfers between devices  675 us (75%)
  starting transfers between devices  102 us (11%)
  matrix products  88.3 us (10%)
  between operations  14.4 us (2%)
  other arithmetic  11.2 us (1%)
    psum x5, waiting for transfers between devices, group_allreduce(): return lax.psum(x, axis)  418 us
    ppermute x44, waiting for transfers between devices, group_allreduce(): lax.ppermute(x, axis, xor_perm(n, bit)).astype(jnp.float32)  256 us
    ppermute x44, starting transfers between devices, group_allreduce(): lax.ppermute(x, axis, xor_perm(n, bit)).astype(jnp.float32)  102 us
    dot_general x10, matrix products, solve(): jnp.einsum('boj,boh->bjh', pair_slice(panel_local, tree_level, distance),...  23.9 us
    dot_general x10, matrix products, solve(): jnp.einsum('sjv,svk->sjk', pair_slice(panel_local, source_level, distance...  20.1 us
  transfers between devices with their start and end apart: 49, of which 48 were waited for; matrix products, arithmetic and copies ran while one was open for 4% of the time, Pallas kernels for 0%

profile of v2, /device:TPU:1, one launch (start us, length us, event | category | flops | bytes accessed | tf_op | source)
XLA Modules:
  0.0 896.2 jit_solution(4329852885535143822)
XLA Ops:
  6.5 4.8 convolution_convert_fusion
  12.2 94.8 %all-reduce.6.cloned.1.call-done = bf16[16,320,256]{2,1,0:T(8,128)(2,1)} async-done(((bf16[16,320,256]{2,1,0:T(8,128)(2,1)}), bf16[16,320,256]{2,1,0:T(8,128)(2,1)}) %all-reduce.6.cloned.1.call-update) | async-done | bytes 2621456 | tf_op jit(solution)/shard_map/psum | solution.py:46
  117.1 14.7 %collective-permute-done.1 = bf16[8,160,256]{2,0,1:T(8,128)(2,1)S(1)} collective-permute-done((bf16[8,160,256]{2,0,1:T(8,128)(2,1)S(1)}, bf16[8,160,256]{2,0,1:T(8,128)(2,1)S(1)}, u32[]{:S(2)}, u32[]{:S(2)}) %collective-permute-start.1) | collective-permute-done | bytes 655392 | tf_op jit(solution)/shard_map/ppermute | solution.py:49
  134.9 13.7 %collective-permute-done.2 = bf16[8,160,256]{2,0,1:T(8,128)(2,1)S(1)} collective-permute-done((bf16[8,160,256]{2,0,1:T(8,128)(2,1)S(1)}, bf16[8,160,256]{2,0,1:T(8,128)(2,1)S(1)}, u32[]{:S(2)}, u32[]{:S(2)}) %collective-permute-start.2) | collective-permute-done | bytes 655392 | tf_op jit(solution)/shard_map/ppermute | solution.py:49
  158.4 81.2 %all-reduce.8.cloned.1.call-done = bf16[8,320,256]{2,1,0:T(8,128)(2,1)} async-done(((bf16[8,320,256]{2,1,0:T(8,128)(2,1)}), bf16[8,320,256]{2,1,0:T(8,128)(2,1)}) %all-reduce.8.cloned.1.call-update) | async-done | bytes 1310736 | tf_op jit(solution)/shard_map/psum | solution.py:46
  248.1 7.7 collective-permute-done.4
  258.9 6.6 collective-permute-done.5
  268.6 13.2 %collective-permute-done.6 = bf16[4,320,256]{2,1,0:T(8,128)(2,1)S(1)} collective-permute-done((bf16[4,320,256]{2,1,0:T(8,128)(2,1)S(1)}, bf16[4,320,256]{2,1,0:T(8,128)(2,1)S(1)}, u32[]{:S(2)}, u32[]{:S(2)}) %collective-permute-start.6) | collective-permute-done | bytes 655392 | tf_op jit(solution)/shard_map/ppermute | solution.py:49
  284.2 12.6 %collective-permute-done.7 = bf16[4,320,256]{2,1,0:T(8,128)(2,1)S(1)} collective-permute-done((bf16[4,320,256]{2,1,0:T(8,128)(2,1)S(1)}, bf16[4,320,256]{2,1,0:T(8,128)(2,1)S(1)}, u32[]{:S(2)}, u32[]{:S(2)}) %collective-permute-start.7) | collective-permute-done | bytes 655392 | tf_op jit(solution)/shard_map/ppermute | solution.py:49
  298.8 10.7 %collective-permute-done.8 = bf16[4,320,256]{2,1,0:T(8,128)(2,1)} collective-permute-done((bf16[4,320,256]{2,1,0:T(8,128)(2,1)S(1)}, bf16[4,320,256]{2,1,0:T(8,128)(2,1)}, u32[]{:S(2)}, u32[]{:S(2)}) %collective-permute-start.8) | collective-permute-done | bytes 655392 | tf_op jit(solution)/shard_map/ppermute | solution.py:49
  319.0 5.3 collective-permute-done.9
  329.8 5.9 collective-permute-start.10
  352.5 5.8 collective-permute-done.13
  378.0 5.2 collective-permute-done.16
  385.4 5.1 collective-permute-start.17
  424.4 7.6 collective-permute-start.24
  444.0 6.2 collective-permute-done.27
  452.4 5.6 collective-permute-done.28
  466.5 8.6 collective-permute-done.30
  476.4 5.4 collective-permute-start.31
  498.1 14.1 %collective-permute-done.34 = bf16[4,320,256]{2,1,0:T(8,128)(2,1)S(1)} collective-permute-done((bf16[4,320,256]{2,1,0:T(8,128)(2,1)S(1)}, bf16[4,320,256]{2,1,0:T(8,128)(2,1)S(1)}, u32[]{:S(2)}, u32[]{:S(2)}) %collective-permute-start.34) | collective-permute-done | bytes 655392 | tf_op jit(solution)/shard_map/ppermute | solution.py:49
  514.3 12.8 %collective-permute-done.35 = bf16[4,320,256]{2,1,0:T(8,128)(2,1)S(1)} collective-permute-done((bf16[4,320,256]{2,1,0:T(8,128)(2,1)S(1)}, bf16[4,320,256]{2,1,0:T(8,128)(2,1)S(1)}, u32[]{:S(2)}, u32[]{:S(2)}) %collective-permute-start.35) | collective-permute-done | bytes 655392 | tf_op jit(solution)/shard_map/ppermute | solution.py:49
  528.8 10.8 %collective-permute-done.36 = bf16[4,320,256]{2,1,0:T(8,128)(2,1)S(1)} collective-permute-done((bf16[4,320,256]{2,1,0:T(8,128)(2,1)S(1)}, bf16[4,320,256]{2,1,0:T(8,128)(2,1)S(1)}, u32[]{:S(2)}, u32[]{:S(2)}) %collective-permute-start.36) | collective-permute-done | bytes 655392 | tf_op jit(solution)/shard_map/ppermute | solution.py:49
  542.4 14.4 %collective-permute-done.37 = bf16[4,320,256]{2,1,0:T(8,128)(2,1)S(1)} collective-permute-done((bf16[4,320,256]{2,1,0:T(8,128)(2,1)S(1)}, bf16[4,320,256]{2,1,0:T(8,128)(2,1)S(1)}, u32[]{:S(2)}, u32[]{:S(2)}) %collective-permute-start.37) | collective-permute-done | bytes 655392 | tf_op jit(solution)/shard_map/ppermute | solution.py:49
  558.4 4.8 collective-permute-start.38
  566.2 7.5 collective-permute-done.39
  578.4 4.9 collective-permute-done.40
  588.9 87.8 %all-reduce.10.cloned.1.call-done = bf16[8,320,256]{2,1,0:T(8,128)(2,1)} async-done(((bf16[8,320,256]{2,1,0:T(8,128)(2,1)}), bf16[8,320,256]{2,1,0:T(8,128)(2,1)}) %all-reduce.10.cloned.1.call-update) | async-done | bytes 1310736 | tf_op jit(solution)/shard_map/psum | solution.py:46
  688.3 11.3 %collective-permute-done.42 = bf16[8,160,256]{2,1,0:T(8,128)(2,1)S(1)} collective-permute-done((bf16[8,160,256]{2,1,0:T(8,128)(2,1)S(1)}, bf16[8,160,256]{2,1,0:T(8,128)(2,1)S(1)}, u32[]{:S(2)}, u32[]{:S(2)}) %collective-permute-start.42) | collective-permute-done | bytes 655392 | tf_op jit(solution)/shard_map/ppermute | solution.py:49
  706.1 10.2 %collective-permute-done.43 = bf16[8,160,256]{2,1,0:T(8,128)(2,1)S(1)} collective-permute-done((bf16[8,160,256]{2,1,0:T(8,128)(2,1)S(1)}, bf16[8,160,256]{2,1,0:T(8,128)(2,1)S(1)}, u32[]{:S(2)}, u32[]{:S(2)}) %collective-permute-start.43) | collective-permute-done | bytes 655392 | tf_op jit(solution)/shard_map/ppermute | solution.py:49
  724.6 93.2 %all-reduce.12.cloned.1.call-done = bf16[16,320,256]{2,1,0:T(8,128)(2,1)} async-done(((bf16[16,320,256]{2,1,0:T(8,128)(2,1)}), bf16[16,320,256]{2,1,0:T(8,128)(2,1)}) %all-reduce.12.cloned.1.call-update) | async-done | bytes 2621456 | tf_op jit(solution)/shard_map/psum | solution.py:46
  822.2 61.5 %all-reduce.14.cloned.1.call-done = bf16[16,160,256]{2,1,0:T(8,128)(2,1)} async-done(((bf16[16,160,256]{2,1,0:T(8,128)(2,1)}), bf16[16,160,256]{2,1,0:T(8,128)(2,1)}) %all-reduce.14.cloned.1.call-update) | async-done | bytes 1310736 | tf_op jit(solution)/shard_map/psum | solution.py:46
  (236 shorter events, 227.9 us)
Async XLA Ops:
  6.5 100.4 %all-reduce.6.cloned.1.call-start = ((), (), s32[]{:S(2)}) async-start(), calls=%async_computation | async-start | bytes 5242880 | tf_op jit(solution)/shard_map/psum | solution.py:46
  11.4 228.2 %all-reduce.8.cloned.1.call-start = ((), (), s32[]{:S(2)}) async-start(), calls=%async_computation.1 | async-start | bytes 2621440 | tf_op jit(solution)/shard_map/psum | solution.py:46
  115.7 16.0 %collective-permute-start.1 = (bf16[8,160,256]{2,0,1:T(8,128)(2,1)S(1)}, bf16[8,160,256]{2,0,1:T(8,128)(2,1)S(1)}, u32[]{:S(2)}, u32[]{:S(2)}) collective-permute-start(bf16[8,160,256]{2,0,1:T(8,128)(2,1)S(1)} %add_convert_fusion.15), channel_id=1, source_target_pairs={{0,2},{1,3},{2,0},{3,1},{4,6},{5,7},{6,4},{7,5},{8,10},{9,11},{10,... | collective-permute-start | bytes 1966088 | tf_op jit(solution)/shard_map/ppermute | solution.py:49
  131.9 16.6 %collective-permute-start.2 = (bf16[8,160,256]{2,0,1:T(8,128)(2,1)S(1)}, bf16[8,160,256]{2,0,1:T(8,128)(2,1)S(1)}, u32[]{:S(2)}, u32[]{:S(2)}) collective-permute-start(bf16[8,160,256]{2,0,1:T(8,128)(2,1)S(1)} %add_convert_fusion.14), channel_id=1, source_target_pairs={{0,4},{1,5},{2,6},{3,7},{4,0},{5,1},{6,2},{7,3},{8,12},{9,13},{10,... | collective-permute-start | bytes 1966088 | tf_op jit(solution)/shard_map/ppermute | solution.py:49
  152.5 524.2 %all-reduce.10.cloned.1.call-start = ((), (), s32[]{:S(2)}) async-start(), calls=%async_computation.2 | async-start | bytes 2621440 | tf_op jit(solution)/shard_map/psum | solution.py:46
  246.8 9.0 %collective-permute-start.4 = (bf16[4,160,256]{2,0,1:T(4,128)(2,1)S(1)}, bf16[4,160,256]{2,0,1:T(4,128)(2,1)S(1)}, u32[]{:S(2)}, u32[]{:S(2)}) collective-permute-start(bf16[4,160,256]{2,0,1:T(4,128)(2,1)S(1)} %add_convert_fusion.29), channel_id=1, source_target_pairs={{0,2},{1,3},{2,0},{3,1},{4,6},{5,7},{6,4},{7,5},{8,10},{9,11},{10,... | collective-permute-start | bytes 983048 | tf_op jit(solution)/shard_map/ppermute | solution.py:49
  256.0 9.6 %collective-permute-start.5 = (bf16[4,160,256]{2,0,1:T(4,128)(2,1)S(1)}, bf16[4,160,256]{2,0,1:T(4,128)(2,1)S(1)}, u32[]{:S(2)}, u32[]{:S(2)}) collective-permute-start(bf16[4,160,256]{2,0,1:T(4,128)(2,1)S(1)} %add_convert_fusion.28), channel_id=1, source_target_pairs={{0,4},{1,5},{2,6},{3,7},{4,0},{5,1},{6,2},{7,3},{8,12},{9,13},{10,... | collective-permute-start | bytes 983048 | tf_op jit(solution)/shard_map/ppermute | solution.py:49
  267.6 14.2 %collective-permute-start.6 = (bf16[4,320,256]{2,1,0:T(8,128)(2,1)S(1)}, bf16[4,320,256]{2,1,0:T(8,128)(2,1)S(1)}, u32[]{:S(2)}, u32[]{:S(2)}) collective-permute-start(bf16[4,320,256]{2,1,0:T(8,128)(2,1)S(1)} %fusion.50), channel_id=1, source_target_pairs={{0,8},{8,0},{16,24},{24,16},{32,40},{40,32},{48,56},{56,48},{64,72... | collective-permute-start | bytes 1966088 | tf_op jit(solution)/shard_map/ppermute | solution.py:49
  282.0 14.8 %collective-permute-start.7 = (bf16[4,320,256]{2,1,0:T(8,128)(2,1)S(1)}, bf16[4,320,256]{2,1,0:T(8,128)(2,1)S(1)}, u32[]{:S(2)}, u32[]{:S(2)}) collective-permute-start(bf16[4,320,256]{2,1,0:T(8,128)(2,1)S(1)} %add_convert_fusion.12), channel_id=1, source_target_pairs={{0,16},{8,24},{16,0},{24,8},{32,48},{40,56},{48,32},{56,40},{64,80... | collective-permute-start | bytes 1966088 | tf_op jit(solution)/shard_map/ppermute | solution.py:49
  297.0 12.5 %collective-permute-start.8 = (bf16[4,320,256]{2,1,0:T(8,128)(2,1)S(1)}, bf16[4,320,256]{2,1,0:T(8,128)(2,1)}, u32[]{:S(2)}, u32[]{:S(2)}) collective-permute-start(bf16[4,320,256]{2,1,0:T(8,128)(2,1)S(1)} %add_convert_fusion.11), channel_id=1, source_target_pairs={{0,32},{8,40},{16,48},{24,56},{32,0},{40,8},{48,16},{56,24},{64,96... | collective-permute-start | bytes 1966088 | tf_op jit(solution)/shard_map/ppermute | solution.py:49
  310.9 13.4 %collective-permute-start.9 = (bf16[4,320,256]{2,1,0:T(8,128)(2,1)S(1)}, bf16[4,320,256]{2,1,0:T(8,128)(2,1)S(1)}, u32[]{:S(2)}, u32[]{:S(2)}) collective-permute-start(bf16[4,320,256]{2,1,0:T(8,128)(2,1)S(1)} %add_convert_fusion.10), channel_id=1, source_target_pairs={{0,64},{8,72},{16,80},{24,88},{32,96},{40,104},{48,112},{56,120},{... | collective-permute-start | bytes 1966088 | tf_op jit(solution)/shard_map/ppermute | solution.py:49
  329.8 6.9 collective-permute-start.10
  351.0 7.4 collective-permute-start.13
  359.5 7.7 collective-permute-start.14
  373.5 9.8 %collective-permute-start.16 = (bf16[2,320,256]{2,1,0:T(8,128)(2,1)S(1)}, bf16[2,320,256]{2,1,0:T(8,128)(2,1)S(1)}, u32[]{:S(2)}, u32[]{:S(2)}) collective-permute-start(bf16[2,320,256]{2,1,0:T(8,128)(2,1)S(1)} %add_convert_fusion.24), channel_id=1, source_target_pairs={{0,64},{8,72},{16,80},{24,88},{32,96},{40,104},{48,112},{56,120},{... | collective-permute-start | bytes 983048 | tf_op jit(solution)/shard_map/ppermute | solution.py:49
  405.6 7.6 collective-permute-start.21
  424.4 8.5 collective-permute-start.24
  443.0 7.2 collective-permute-start.27
  450.3 7.7 collective-permute-start.28
  458.1 6.1 collective-permute-start.29
  464.3 10.8 %collective-permute-start.30 = (bf16[2,320,256]{2,1,0:T(8,128)(2,1)S(1)}, bf16[2,320,256]{2,1,0:T(8,128)(2,1)S(1)}, u32[]{:S(2)}, u32[]{:S(2)}) collective-permute-start(bf16[2,320,256]{2,1,0:T(8,128)(2,1)S(1)} %add_convert_fusion.20), channel_id=1, source_target_pairs={{0,64},{8,72},{16,80},{24,88},{32,96},{40,104},{48,112},{56,120},{... | collective-permute-start | bytes 983048 | tf_op jit(solution)/shard_map/ppermute | solution.py:49
  476.4 6.5 collective-permute-start.31
  498.0 14.2 %collective-permute-start.34 = (bf16[4,320,256]{2,1,0:T(8,128)(2,1)S(1)}, bf16[4,320,256]{2,1,0:T(8,128)(2,1)S(1)}, u32[]{:S(2)}, u32[]{:S(2)}) collective-permute-start(bf16[4,320,256]{2,1,0:T(8,128)(2,1)S(1)} %fusion.51), channel_id=1, source_target_pairs={{0,8},{8,0},{16,24},{24,16},{32,40},{40,32},{48,56},{56,48},{64,72... | collective-permute-start | bytes 1966088 | tf_op jit(solution)/shard_map/ppermute | solution.py:49
  512.4 14.8 %collective-permute-start.35 = (bf16[4,320,256]{2,1,0:T(8,128)(2,1)S(1)}, bf16[4,320,256]{2,1,0:T(8,128)(2,1)S(1)}, u32[]{:S(2)}, u32[]{:S(2)}) collective-permute-start(bf16[4,320,256]{2,1,0:T(8,128)(2,1)S(1)} %add_convert_fusion.8), channel_id=1, source_target_pairs={{0,16},{8,24},{16,0},{24,8},{32,48},{40,56},{48,32},{56,40},{64,80... | collective-permute-start | bytes 1966088 | tf_op jit(solution)/shard_map/ppermute | solution.py:49
  527.3 12.3 %collective-permute-start.36 = (bf16[4,320,256]{2,1,0:T(8,128)(2,1)S(1)}, bf16[4,320,256]{2,1,0:T(8,128)(2,1)S(1)}, u32[]{:S(2)}, u32[]{:S(2)}) collective-permute-start(bf16[4,320,256]{2,1,0:T(8,128)(2,1)S(1)} %add_convert_fusion.7), channel_id=1, source_target_pairs={{0,32},{8,40},{16,48},{24,56},{32,0},{40,8},{48,16},{56,24},{64,96... | collective-permute-start | bytes 1966088 | tf_op jit(solution)/shard_map/ppermute | solution.py:49
  539.9 17.0 %collective-permute-start.37 = (bf16[4,320,256]{2,1,0:T(8,128)(2,1)S(1)}, bf16[4,320,256]{2,1,0:T(8,128)(2,1)S(1)}, u32[]{:S(2)}, u32[]{:S(2)}) collective-permute-start(bf16[4,320,256]{2,1,0:T(8,128)(2,1)S(1)} %add_convert_fusion.6), channel_id=1, source_target_pairs={{0,64},{8,72},{16,80},{24,88},{32,96},{40,104},{48,112},{56,120},{... | collective-permute-start | bytes 1966088 | tf_op jit(solution)/shard_map/ppermute | solution.py:49
  564.6 9.0 %collective-permute-start.39 = (bf16[4,160,256]{2,1,0:T(8,128)(2,1)S(1)}, bf16[4,160,256]{2,1,0:T(8,128)(2,1)S(1)}, u32[]{:S(2)}, u32[]{:S(2)}) collective-permute-start(bf16[4,160,256]{2,1,0:T(8,128)(2,1)S(1)} %add_convert_fusion.18), channel_id=1, source_target_pairs={{0,2},{1,3},{2,0},{3,1},{4,6},{5,7},{6,4},{7,5},{8,10},{9,11},{10,... | collective-permute-start | bytes 983048 | tf_op jit(solution)/shard_map/ppermute | solution.py:49
  573.7 9.6 %collective-permute-start.40 = (bf16[4,160,256]{2,1,0:T(8,128)(2,1)S(1)}, bf16[4,160,256]{2,1,0:T(8,128)(2,1)S(1)}, u32[]{:S(2)}, u32[]{:S(2)}) collective-permute-start(bf16[4,160,256]{2,1,0:T(8,128)(2,1)S(1)} %add_convert_fusion.17), channel_id=1, source_target_pairs={{0,4},{1,5},{2,6},{3,7},{4,0},{5,1},{6,2},{7,3},{8,12},{9,13},{10,... | collective-permute-start | bytes 983048 | tf_op jit(solution)/shard_map/ppermute | solution.py:49
  588.9 228.9 %all-reduce.12.cloned.1.call-start = ((), (), s32[]{:S(2)}) async-start(), calls=%async_computation.3 | async-start | bytes 5242880 | tf_op jit(solution)/shard_map/psum | solution.py:46
  683.3 16.3 %collective-permute-start.42 = (bf16[8,160,256]{2,1,0:T(8,128)(2,1)S(1)}, bf16[8,160,256]{2,1,0:T(8,128)(2,1)S(1)}, u32[]{:S(2)}, u32[]{:S(2)}) collective-permute-start(bf16[8,160,256]{2,1,0:T(8,128)(2,1)S(1)} %add_convert_fusion.4), channel_id=1, source_target_pairs={{0,2},{1,3},{2,0},{3,1},{4,6},{5,7},{6,4},{7,5},{8,10},{9,11},{10,... | collective-permute-start | bytes 1966088 | tf_op jit(solution)/shard_map/ppermute | solution.py:49
  699.7 16.6 %collective-permute-start.43 = (bf16[8,160,256]{2,1,0:T(8,128)(2,1)S(1)}, bf16[8,160,256]{2,1,0:T(8,128)(2,1)S(1)}, u32[]{:S(2)}, u32[]{:S(2)}) collective-permute-start(bf16[8,160,256]{2,1,0:T(8,128)(2,1)S(1)} %add_convert_fusion.3), channel_id=1, source_target_pairs={{0,4},{1,5},{2,6},{3,7},{4,0},{5,1},{6,2},{7,3},{8,12},{9,13},{10,... | collective-permute-start | bytes 1966088 | tf_op jit(solution)/shard_map/ppermute | solution.py:49
  724.5 159.2 %all-reduce.14.cloned.1.call-start = ((), (), s32[]{:S(2)}) async-start(), calls=%async_computation.4 | async-start | bytes 2621440 | tf_op jit(solution)/shard_map/psum | solution.py:46
  (42 other events, 977.5 us)
Sparse Core Ops, SparseCore 0:
  11.5 95.3 all-reduce.5
  152.6 86.9 all-reduce.7
  589.0 87.6 all-reduce.9
  724.6 93.0 all-reduce.11
  822.3 61.3 all-reduce.13

commit v3 on v2

--- a/solution.py
+++ b/solution.py
@@ -41,14 +41,33 @@
     return [(i, i ^ bit) for i in range(n)]
 
 
-def group_allreduce(x, axis, n):
-    if x.size * 2 >= (1 << 20):
-        return lax.psum(x, axis)
+def a2a_allreduce(x, axis, n):
+    shape = x.shape
+    k = shape[0]
+    if k >= n:
+        pieces = x.reshape((n, k // n) + shape[1:])
+    else:
+        rows = shape[1] * k // n
+        pieces = x.reshape((n, 1, rows) + shape[2:])
+    got = lax.all_to_all(pieces, axis, 0, 0, tiled=False)
+    owned = jnp.sum(got.astype(jnp.float32), axis=0).astype(jnp.bfloat16)
+    spread = lax.all_to_all(jnp.broadcast_to(owned[None], (n,) + owned.shape), axis, 0, 0, tiled=False)
+    return spread.reshape(shape)
+
+
+def doubling_allreduce(x, axis, n):
     bit = 1
     while bit < n:
         x = (x.astype(jnp.float32) + lax.ppermute(x, axis, xor_perm(n, bit)).astype(jnp.float32)).astype(jnp.bfloat16)
         bit *= 2
     return x
+
+
+def group_allreduce(x, axis, n):
+    small = 1 if axis == "leaf" else 4
+    if x.shape[0] <= small:
+        return doubling_allreduce(x, axis, n)
+    return a2a_allreduce(x, axis, n)
 
 
 def solve(right_side, diag_local, panel_local, parent):

time: 904 us -> 675 us (0.75)
  waiting for transfers between devices: 675 us -> 173 us
  blocking collectives: 0 us -> 284 us
  starting transfers between devices: 102 us -> 80.8 us
  between operations: 14.4 us -> 0.93 us
  local copies, waits for them, and re-layouts: 5.58 us -> 16.1 us
    psum x5 -> x0, waiting for transfers between devices: 418 us -> none  [group_allreduce(): return lax.psum(x, axis)]
    all_to_all x0 -> x13, blocking collectives: none -> 284 us  [the longest x8 189 us: a2a_allreduce(): got = lax.all_to_all(pieces, axis, 0, 0, tiled=False)]
    ppermute x44 -> x22, waiting for transfers between devices: 256 us -> 89.1 us  [doubling_allreduce(): lax.ppermute(x, axis, xor_perm(n, bit)).astype(jnp.float32)]
    all_to_all x0 -> x9, waiting for transfers between devices: none -> 83.5 us  [the longest x6 67.3 us: a2a_allreduce(): lax.all_to_all(jnp.broadcast_to(owned[None], (n,) + owned.shape), axis, 0...]
    ppermute x44 -> x22, starting transfers between devices: 102 us -> 39 us  [doubling_allreduce(): lax.ppermute(x, axis, xor_perm(n, bit)).astype(jnp.float32)]
    all_to_all x0 -> x9, starting transfers between devices: none -> 41.9 us  [the longest x6 26.1 us: a2a_allreduce(): lax.all_to_all(jnp.broadcast_to(owned[None], (n,) + owned.shape), axis, 0...]
    reduce_sum x0 -> x11, other arithmetic: none -> 10.5 us  [a2a_allreduce(): owned = jnp.sum(got.astype(jnp.float32), axis=0).astype(jnp.bfloat16)]
  transfers between devices with their start and end apart: 49 -> 31, of which waited for: 48 -> 31; matrix products, arithmetic and copies ran while one was open for 4% -> 7% of each run, Pallas kernels for 0% -> 0%
where the time goes in v3:
time: 675 us; the launch traced here: 667 us
  blocking collectives  284 us (42%)
  waiting for transfers between devices  173 us (26%)
  matrix products  94.7 us (14%)
  starting transfers between devices  80.8 us (12%)
  other arithmetic  17 us (3%)
  local copies, waits for them, and re-layouts  16.1 us (2%)
    all_to_all x8, blocking collectives, a2a_allreduce(): got = lax.all_to_all(pieces, axis, 0, 0, tiled=False)  189 us
    all_to_all x5, blocking collectives, a2a_allreduce(): lax.all_to_all(jnp.broadcast_to(owned[None], (n,) + owned.shape), axis, 0...  95.7 us
    ppermute x22, waiting for transfers between devices, doubling_allreduce(): lax.ppermute(x, axis, xor_perm(n, bit)).astype(jnp.float32)  89.1 us
    all_to_all x6, waiting for transfers between devices, a2a_allreduce(): lax.all_to_all(jnp.broadcast_to(owned[None], (n,) + owned.shape), axis, 0...  67.3 us
    ppermute x22, starting transfers between devices, doubling_allreduce(): lax.ppermute(x, axis, xor_perm(n, bit)).astype(jnp.float32)  39 us
    dot_general x10, matrix products, solve(): jnp.einsum('boj,boh->bjh', pair_slice(panel_local, tree_level, distance),...  26.5 us
    all_to_all x6, starting transfers between devices, a2a_allreduce(): lax.all_to_all(jnp.broadcast_to(owned[None], (n,) + owned.shape), axis, 0...  26.1 us
    dot_general x10, matrix products, solve(): jnp.einsum('sjv,svk->sjk', pair_slice(panel_local, source_level, distance...  21.7 us
  transfers between devices with their start and end apart: 31, of which 31 were waited for; matrix products, arithmetic and copies ran while one was open for 7% of the time, Pallas kernels for 0%

profile of v3, /device:TPU:1, one launch (start us, length us, event | category | flops | bytes accessed | tf_op | source)
XLA Modules:
  0.0 666.5 jit_solution(6722524267757479321)
XLA Ops:
  3.3 39.6 %all_to_all.110 = bf16[16,1,320,256]{3,2,1,0:T(8,128)(2,1)S(1)} all-to-all(bf16[16,1,320,256]{3,2,1,0:T(8,128)(2,1)S(1)} %convert_bitcast_fusion), channel_id=1, replica_groups=mesh['leaf'=16,'col'=8] {'leaf'}, dimensions={0} | all-to-all | bytes 5242880 | tf_op jit(solution)/shard_map/all_to_all | solution.py:52
  50.2 29.9 %all-to-all-done.1 = bf16[16,1,320,256]{3,2,1,0:T(8,128)(2,1)S(1)} async-done(((bf16[16,1,320,256]{3,2,1,0:T(8,128)(2,1)}), bf16[16,1,320,256]{3,2,1,0:T(8,128)(2,1)S(1)}, u32[]{:S(2)}, u32[]{:S(2)}) %all-to-all-start.1) | async-done | bytes 2621472 | tf_op jit(solution)/shard_map/all_to_all | solution.py:54
  85.1 22.2 %all_to_all.111 = bf16[8,1,160,256]{3,2,1,0:T(8,128)(2,1)S(1)} all-to-all(bf16[8,1,160,256]{3,2,1,0:T(8,128)(2,1)S(1)} %copy.15), channel_id=1, replica_groups=mesh['leaf'=16,'col'=8] {'col'}, dimensions={0} | all-to-all | bytes 1310720 | tf_op jit(solution)/shard_map/all_to_all | solution.py:52
  107.5 14.2 %all_to_all.112 = bf16[8,1,160,256]{3,2,1,0:T(8,128)(2,1)S(1)} all-to-all(bf16[8,1,160,256]{3,2,1,0:T(8,128)(2,1)S(1)} %broadcast_in_dim.26), channel_id=1, replica_groups=mesh['leaf'=16,'col'=8] {'col'}, dimensions={0} | all-to-all | bytes 1310720 | tf_op jit(solution)/shard_map/all_to_all | solution.py:54
  123.9 22.0 %all_to_all.113 = bf16[16,1,160,256]{3,2,1,0:T(8,128)(2,1)} all-to-all(bf16[16,1,160,256]{3,2,1,0:T(8,128)(2,1)S(1)} %bitcast.232), channel_id=1, replica_groups=mesh['leaf'=16,'col'=8] {'leaf'}, dimensions={0} | all-to-all | bytes 2621440 | tf_op jit(solution)/shard_map/all_to_all | solution.py:52
  148.5 4.9 all-to-all-start.5
  160.0 10.6 %all-to-all-done.5 = bf16[16,1,160,256]{3,2,1,0:T(8,128)(2,1)} async-done(((bf16[16,1,160,256]{3,2,1,0:T(8,128)(2,1)}), bf16[16,1,160,256]{3,2,1,0:T(8,128)(2,1)}, u32[]{:S(2)}, u32[]{:S(2)}) %all-to-all-start.5) | async-done | bytes 1310752 | tf_op jit(solution)/shard_map/all_to_all | solution.py:54
  180.0 8.6 %collective-permute-done.1 = bf16[4,160,256]{2,0,1:T(4,128)(2,1)S(1)} collective-permute-done((bf16[4,160,256]{2,0,1:T(4,128)(2,1)S(1)}, bf16[4,160,256]{2,0,1:T(4,128)(2,1)S(1)}, u32[]{:S(2)}, u32[]{:S(2)}) %collective-permute-start.1) | collective-permute-done | bytes 327712 | tf_op jit(solution)/shard_map/ppermute | solution.py:61
  189.6 8.8 %collective-permute-done.2 = bf16[4,160,256]{2,0,1:T(4,128)(2,1)S(1)} collective-permute-done((bf16[4,160,256]{2,0,1:T(4,128)(2,1)S(1)}, bf16[4,160,256]{2,0,1:T(4,128)(2,1)S(1)}, u32[]{:S(2)}, u32[]{:S(2)}) %collective-permute-start.2) | collective-permute-done | bytes 327712 | tf_op jit(solution)/shard_map/ppermute | solution.py:61
  206.5 8.6 %all-to-all-done.6 = bf16[16,1,80,256]{3,2,1,0:T(8,128)(2,1)S(1)} async-done(((bf16[16,1,80,256]{3,2,1,0:T(8,128)(2,1)}), bf16[16,1,80,256]{3,2,1,0:T(8,128)(2,1)S(1)}, u32[]{:S(2)}, u32[]{:S(2)}) %all-to-all-start.6) | async-done | bytes 655392 | tf_op jit(solution)/shard_map/all_to_all | solution.py:52
  235.8 4.8 collective-permute-start.3
  285.0 4.8 collective-permute-start.6
  316.4 6.1 collective-permute-done.12
  323.6 6.5 collective-permute-start.13
  341.6 11.4 %all_to_all.114 = bf16[16,1,40,256]{3,2,1,0:T(8,128)(2,1)} all-to-all(bf16[16,1,40,256]{3,2,1,0:T(8,128)(2,1)S(1)} %bitcast.241), channel_id=1, replica_groups=mesh['leaf'=16,'col'=8] {'leaf'}, dimensions={0} | all-to-all | bytes 655360 | tf_op jit(solution)/shard_map/all_to_all | solution.py:52
  354.1 11.0 %all_to_all.115 = bf16[16,1,40,256]{3,2,1,0:T(8,128)(2,1)S(1)} all-to-all(bf16[16,1,40,256]{3,2,1,0:T(8,128)(2,1)S(1)} %broadcast_in_dim.30), channel_id=1, replica_groups=mesh['leaf'=16,'col'=8] {'leaf'}, dimensions={0} | all-to-all | bytes 655360 | tf_op jit(solution)/shard_map/all_to_all | solution.py:54
  366.5 5.0 collective-permute-start.16
  372.9 5.1 collective-permute-done.17
  378.9 5.2 collective-permute-done.18
  388.9 13.4 %all_to_all.116 = bf16[16,1,80,256]{3,2,1,0:T(8,128)(2,1)} all-to-all(bf16[16,1,80,256]{3,2,1,0:T(8,128)(2,1)S(1)} %bitcast.238), channel_id=1, replica_groups=mesh['leaf'=16,'col'=8] {'leaf'}, dimensions={0} | all-to-all | bytes 1310720 | tf_op jit(solution)/shard_map/all_to_all | solution.py:52
  404.9 13.4 %all_to_all.117 = bf16[16,1,80,256]{3,2,1,0:T(8,128)(2,1)S(1)} all-to-all(bf16[16,1,80,256]{3,2,1,0:T(8,128)(2,1)S(1)} %broadcast_in_dim.31), channel_id=1, replica_groups=mesh['leaf'=16,'col'=8] {'leaf'}, dimensions={0} | all-to-all | bytes 1310720 | tf_op jit(solution)/shard_map/all_to_all | solution.py:54
  426.8 8.1 %collective-permute-done.20 = bf16[4,160,256]{2,1,0:T(8,128)(2,1)S(1)} collective-permute-done((bf16[4,160,256]{2,1,0:T(8,128)(2,1)S(1)}, bf16[4,160,256]{2,1,0:T(8,128)(2,1)S(1)}, u32[]{:S(2)}, u32[]{:S(2)}) %collective-permute-start.20) | collective-permute-done | bytes 327712 | tf_op jit(solution)/shard_map/ppermute | solution.py:61
  437.6 7.0 %collective-permute-done.21 = bf16[4,160,256]{2,1,0:T(8,128)(2,1)S(1)} collective-permute-done((bf16[4,160,256]{2,1,0:T(8,128)(2,1)S(1)}, bf16[4,160,256]{2,1,0:T(8,128)(2,1)S(1)}, u32[]{:S(2)}, u32[]{:S(2)}) %collective-permute-start.21) | collective-permute-done | bytes 327712 | tf_op jit(solution)/shard_map/ppermute | solution.py:61
  449.7 20.7 %all_to_all.118 = bf16[16,1,160,256]{3,2,1,0:T(8,128)(2,1)} all-to-all(bf16[16,1,160,256]{3,2,1,0:T(8,128)(2,1)S(1)} %bitcast.234), channel_id=1, replica_groups=mesh['leaf'=16,'col'=8] {'leaf'}, dimensions={0} | all-to-all | bytes 2621440 | tf_op jit(solution)/shard_map/all_to_all | solution.py:52
  477.5 16.9 %all-to-all-done.15 = bf16[16,1,160,256]{3,2,1,0:T(8,128)(2,1)} async-done(((bf16[16,1,160,256]{3,2,1,0:T(8,128)(2,1)}), bf16[16,1,160,256]{3,2,1,0:T(8,128)(2,1)}, u32[]{:S(2)}, u32[]{:S(2)}) %all-to-all-start.15) | async-done | bytes 1310752 | tf_op jit(solution)/shard_map/all_to_all | solution.py:54
  497.8 7.7 %all-to-all-start.16 = ((bf16[8,1,160,256]{3,2,1,0:T(8,128)(2,1)}), bf16[8,1,160,256]{3,2,1,0:T(8,128)(2,1)S(1)}, u32[]{:S(2)}, u32[]{:S(2)}) async-start(bf16[8,1,160,256]{3,2,1,0:T(8,128)(2,1)} %fusion.70), calls=%async_computation.16 | async-start | bytes 1310720 | tf_op jit(solution)/shard_map/all_to_all | solution.py:52
  507.0 5.2 fusion.38
  525.0 5.2 fusion.41
  542.2 36.0 %all_to_all.119 = bf16[16,1,320,256]{3,2,1,0:T(8,128)(2,1)} all-to-all(bf16[16,1,320,256]{3,2,1,0:T(8,128)(2,1)S(1)} %fusion.1), channel_id=1, replica_groups=mesh['leaf'=16,'col'=8] {'leaf'}, dimensions={0} | all-to-all | bytes 5242880 | tf_op jit(solution)/shard_map/all_to_all | solution.py:52
  580.6 35.7 %all_to_all.120 = bf16[16,1,320,256]{3,2,1,0:T(8,128)(2,1)S(1)} all-to-all(bf16[16,1,320,256]{3,2,1,0:T(8,128)(2,1)S(1)} %broadcast_in_dim.34), channel_id=1, replica_groups=mesh['leaf'=16,'col'=8] {'leaf'}, dimensions={0} | all-to-all | bytes 5242880 | tf_op jit(solution)/shard_map/all_to_all | solution.py:54
  617.2 23.5 %all_to_all.121 = bf16[8,2,160,256]{3,2,1,0:T(8,128)(2,1)S(1)} all-to-all(bf16[8,2,160,256]{3,2,1,0:T(8,128)(2,1)S(1)} %bitcast.235), channel_id=1, replica_groups=mesh['leaf'=16,'col'=8] {'col'}, dimensions={0} | all-to-all | bytes 2621440 | tf_op jit(solution)/shard_map/all_to_all | solution.py:52
  641.0 21.4 %all_to_all.122 = bf16[8,2,160,256]{3,2,1,0:T(8,128)(2,1)S(1)} all-to-all(bf16[8,2,160,256]{3,2,1,0:T(8,128)(2,1)S(1)} %broadcast_in_dim.35), channel_id=1, replica_groups=mesh['leaf'=16,'col'=8] {'col'}, dimensions={0} | all-to-all | bytes 2621440 | tf_op jit(solution)/shard_map/all_to_all | solution.py:54
  (223 shorter events, 222.2 us)
Async XLA Ops:
  45.1 35.0 %all-to-all-start.1 = ((bf16[16,1,320,256]{3,2,1,0:T(8,128)(2,1)}), bf16[16,1,320,256]{3,2,1,0:T(8,128)(2,1)S(1)}, u32[]{:S(2)}, u32[]{:S(2)}) async-start(bf16[16,1,320,256]{3,2,1,0:T(8,128)(2,1)} %broadcast_in_dim.25), calls=%async_computation.1 | async-start | bytes 5242880 | tf_op jit(solution)/shard_map/all_to_all | solution.py:54
  50.2 285.3 %copy-start.17 = (s32[31]{0:T(128)}, s32[31]{0:T(128)S(1)}, u32[]{:S(2)}) copy-start(s32[31]{0:T(128)S(1)} %get-tuple-element.10) | copy-start | bytes 376
  148.5 22.0 %all-to-all-start.5 = ((bf16[16,1,160,256]{3,2,1,0:T(8,128)(2,1)}), bf16[16,1,160,256]{3,2,1,0:T(8,128)(2,1)}, u32[]{:S(2)}, u32[]{:S(2)}) async-start(bf16[16,1,160,256]{3,2,1,0:T(8,128)(2,1)} %broadcast_in_dim.27), calls=%async_computation.5 | async-start | bytes 2621440 | tf_op jit(solution)/shard_map/all_to_all | solution.py:54
  174.4 5.1 collective-permute-start
  179.7 9.0 %collective-permute-start.1 = (bf16[4,160,256]{2,0,1:T(4,128)(2,1)S(1)}, bf16[4,160,256]{2,0,1:T(4,128)(2,1)S(1)}, u32[]{:S(2)}, u32[]{:S(2)}) collective-permute-start(bf16[4,160,256]{2,0,1:T(4,128)(2,1)S(1)} %add_convert_fusion.7), channel_id=1, source_target_pairs={{0,2},{1,3},{2,0},{3,1},{4,6},{5,7},{6,4},{7,5},{8,10},{9,11},{10,... | collective-permute-start | bytes 983048 | tf_op jit(solution)/shard_map/ppermute | solution.py:61
  188.8 9.6 %collective-permute-start.2 = (bf16[4,160,256]{2,0,1:T(4,128)(2,1)S(1)}, bf16[4,160,256]{2,0,1:T(4,128)(2,1)S(1)}, u32[]{:S(2)}, u32[]{:S(2)}) collective-permute-start(bf16[4,160,256]{2,0,1:T(4,128)(2,1)S(1)} %add_convert_fusion.6), channel_id=1, source_target_pairs={{0,4},{1,5},{2,6},{3,7},{4,0},{5,1},{6,2},{7,3},{8,12},{9,13},{10,... | collective-permute-start | bytes 983048 | tf_op jit(solution)/shard_map/ppermute | solution.py:61
  201.3 13.8 %all-to-all-start.6 = ((bf16[16,1,80,256]{3,2,1,0:T(8,128)(2,1)}), bf16[16,1,80,256]{3,2,1,0:T(8,128)(2,1)S(1)}, u32[]{:S(2)}, u32[]{:S(2)}) async-start(bf16[16,1,80,256]{3,2,1,0:T(8,128)(2,1)} %bitcast.236), calls=%async_computation.6 | async-start | bytes 1310720 | tf_op jit(solution)/shard_map/all_to_all | solution.py:52
  216.0 13.5 %all-to-all-start.7 = ((bf16[16,1,80,256]{3,2,1,0:T(8,128)(2,1)}), bf16[16,1,80,256]{3,2,1,0:T(8,128)(2,1)S(1)}, u32[]{:S(2)}, u32[]{:S(2)}) async-start(bf16[16,1,80,256]{3,2,1,0:T(8,128)(2,1)} %broadcast_in_dim.28), calls=%async_computation.7 | async-start | bytes 1310720 | tf_op jit(solution)/shard_map/all_to_all | solution.py:54
  235.8 5.8 collective-permute-start.3
  241.8 5.5 collective-permute-start.4
  247.4 6.1 collective-permute-start.5
  255.9 12.2 %all-to-all-start.8 = ((bf16[16,1,40,256]{3,2,1,0:T(8,128)(2,1)}), bf16[16,1,40,256]{3,2,1,0:T(8,128)(2,1)}, u32[]{:S(2)}, u32[]{:S(2)}) async-start(bf16[16,1,40,256]{3,2,1,0:T(8,128)(2,1)} %bitcast.239), calls=%async_computation.8 | async-start | bytes 655360 | tf_op jit(solution)/shard_map/all_to_all | solution.py:52
  269.9 11.9 %all-to-all-start.9 = ((bf16[16,1,40,256]{3,2,1,0:T(8,128)(2,1)}), bf16[16,1,40,256]{3,2,1,0:T(8,128)(2,1)}, u32[]{:S(2)}, u32[]{:S(2)}) async-start(bf16[16,1,40,256]{3,2,1,0:T(8,128)(2,1)} %broadcast_in_dim.29), calls=%async_computation.9 | async-start | bytes 655360 | tf_op jit(solution)/shard_map/all_to_all | solution.py:54
  285.0 5.7 collective-permute-start.6
  290.7 3.8 collective-permute-start.7
  294.5 4.9 collective-permute-start.8
  300.6 4.2 collective-permute-start.9
  304.9 5.8 collective-permute-start.10
  310.7 4.5 collective-permute-start.11
  315.3 7.2 %collective-permute-start.12 = (bf16[1,320,256]{2,1,0:T(8,128)(2,1)S(1)}, bf16[1,320,256]{2,1,0:T(8,128)(2,1)S(1)}, u32[]{:S(2)}, u32[]{:S(2)}) collective-permute-start(bf16[1,320,256]{2,1,0:T(8,128)(2,1)S(1)} %add_convert_fusion.12), channel_id=1, source_target_pairs={{0,64},{8,72},{16,80},{24,88},{32,96},{40,104},{48,112},{56,120},{... | collective-permute-start | bytes 491528 | tf_op jit(solution)/shard_map/ppermute | solution.py:61
  323.6 7.4 %collective-permute-start.13 = (bf16[1,160,256]{2,1,0:T(8,128)(2,1)S(1)}, bf16[1,160,256]{2,1,0:T(8,128)(2,1)S(1)}, u32[]{:S(2)}, u32[]{:S(2)}) collective-permute-start(bf16[1,160,256]{2,1,0:T(8,128)(2,1)S(1)} %fusion.94), channel_id=1, source_target_pairs={{0,1},{1,0},{2,3},{3,2},{4,5},{5,4},{6,7},{7,6},{8,9},{9,8},{10,11... | collective-permute-start | bytes 245768 | tf_op jit(solution)/shard_map/ppermute | solution.py:61
  331.0 3.8 collective-permute-start.14
  334.8 4.9 collective-permute-start.15
  366.5 6.0 collective-permute-start.16
  372.6 5.5 collective-permute-start.17
  378.1 6.1 collective-permute-start.18
  419.8 6.0 collective-permute-start.19
  425.9 9.0 %collective-permute-start.20 = (bf16[4,160,256]{2,1,0:T(8,128)(2,1)S(1)}, bf16[4,160,256]{2,1,0:T(8,128)(2,1)S(1)}, u32[]{:S(2)}, u32[]{:S(2)}) collective-permute-start(bf16[4,160,256]{2,1,0:T(8,128)(2,1)S(1)} %add_convert_fusion.4), channel_id=1, source_target_pairs={{0,2},{1,3},{2,0},{3,1},{4,6},{5,7},{6,4},{7,5},{8,10},{9,11},{10,... | collective-permute-start | bytes 983048 | tf_op jit(solution)/shard_map/ppermute | solution.py:61
  435.0 9.6 %collective-permute-start.21 = (bf16[4,160,256]{2,1,0:T(8,128)(2,1)S(1)}, bf16[4,160,256]{2,1,0:T(8,128)(2,1)S(1)}, u32[]{:S(2)}, u32[]{:S(2)}) collective-permute-start(bf16[4,160,256]{2,1,0:T(8,128)(2,1)S(1)} %add_convert_fusion.3), channel_id=1, source_target_pairs={{0,4},{1,5},{2,6},{3,7},{4,0},{5,1},{6,2},{7,3},{8,12},{9,13},{10,... | collective-permute-start | bytes 983048 | tf_op jit(solution)/shard_map/ppermute | solution.py:61
  473.1 21.3 %all-to-all-start.15 = ((bf16[16,1,160,256]{3,2,1,0:T(8,128)(2,1)}), bf16[16,1,160,256]{3,2,1,0:T(8,128)(2,1)}, u32[]{:S(2)}, u32[]{:S(2)}) async-start(bf16[16,1,160,256]{3,2,1,0:T(8,128)(2,1)} %broadcast_in_dim.32), calls=%async_computation.15 | async-start | bytes 2621440 | tf_op jit(solution)/shard_map/all_to_all | solution.py:54
  497.8 18.6 %all-to-all-start.16 = ((bf16[8,1,160,256]{3,2,1,0:T(8,128)(2,1)}), bf16[8,1,160,256]{3,2,1,0:T(8,128)(2,1)S(1)}, u32[]{:S(2)}, u32[]{:S(2)}) async-start(bf16[8,1,160,256]{3,2,1,0:T(8,128)(2,1)} %fusion.70), calls=%async_computation.16 | async-start | bytes 1310720 | tf_op jit(solution)/shard_map/all_to_all | solution.py:52
  518.8 15.4 %all-to-all-start.17 = ((bf16[8,1,160,256]{3,2,1,0:T(8,128)(2,1)}), bf16[8,1,160,256]{3,2,1,0:T(8,128)(2,1)S(1)}, u32[]{:S(2)}, u32[]{:S(2)}) async-start(bf16[8,1,160,256]{3,2,1,0:T(8,128)(2,1)} %broadcast_in_dim.33), calls=%async_computation.17 | async-start | bytes 1310720 | tf_op jit(solution)/shard_map/all_to_all | solution.py:54
  (29 other events, 359.0 us)

commit v4 on v3

--- a/solution.py
+++ b/solution.py
@@ -114,22 +114,26 @@
         node_count = level_counts[tree_level]
         corrected = forward_levels[tree_level]
         if tree_level < 4:
-            partial_value = None
-            for distance in range(1, 5 - tree_level):
-                onehot = level_onehot(climbed, tree_level, distance)
-                upper_node = jnp.einsum(
-                    "ks,kjr->sjr",
-                    onehot,
-                    solution_half[tree_level + distance].astype(jnp.float32),
-                    precision=lax.Precision.HIGHEST,
-                ).astype(jnp.bfloat16)
-                term = jnp.einsum(
-                    "boj,boh->bjh",
-                    pair_slice(panel_local, tree_level, distance),
-                    upper_node,
-                    preferred_element_type=jnp.float32,
-                )
-                partial_value = term if partial_value is None else partial_value + term
+            spread = 4 - tree_level
+            first = pair_offset(tree_level)
+            panel_block = panel_local[first : first + node_count * spread].reshape(
+                (node_count, spread) + panel_local.shape[1:]
+            )
+            upper_node = jnp.stack(
+                [
+                    jnp.einsum(
+                        "ks,kjr->sjr",
+                        level_onehot(climbed, tree_level, distance),
+                        solution_half[tree_level + distance].astype(jnp.float32),
+                        precision=lax.Precision.HIGHEST,
+                    )
+                    for distance in range(1, spread + 1)
+                ],
+                axis=1,
+            ).astype(jnp.bfloat16)
+            partial_value = jnp.einsum(
+                "sdoj,sdoh->sjh", panel_block, upper_node, preferred_element_type=jnp.float32
+            )
             corrected = corrected - group_allreduce(
                 partial_value.astype(jnp.bfloat16), "leaf", n_leaf
             ).astype(jnp.float32)

time: 675 us -> 679 us (level)
  blocking collectives: 284 us -> 325 us
  waiting for transfers between devices: 173 us -> 149 us
  matrix products: 94.7 us -> 80.3 us
  starting transfers between devices: 80.8 us -> 68.4 us
  other arithmetic: 17 us -> 24.1 us
  local copies, waits for them, and re-layouts: 16.1 us -> 22.9 us
    all_to_all x8 -> x9, blocking collectives: 189 us -> 210 us  [a2a_allreduce(): got = lax.all_to_all(pieces, axis, 0, 0, tiled=False)]
    all_to_all x6 -> x5, waiting for transfers between devices: 67.3 us -> 46.5 us  [a2a_allreduce(): lax.all_to_all(jnp.broadcast_to(owned[None], (n,) + owned.shape), axis, 0...]
    all_to_all x5 -> x6, blocking collectives: 95.7 us -> 115 us  [a2a_allreduce(): lax.all_to_all(jnp.broadcast_to(owned[None], (n,) + owned.shape), axis, 0...]
    dot_general x16 -> x10, matrix products: 32.3 us -> 19.2 us  [the longest x4 13.7 us: solve(): jnp.einsum('sdoj,sdoh->sjh', panel_block, upper_node, preferred_element_t...]
    slice x0 -> x5, local copies, waits for them, and re-layouts: none -> 8.25 us  [solve(): panel_local[first:first + node_count * spread]]
    all_to_all x3 -> x2, starting transfers between devices: 15.7 us -> 8.06 us  [a2a_allreduce(): got = lax.all_to_all(pieces, axis, 0, 0, tiled=False)]
    another operation x5 -> x11, other arithmetic: 0.24 us -> 7.35 us  [the longest x6 7.11 us: solve(): jnp.stack([jnp.einsum('ks,kjr->sjr', level_onehot(climbed, tree_level, di...]
    all_to_all x6 -> x5, starting transfers between devices: 26.1 us -> 21.5 us  [a2a_allreduce(): lax.all_to_all(jnp.broadcast_to(owned[None], (n,) + owned.shape), axis, 0...]
  transfers between devices with their start and end apart: 31 -> 29, of which waited for: 31 -> 28; matrix products, arithmetic and copies ran while one was open for 7% -> 6% of each run, Pallas kernels for 0% -> 0%
where the time goes in v4:
time: 679 us; the launch traced here: 671 us
  blocking collectives  325 us (48%)
  waiting for transfers between devices  149 us (22%)
  matrix products  80.3 us (12%)
  starting transfers between devices  68.4 us (10%)
  other arithmetic  24.1 us (4%)
  local copies, waits for them, and re-layouts  22.9 us (3%)
    all_to_all x9, blocking collectives, a2a_allreduce(): got = lax.all_to_all(pieces, axis, 0, 0, tiled=False)  210 us
    all_to_all x6, blocking collectives, a2a_allreduce(): lax.all_to_all(jnp.broadcast_to(owned[None], (n,) + owned.shape), axis, 0...  115 us
    ppermute x22, waiting for transfers between devices, doubling_allreduce(): lax.ppermute(x, axis, xor_perm(n, bit)).astype(jnp.float32)  90.5 us
    all_to_all x5, waiting for transfers between devices, a2a_allreduce(): lax.all_to_all(jnp.broadcast_to(owned[None], (n,) + owned.shape), axis, 0...  46.5 us
    ppermute x22, starting transfers between devices, doubling_allreduce(): lax.ppermute(x, axis, xor_perm(n, bit)).astype(jnp.float32)  38.9 us
    dot_general x10, matrix products, solve(): jnp.einsum('sjv,svk->sjk', pair_slice(panel_local, source_level, distance...  21.7 us
    all_to_all x5, starting transfers between devices, a2a_allreduce(): lax.all_to_all(jnp.broadcast_to(owned[None], (n,) + owned.shape), axis, 0...  21.5 us
    dot_general x10, matrix products, solve(): jnp.einsum('ks,sjr->kjr', onehot, products, precision=lax.Precision.HIGHEST)  21.3 us
  transfers between devices with their start and end apart: 29, of which 28 were waited for; matrix products, arithmetic and copies ran while one was open for 6% of the time, Pallas kernels for 0%

profile of v4, /device:TPU:1, one launch (start us, length us, event | category | flops | bytes accessed | tf_op | source)
XLA Modules:
  0.0 671.0 jit_solution(274034258781027609)
XLA Ops:
  3.3 39.6 %all_to_all.110 = bf16[16,1,320,256]{3,2,1,0:T(8,128)(2,1)S(1)} all-to-all(bf16[16,1,320,256]{3,2,1,0:T(8,128)(2,1)S(1)} %convert_bitcast_fusion), channel_id=1, replica_groups=mesh['leaf'=16,'col'=8] {'leaf'}, dimensions={0} | all-to-all | bytes 5242880 | tf_op jit(solution)/shard_map/all_to_all | solution.py:52
  50.2 29.9 %all-to-all-done.1 = bf16[16,1,320,256]{3,2,1,0:T(8,128)(2,1)S(1)} async-done(((bf16[16,1,320,256]{3,2,1,0:T(8,128)(2,1)}), bf16[16,1,320,256]{3,2,1,0:T(8,128)(2,1)S(1)}, u32[]{:S(2)}, u32[]{:S(2)}) %all-to-all-start.1) | async-done | bytes 2621472 | tf_op jit(solution)/shard_map/all_to_all | solution.py:54
  85.1 22.2 %all_to_all.111 = bf16[8,1,160,256]{3,2,1,0:T(8,128)(2,1)S(1)} all-to-all(bf16[8,1,160,256]{3,2,1,0:T(8,128)(2,1)S(1)} %copy.33), channel_id=1, replica_groups=mesh['leaf'=16,'col'=8] {'col'}, dimensions={0} | all-to-all | bytes 1310720 | tf_op jit(solution)/shard_map/all_to_all | solution.py:52
  107.5 14.2 %all_to_all.112 = bf16[8,1,160,256]{3,2,1,0:T(8,128)(2,1)S(1)} all-to-all(bf16[8,1,160,256]{3,2,1,0:T(8,128)(2,1)S(1)} %broadcast_in_dim.26), channel_id=1, replica_groups=mesh['leaf'=16,'col'=8] {'col'}, dimensions={0} | all-to-all | bytes 1310720 | tf_op jit(solution)/shard_map/all_to_all | solution.py:54
  123.9 22.0 %all_to_all.113 = bf16[16,1,160,256]{3,2,1,0:T(8,128)(2,1)} all-to-all(bf16[16,1,160,256]{3,2,1,0:T(8,128)(2,1)S(1)} %bitcast.271), channel_id=1, replica_groups=mesh['leaf'=16,'col'=8] {'leaf'}, dimensions={0} | all-to-all | bytes 2621440 | tf_op jit(solution)/shard_map/all_to_all | solution.py:52
  159.7 10.6 %all-to-all-done.5 = bf16[16,1,160,256]{3,2,1,0:T(8,128)(2,1)} async-done(((bf16[16,1,160,256]{3,2,1,0:T(8,128)(2,1)}), bf16[16,1,160,256]{3,2,1,0:T(8,128)(2,1)}, u32[]{:S(2)}, u32[]{:S(2)}) %all-to-all-start.5) | async-done | bytes 1310752 | tf_op jit(solution)/shard_map/all_to_all | solution.py:54
  179.7 8.6 %collective-permute-done.1 = bf16[4,160,256]{2,0,1:T(4,128)(2,1)S(1)} collective-permute-done((bf16[4,160,256]{2,0,1:T(4,128)(2,1)S(1)}, bf16[4,160,256]{2,0,1:T(4,128)(2,1)S(1)}, u32[]{:S(2)}, u32[]{:S(2)}) %collective-permute-start.1) | collective-permute-done | bytes 327712 | tf_op jit(solution)/shard_map/ppermute | solution.py:61
  189.3 8.8 %collective-permute-done.2 = bf16[4,160,256]{2,0,1:T(4,128)(2,1)S(1)} collective-permute-done((bf16[4,160,256]{2,0,1:T(4,128)(2,1)S(1)}, bf16[4,160,256]{2,0,1:T(4,128)(2,1)S(1)}, u32[]{:S(2)}, u32[]{:S(2)}) %collective-permute-start.2) | collective-permute-done | bytes 327712 | tf_op jit(solution)/shard_map/ppermute | solution.py:61
  206.2 8.6 %all-to-all-done.6 = bf16[16,1,80,256]{3,2,1,0:T(8,128)(2,1)S(1)} async-done(((bf16[16,1,80,256]{3,2,1,0:T(8,128)(2,1)}), bf16[16,1,80,256]{3,2,1,0:T(8,128)(2,1)S(1)}, u32[]{:S(2)}, u32[]{:S(2)}) %all-to-all-start.6) | async-done | bytes 655392 | tf_op jit(solution)/shard_map/all_to_all | solution.py:52
  235.7 4.8 collective-permute-start.3
  284.9 4.8 collective-permute-start.6
  316.3 6.1 collective-permute-done.12
  323.5 6.5 collective-permute-start.13
  341.6 11.4 %all_to_all.114 = bf16[16,1,40,256]{3,2,1,0:T(8,128)(2,1)} all-to-all(bf16[16,1,40,256]{3,2,1,0:T(8,128)(2,1)S(1)} %bitcast.280), channel_id=1, replica_groups=mesh['leaf'=16,'col'=8] {'leaf'}, dimensions={0} | all-to-all | bytes 655360 | tf_op jit(solution)/shard_map/all_to_all | solution.py:52
  354.0 11.0 %all_to_all.115 = bf16[16,1,40,256]{3,2,1,0:T(8,128)(2,1)S(1)} all-to-all(bf16[16,1,40,256]{3,2,1,0:T(8,128)(2,1)S(1)} %broadcast_in_dim.30), channel_id=1, replica_groups=mesh['leaf'=16,'col'=8] {'leaf'}, dimensions={0} | all-to-all | bytes 655360 | tf_op jit(solution)/shard_map/all_to_all | solution.py:54
  366.4 5.0 collective-permute-start.16
  372.9 5.1 collective-permute-done.17
  379.0 5.2 collective-permute-done.18
  386.4 13.6 %all_to_all.116 = bf16[16,1,80,256]{3,2,1,0:T(8,128)(2,1)} all-to-all(bf16[16,1,80,256]{3,2,1,0:T(8,128)(2,1)S(1)} %bitcast.276), channel_id=1, replica_groups=mesh['leaf'=16,'col'=8] {'leaf'}, dimensions={0} | all-to-all | bytes 1310720 | tf_op jit(solution)/shard_map/all_to_all | solution.py:52
  402.6 13.0 %all_to_all.117 = bf16[16,1,80,256]{3,2,1,0:T(8,128)(2,1)S(1)} all-to-all(bf16[16,1,80,256]{3,2,1,0:T(8,128)(2,1)S(1)} %broadcast_in_dim.31), channel_id=1, replica_groups=mesh['leaf'=16,'col'=8] {'leaf'}, dimensions={0} | all-to-all | bytes 1310720 | tf_op jit(solution)/shard_map/all_to_all | solution.py:54
  417.0 4.8 collective-permute-start.19
  423.6 8.6 %collective-permute-done.20 = bf16[4,160,256]{2,1,0:T(8,128)(2,1)S(1)} collective-permute-done((bf16[4,160,256]{2,1,0:T(8,128)(2,1)S(1)}, bf16[4,160,256]{2,1,0:T(8,128)(2,1)S(1)}, u32[]{:S(2)}, u32[]{:S(2)}) %collective-permute-start.20) | collective-permute-done | bytes 327712 | tf_op jit(solution)/shard_map/ppermute | solution.py:61
  433.6 8.2 %collective-permute-done.21 = bf16[4,160,256]{2,1,0:T(8,128)(2,1)S(1)} collective-permute-done((bf16[4,160,256]{2,1,0:T(8,128)(2,1)S(1)}, bf16[4,160,256]{2,1,0:T(8,128)(2,1)S(1)}, u32[]{:S(2)}, u32[]{:S(2)}) %collective-permute-start.21) | collective-permute-done | bytes 327712 | tf_op jit(solution)/shard_map/ppermute | solution.py:61
  445.7 20.7 %all_to_all.118 = bf16[16,1,160,256]{3,2,1,0:T(8,128)(2,1)} all-to-all(bf16[16,1,160,256]{3,2,1,0:T(8,128)(2,1)S(1)} %bitcast.277), channel_id=1, replica_groups=mesh['leaf'=16,'col'=8] {'leaf'}, dimensions={0} | all-to-all | bytes 2621440 | tf_op jit(solution)/shard_map/all_to_all | solution.py:52
  468.1 19.4 %all_to_all.119 = bf16[16,1,160,256]{3,2,1,0:T(8,128)(2,1)S(1)} all-to-all(bf16[16,1,160,256]{3,2,1,0:T(8,128)(2,1)S(1)} %broadcast_in_dim.32), channel_id=1, replica_groups=mesh['leaf'=16,'col'=8] {'leaf'}, dimensions={0} | all-to-all | bytes 2621440 | tf_op jit(solution)/shard_map/all_to_all | solution.py:54
  489.7 17.9 %all_to_all.120 = bf16[8,1,160,256]{3,2,1,0:T(8,128)(2,1)S(1)} all-to-all(bf16[8,1,160,256]{3,2,1,0:T(8,128)(2,1)S(1)} %fusion.80), channel_id=1, replica_groups=mesh['leaf'=16,'col'=8] {'col'}, dimensions={0} | all-to-all | bytes 1310720 | tf_op jit(solution)/shard_map/all_to_all | solution.py:52
  514.4 7.1 %slice.148 = bf16[64,160,320]{2,1,0:T(8,128)(2,1)} slice(bf16[98,160,320]{2,1,0:T(8,128)(2,1)} %param.8), slice={[0:64], [0:160], [0:320]} | slice | bytes 13107200 | tf_op jit(solution)/shard_map/slice | solution.py:119
  532.4 10.6 %fusion.3 = bf16[16,1,320,256]{3,2,1,0:T(8,128)(2,1)} fusion(bf16[16,4,160,320]{3,2,1,0:T(8,128)(2,1)} %bitcast.269, bf16[16,4,160,256]{3,0,2,1:T(8,128)(2,1)} %pad_maximum_fusion), kind=kOutput, calls=%fused_computation.10 | convolution fusion | flops 1679032320 | bytes 14417920 | tf_op jit(solution)/shard_map/sdoj,sdoh->sjh/dot_general | solution.py:134
  543.0 37.4 %all_to_all.121 = bf16[16,1,320,256]{3,2,1,0:T(8,128)(2,1)} all-to-all(bf16[16,1,320,256]{3,2,1,0:T(8,128)(2,1)} %fusion.3), channel_id=1, replica_groups=mesh['leaf'=16,'col'=8] {'leaf'}, dimensions={0} | all-to-all | bytes 5242880 | tf_op jit(solution)/shard_map/all_to_all | solution.py:52
  582.8 35.7 %all_to_all.122 = bf16[16,1,320,256]{3,2,1,0:T(8,128)(2,1)S(1)} all-to-all(bf16[16,1,320,256]{3,2,1,0:T(8,128)(2,1)S(1)} %broadcast_in_dim.34), channel_id=1, replica_groups=mesh['leaf'=16,'col'=8] {'leaf'}, dimensions={0} | all-to-all | bytes 5242880 | tf_op jit(solution)/shard_map/all_to_all | solution.py:54
  619.4 25.4 %all_to_all.123 = bf16[8,2,160,256]{3,2,1,0:T(8,128)(2,1)S(1)} all-to-all(bf16[8,2,160,256]{3,2,1,0:T(8,128)(2,1)S(1)} %bitcast.273), channel_id=1, replica_groups=mesh['leaf'=16,'col'=8] {'col'}, dimensions={0} | all-to-all | bytes 2621440 | tf_op jit(solution)/shard_map/all_to_all | solution.py:52
  645.2 21.4 %all_to_all.124 = bf16[8,2,160,256]{3,2,1,0:T(8,128)(2,1)S(1)} all-to-all(bf16[8,2,160,256]{3,2,1,0:T(8,128)(2,1)S(1)} %broadcast_in_dim.35), channel_id=1, replica_groups=mesh['leaf'=16,'col'=8] {'col'}, dimensions={0} | all-to-all | bytes 2621440 | tf_op jit(solution)/shard_map/all_to_all | solution.py:54
  (227 shorter events, 201.9 us)
Async XLA Ops:
  0.0 49.5 %copy-start = (s32[31]{0:T(128)S(1)}, s32[31]{0:T(128)}, u32[]{:S(2)}) copy-start(s32[31]{0:T(128)} %param.9) | copy-start | bytes 376
  45.1 35.0 %all-to-all-start.1 = ((bf16[16,1,320,256]{3,2,1,0:T(8,128)(2,1)}), bf16[16,1,320,256]{3,2,1,0:T(8,128)(2,1)S(1)}, u32[]{:S(2)}, u32[]{:S(2)}) async-start(bf16[16,1,320,256]{3,2,1,0:T(8,128)(2,1)} %broadcast_in_dim.25), calls=%async_computation.1 | async-start | bytes 5242880 | tf_op jit(solution)/shard_map/all_to_all | solution.py:54
  50.2 285.3 %copy-start.19 = (s32[31]{0:T(128)}, s32[31]{0:T(128)S(1)}, u32[]{:S(2)}) copy-start(s32[31]{0:T(128)S(1)} %get-tuple-element.10) | copy-start | bytes 376
  148.5 21.7 %all-to-all-start.5 = ((bf16[16,1,160,256]{3,2,1,0:T(8,128)(2,1)}), bf16[16,1,160,256]{3,2,1,0:T(8,128)(2,1)}, u32[]{:S(2)}, u32[]{:S(2)}) async-start(bf16[16,1,160,256]{3,2,1,0:T(8,128)(2,1)} %broadcast_in_dim.27), calls=%async_computation.5 | async-start | bytes 2621440 | tf_op jit(solution)/shard_map/all_to_all | solution.py:54
  174.0 5.1 collective-permute-start
  179.4 9.0 %collective-permute-start.1 = (bf16[4,160,256]{2,0,1:T(4,128)(2,1)S(1)}, bf16[4,160,256]{2,0,1:T(4,128)(2,1)S(1)}, u32[]{:S(2)}, u32[]{:S(2)}) collective-permute-start(bf16[4,160,256]{2,0,1:T(4,128)(2,1)S(1)} %add_convert_fusion.5), channel_id=1, source_target_pairs={{0,2},{1,3},{2,0},{3,1},{4,6},{5,7},{6,4},{7,5},{8,10},{9,11},{10,... | collective-permute-start | bytes 983048 | tf_op jit(solution)/shard_map/ppermute | solution.py:61
  188.5 9.6 %collective-permute-start.2 = (bf16[4,160,256]{2,0,1:T(4,128)(2,1)S(1)}, bf16[4,160,256]{2,0,1:T(4,128)(2,1)S(1)}, u32[]{:S(2)}, u32[]{:S(2)}) collective-permute-start(bf16[4,160,256]{2,0,1:T(4,128)(2,1)S(1)} %add_convert_fusion.4), channel_id=1, source_target_pairs={{0,4},{1,5},{2,6},{3,7},{4,0},{5,1},{6,2},{7,3},{8,12},{9,13},{10,... | collective-permute-start | bytes 983048 | tf_op jit(solution)/shard_map/ppermute | solution.py:61
  201.0 13.8 %all-to-all-start.6 = ((bf16[16,1,80,256]{3,2,1,0:T(8,128)(2,1)}), bf16[16,1,80,256]{3,2,1,0:T(8,128)(2,1)S(1)}, u32[]{:S(2)}, u32[]{:S(2)}) async-start(bf16[16,1,80,256]{3,2,1,0:T(8,128)(2,1)} %bitcast.274), calls=%async_computation.6 | async-start | bytes 1310720 | tf_op jit(solution)/shard_map/all_to_all | solution.py:52
  215.8 13.7 %all-to-all-start.7 = ((bf16[16,1,80,256]{3,2,1,0:T(8,128)(2,1)}), bf16[16,1,80,256]{3,2,1,0:T(8,128)(2,1)S(1)}, u32[]{:S(2)}, u32[]{:S(2)}) async-start(bf16[16,1,80,256]{3,2,1,0:T(8,128)(2,1)} %broadcast_in_dim.28), calls=%async_computation.7 | async-start | bytes 1310720 | tf_op jit(solution)/shard_map/all_to_all | solution.py:54
  235.7 5.8 collective-permute-start.3
  241.7 5.5 collective-permute-start.4
  247.4 6.1 collective-permute-start.5
  255.8 12.2 %all-to-all-start.8 = ((bf16[16,1,40,256]{3,2,1,0:T(8,128)(2,1)}), bf16[16,1,40,256]{3,2,1,0:T(8,128)(2,1)}, u32[]{:S(2)}, u32[]{:S(2)}) async-start(bf16[16,1,40,256]{3,2,1,0:T(8,128)(2,1)} %bitcast.278), calls=%async_computation.8 | async-start | bytes 655360 | tf_op jit(solution)/shard_map/all_to_all | solution.py:52
  269.8 11.9 %all-to-all-start.9 = ((bf16[16,1,40,256]{3,2,1,0:T(8,128)(2,1)}), bf16[16,1,40,256]{3,2,1,0:T(8,128)(2,1)}, u32[]{:S(2)}, u32[]{:S(2)}) async-start(bf16[16,1,40,256]{3,2,1,0:T(8,128)(2,1)} %broadcast_in_dim.29), calls=%async_computation.9 | async-start | bytes 655360 | tf_op jit(solution)/shard_map/all_to_all | solution.py:54
  284.9 5.7 collective-permute-start.6
  290.6 3.8 collective-permute-start.7
  294.4 4.9 collective-permute-start.8
  300.5 4.2 collective-permute-start.9
  304.8 5.8 collective-permute-start.10
  310.6 4.5 collective-permute-start.11
  315.2 7.2 %collective-permute-start.12 = (bf16[1,320,256]{2,1,0:T(8,128)(2,1)S(1)}, bf16[1,320,256]{2,1,0:T(8,128)(2,1)S(1)}, u32[]{:S(2)}, u32[]{:S(2)}) collective-permute-start(bf16[1,320,256]{2,1,0:T(8,128)(2,1)S(1)} %add_convert_fusion.10), channel_id=1, source_target_pairs={{0,64},{8,72},{16,80},{24,88},{32,96},{40,104},{48,112},{56,120},{... | collective-permute-start | bytes 491528 | tf_op jit(solution)/shard_map/ppermute | solution.py:61
  323.5 7.4 %collective-permute-start.13 = (bf16[1,160,256]{2,1,0:T(8,128)(2,1)S(1)}, bf16[1,160,256]{2,1,0:T(8,128)(2,1)S(1)}, u32[]{:S(2)}, u32[]{:S(2)}) collective-permute-start(bf16[1,160,256]{2,1,0:T(8,128)(2,1)S(1)} %fusion.105), channel_id=1, source_target_pairs={{0,1},{1,0},{2,3},{3,2},{4,5},{5,4},{6,7},{7,6},{8,9},{9,8},{10,11... | collective-permute-start | bytes 245768 | tf_op jit(solution)/shard_map/ppermute | solution.py:61
  331.0 3.8 collective-permute-start.14
  334.8 4.9 collective-permute-start.15
  366.4 6.0 collective-permute-start.16
  372.5 5.5 collective-permute-start.17
  378.0 6.1 collective-permute-start.18
  417.0 6.0 collective-permute-start.19
  423.1 9.0 %collective-permute-start.20 = (bf16[4,160,256]{2,1,0:T(8,128)(2,1)S(1)}, bf16[4,160,256]{2,1,0:T(8,128)(2,1)S(1)}, u32[]{:S(2)}, u32[]{:S(2)}) collective-permute-start(bf16[4,160,256]{2,1,0:T(8,128)(2,1)S(1)} %add_convert_fusion.2), channel_id=1, source_target_pairs={{0,2},{1,3},{2,0},{3,1},{4,6},{5,7},{6,4},{7,5},{8,10},{9,11},{10,... | collective-permute-start | bytes 983048 | tf_op jit(solution)/shard_map/ppermute | solution.py:61
  432.2 9.6 %collective-permute-start.21 = (bf16[4,160,256]{2,1,0:T(8,128)(2,1)S(1)}, bf16[4,160,256]{2,1,0:T(8,128)(2,1)S(1)}, u32[]{:S(2)}, u32[]{:S(2)}) collective-permute-start(bf16[4,160,256]{2,1,0:T(8,128)(2,1)S(1)} %add_convert_fusion.1), channel_id=1, source_target_pairs={{0,4},{1,5},{2,6},{3,7},{4,0},{5,1},{6,2},{7,3},{8,12},{9,13},{10,... | collective-permute-start | bytes 983048 | tf_op jit(solution)/shard_map/ppermute | solution.py:61
  510.1 16.4 %all-to-all-start.17 = ((bf16[8,1,160,256]{3,2,1,0:T(8,128)(2,1)}), bf16[8,1,160,256]{3,2,1,0:T(8,128)(2,1)S(1)}, u32[]{:S(2)}, u32[]{:S(2)}) async-start(bf16[8,1,160,256]{3,2,1,0:T(8,128)(2,1)} %broadcast_in_dim.33), calls=%async_computation.17 | async-start | bytes 1310720 | tf_op jit(solution)/shard_map/all_to_all | solution.py:54
  582.8 35.7 %copy-start.3 = (bf16[31,320,160]{1,2,0:T(8,128)(2,1)S(1)}, bf16[31,320,160]{1,2,0:T(8,128)(2,1)}, u32[]{:S(2)}) copy-start(bf16[31,320,160]{1,2,0:T(8,128)(2,1)} %param.7) | copy-start | bytes 9523204
  (30 other events, 319.6 us)

commit v5 on v3

--- a/solution.py
+++ b/solution.py
@@ -64,7 +64,7 @@
 
 
 def group_allreduce(x, axis, n):
-    small = 1 if axis == "leaf" else 4
+    small = 1 if axis == "leaf" else 2
     if x.shape[0] <= small:
         return doubling_allreduce(x, axis, n)
     return a2a_allreduce(x, axis, n)

time: 675 us -> 679 us (level)
  blocking collectives: 284 us -> 309 us
  waiting for transfers between devices: 173 us -> 148 us
    ppermute x22 -> x16, waiting for transfers between devices: 89.1 us -> 53.8 us  [doubling_allreduce(): lax.ppermute(x, axis, xor_perm(n, bit)).astype(jnp.float32)]
    all_to_all x8 -> x9, blocking collectives: 189 us -> 202 us  [a2a_allreduce(): got = lax.all_to_all(pieces, axis, 0, 0, tiled=False)]
    ppermute x22 -> x16, starting transfers between devices: 39 us -> 27 us  [doubling_allreduce(): lax.ppermute(x, axis, xor_perm(n, bit)).astype(jnp.float32)]
    all_to_all x5 -> x6, blocking collectives: 95.7 us -> 107 us  [a2a_allreduce(): lax.all_to_all(jnp.broadcast_to(owned[None], (n,) + owned.shape), axis, 0...]
    all_to_all x3 -> x4, starting transfers between devices: 15.7 us -> 23.8 us  [a2a_allreduce(): got = lax.all_to_all(pieces, axis, 0, 0, tiled=False)]
    all_to_all x3 -> x4, waiting for transfers between devices: 16.2 us -> 22.4 us  [a2a_allreduce(): got = lax.all_to_all(pieces, axis, 0, 0, tiled=False)]
    all_to_all x6 -> x7, waiting for transfers between devices: 67.3 us -> 72.2 us  [a2a_allreduce(): lax.all_to_all(jnp.broadcast_to(owned[None], (n,) + owned.shape), axis, 0...]
    all_to_all x6 -> x7, starting transfers between devices: 26.1 us -> 30.6 us  [a2a_allreduce(): lax.all_to_all(jnp.broadcast_to(owned[None], (n,) + owned.shape), axis, 0...]
  transfers between devices with their start and end apart: 31 -> 27, of which waited for: 31 -> 27; matrix products, arithmetic and copies ran while one was open for 7% -> 7% of each run, Pallas kernels for 0% -> 0%
where the time goes in v5:
time: 679 us; the launch traced here: 670 us
  blocking collectives  309 us (46%)
  waiting for transfers between devices  148 us (22%)
  matrix products  98.4 us (14%)
  starting transfers between devices  81.4 us (12%)
  local copies, waits for them, and re-layouts  16.1 us (2%)
  other arithmetic  15.9 us (2%)
    all_to_all x9, blocking collectives, a2a_allreduce(): got = lax.all_to_all(pieces, axis, 0, 0, tiled=False)  202 us
    all_to_all x6, blocking collectives, a2a_allreduce(): lax.all_to_all(jnp.broadcast_to(owned[None], (n,) + owned.shape), axis, 0...  107 us
    all_to_all x7, waiting for transfers between devices, a2a_allreduce(): lax.all_to_all(jnp.broadcast_to(owned[None], (n,) + owned.shape), axis, 0...  72.2 us
    ppermute x16, waiting for transfers between devices, doubling_allreduce(): lax.ppermute(x, axis, xor_perm(n, bit)).astype(jnp.float32)  53.8 us
    all_to_all x7, starting transfers between devices, a2a_allreduce(): lax.all_to_all(jnp.broadcast_to(owned[None], (n,) + owned.shape), axis, 0...  30.6 us
    dot_general x10, matrix products, solve(): jnp.einsum('boj,boh->bjh', pair_slice(panel_local, tree_level, distance),...  28.6 us
    ppermute x16, starting transfers between devices, doubling_allreduce(): lax.ppermute(x, axis, xor_perm(n, bit)).astype(jnp.float32)  27 us
    all_to_all x4, starting transfers between devices, a2a_allreduce(): got = lax.all_to_all(pieces, axis, 0, 0, tiled=False)  23.8 us
  transfers between devices with their start and end apart: 27, of which 27 were waited for; matrix products, arithmetic and copies ran while one was open for 7% of the time, Pallas kernels for 0%

profile of v5, /device:TPU:1, one launch (start us, length us, event | category | flops | bytes accessed | tf_op | source)
XLA Modules:
  0.0 670.4 jit_solution(11229427575914038210)
XLA Ops:
  3.3 39.6 %all_to_all.130 = bf16[16,1,320,256]{3,2,1,0:T(8,128)(2,1)S(1)} all-to-all(bf16[16,1,320,256]{3,2,1,0:T(8,128)(2,1)S(1)} %convert_bitcast_fusion), channel_id=1, replica_groups=mesh['leaf'=16,'col'=8] {'leaf'}, dimensions={0} | all-to-all | bytes 5242880 | tf_op jit(solution)/shard_map/all_to_all | solution.py:52
  50.2 29.9 %all-to-all-done.1 = bf16[16,1,320,256]{3,2,1,0:T(8,128)(2,1)S(1)} async-done(((bf16[16,1,320,256]{3,2,1,0:T(8,128)(2,1)}), bf16[16,1,320,256]{3,2,1,0:T(8,128)(2,1)S(1)}, u32[]{:S(2)}, u32[]{:S(2)}) %all-to-all-start.1) | async-done | bytes 2621472 | tf_op jit(solution)/shard_map/all_to_all | solution.py:54
  85.1 22.2 %all_to_all.131 = bf16[8,1,160,256]{3,2,1,0:T(8,128)(2,1)S(1)} all-to-all(bf16[8,1,160,256]{3,2,1,0:T(8,128)(2,1)S(1)} %copy.46), channel_id=1, replica_groups=mesh['leaf'=16,'col'=8] {'col'}, dimensions={0} | all-to-all | bytes 1310720 | tf_op jit(solution)/shard_map/all_to_all | solution.py:52
  107.5 14.2 %all_to_all.132 = bf16[8,1,160,256]{3,2,1,0:T(8,128)(2,1)S(1)} all-to-all(bf16[8,1,160,256]{3,2,1,0:T(8,128)(2,1)S(1)} %broadcast_in_dim.30), channel_id=1, replica_groups=mesh['leaf'=16,'col'=8] {'col'}, dimensions={0} | all-to-all | bytes 1310720 | tf_op jit(solution)/shard_map/all_to_all | solution.py:54
  123.9 22.0 %all_to_all.133 = bf16[16,1,160,256]{3,2,1,0:T(8,128)(2,1)} all-to-all(bf16[16,1,160,256]{3,2,1,0:T(8,128)(2,1)S(1)} %bitcast.241), channel_id=1, replica_groups=mesh['leaf'=16,'col'=8] {'leaf'}, dimensions={0} | all-to-all | bytes 2621440 | tf_op jit(solution)/shard_map/all_to_all | solution.py:52
  148.5 4.9 all-to-all-start.5
  159.1 11.5 %all-to-all-done.5 = bf16[16,1,160,256]{3,2,1,0:T(8,128)(2,1)} async-done(((bf16[16,1,160,256]{3,2,1,0:T(8,128)(2,1)}), bf16[16,1,160,256]{3,2,1,0:T(8,128)(2,1)}, u32[]{:S(2)}, u32[]{:S(2)}) %all-to-all-start.5) | async-done | bytes 1310752 | tf_op jit(solution)/shard_map/all_to_all | solution.py:54
  174.3 13.7 %all_to_all.134 = bf16[8,1,80,256]{3,2,1,0:T(8,128)(2,1)S(1)} all-to-all(bf16[8,1,80,256]{3,2,1,0:T(8,128)(2,1)S(1)} %bitcast.253), channel_id=1, replica_groups=mesh['leaf'=16,'col'=8] {'col'}, dimensions={0} | all-to-all | bytes 655360 | tf_op jit(solution)/shard_map/all_to_all | solution.py:52
  188.1 10.6 %all_to_all.135 = bf16[8,1,80,256]{3,2,1,0:T(8,128)(2,1)S(1)} all-to-all(bf16[8,1,80,256]{3,2,1,0:T(8,128)(2,1)S(1)} %broadcast_in_dim.32), channel_id=1, replica_groups=mesh['leaf'=16,'col'=8] {'col'}, dimensions={0} | all-to-all | bytes 655360 | tf_op jit(solution)/shard_map/all_to_all | solution.py:54
  206.4 10.0 %all-to-all-done.8 = bf16[16,1,80,256]{3,2,1,0:T(8,128)(2,1)S(1)} async-done(((bf16[16,1,80,256]{3,2,1,0:T(8,128)(2,1)}), bf16[16,1,80,256]{3,2,1,0:T(8,128)(2,1)S(1)}, u32[]{:S(2)}, u32[]{:S(2)}) %all-to-all-start.8) | async-done | bytes 655392 | tf_op jit(solution)/shard_map/all_to_all | solution.py:52
  277.8 4.6 all-to-all-done.11
  316.7 6.1 collective-permute-done.9
  323.9 6.5 collective-permute-start.10
  342.0 11.4 %all_to_all.136 = bf16[16,1,40,256]{3,2,1,0:T(8,128)(2,1)} all-to-all(bf16[16,1,40,256]{3,2,1,0:T(8,128)(2,1)S(1)} %bitcast.254), channel_id=1, replica_groups=mesh['leaf'=16,'col'=8] {'leaf'}, dimensions={0} | all-to-all | bytes 655360 | tf_op jit(solution)/shard_map/all_to_all | solution.py:52
  354.4 11.0 %all_to_all.137 = bf16[16,1,40,256]{3,2,1,0:T(8,128)(2,1)S(1)} all-to-all(bf16[16,1,40,256]{3,2,1,0:T(8,128)(2,1)S(1)} %broadcast_in_dim.35), channel_id=1, replica_groups=mesh['leaf'=16,'col'=8] {'leaf'}, dimensions={0} | all-to-all | bytes 655360 | tf_op jit(solution)/shard_map/all_to_all | solution.py:54
  366.8 5.0 collective-permute-start.13
  373.2 5.1 collective-permute-done.14
  379.3 5.2 collective-permute-done.15
  389.2 13.4 %all_to_all.138 = bf16[16,1,80,256]{3,2,1,0:T(8,128)(2,1)} all-to-all(bf16[16,1,80,256]{3,2,1,0:T(8,128)(2,1)S(1)} %bitcast.250), channel_id=1, replica_groups=mesh['leaf'=16,'col'=8] {'leaf'}, dimensions={0} | all-to-all | bytes 1310720 | tf_op jit(solution)/shard_map/all_to_all | solution.py:52
  405.2 13.4 %all_to_all.139 = bf16[16,1,80,256]{3,2,1,0:T(8,128)(2,1)S(1)} all-to-all(bf16[16,1,80,256]{3,2,1,0:T(8,128)(2,1)S(1)} %broadcast_in_dim.36), channel_id=1, replica_groups=mesh['leaf'=16,'col'=8] {'leaf'}, dimensions={0} | all-to-all | bytes 1310720 | tf_op jit(solution)/shard_map/all_to_all | solution.py:54
  420.7 8.0 %all-to-all-start.16 = ((bf16[8,1,80,256]{3,2,1,0:T(8,128)(2,1)}), bf16[8,1,80,256]{3,2,1,0:T(8,128)(2,1)S(1)}, u32[]{:S(2)}, u32[]{:S(2)}) async-start(bf16[8,1,80,256]{3,2,1,0:T(8,128)(2,1)} %bitcast.255), calls=%async_computation.16 | async-start | bytes 655360 | tf_op jit(solution)/shard_map/all_to_all | solution.py:52
  431.0 4.9 all-to-all-done.16
  453.1 21.2 %all_to_all.140 = bf16[16,1,160,256]{3,2,1,0:T(8,128)(2,1)} all-to-all(bf16[16,1,160,256]{3,2,1,0:T(8,128)(2,1)S(1)} %bitcast.246), channel_id=1, replica_groups=mesh['leaf'=16,'col'=8] {'leaf'}, dimensions={0} | all-to-all | bytes 2621440 | tf_op jit(solution)/shard_map/all_to_all | solution.py:52
  481.3 16.8 %all-to-all-done.19 = bf16[16,1,160,256]{3,2,1,0:T(8,128)(2,1)} async-done(((bf16[16,1,160,256]{3,2,1,0:T(8,128)(2,1)}), bf16[16,1,160,256]{3,2,1,0:T(8,128)(2,1)}, u32[]{:S(2)}, u32[]{:S(2)}) %all-to-all-start.19) | async-done | bytes 1310752 | tf_op jit(solution)/shard_map/all_to_all | solution.py:54
  501.6 7.8 %all-to-all-start.20 = ((bf16[8,1,160,256]{3,2,1,0:T(8,128)(2,1)}), bf16[8,1,160,256]{3,2,1,0:T(8,128)(2,1)S(1)}, u32[]{:S(2)}, u32[]{:S(2)}) async-start(bf16[8,1,160,256]{3,2,1,0:T(8,128)(2,1)} %fusion.70), calls=%async_computation.20 | async-start | bytes 1310720 | tf_op jit(solution)/shard_map/all_to_all | solution.py:52
  510.9 5.2 fusion.38
  522.7 4.5 all-to-all-start.21
  528.9 5.2 fusion.41
  546.0 35.4 %all_to_all.141 = bf16[16,1,320,256]{3,2,1,0:T(8,128)(2,1)} all-to-all(bf16[16,1,320,256]{3,2,1,0:T(8,128)(2,1)S(1)} %fusion.1), channel_id=1, replica_groups=mesh['leaf'=16,'col'=8] {'leaf'}, dimensions={0} | all-to-all | bytes 5242880 | tf_op jit(solution)/shard_map/all_to_all | solution.py:52
  583.8 36.3 %all_to_all.142 = bf16[16,1,320,256]{3,2,1,0:T(8,128)(2,1)S(1)} all-to-all(bf16[16,1,320,256]{3,2,1,0:T(8,128)(2,1)S(1)} %broadcast_in_dim.40), channel_id=1, replica_groups=mesh['leaf'=16,'col'=8] {'leaf'}, dimensions={0} | all-to-all | bytes 5242880 | tf_op jit(solution)/shard_map/all_to_all | solution.py:54
  621.1 23.5 %all_to_all.143 = bf16[8,2,160,256]{3,2,1,0:T(8,128)(2,1)S(1)} all-to-all(bf16[8,2,160,256]{3,2,1,0:T(8,128)(2,1)S(1)} %bitcast.247), channel_id=1, replica_groups=mesh['leaf'=16,'col'=8] {'col'}, dimensions={0} | all-to-all | bytes 2621440 | tf_op jit(solution)/shard_map/all_to_all | solution.py:52
  644.8 21.4 %all_to_all.144 = bf16[8,2,160,256]{3,2,1,0:T(8,128)(2,1)S(1)} all-to-all(bf16[8,2,160,256]{3,2,1,0:T(8,128)(2,1)S(1)} %broadcast_in_dim.41), channel_id=1, replica_groups=mesh['leaf'=16,'col'=8] {'col'}, dimensions={0} | all-to-all | bytes 2621440 | tf_op jit(solution)/shard_map/all_to_all | solution.py:54
  (212 shorter events, 219.2 us)
Async XLA Ops:
  0.0 49.5 %copy-start = (s32[31]{0:T(128)S(1)}, s32[31]{0:T(128)}, u32[]{:S(2)}) copy-start(s32[31]{0:T(128)} %param.9) | copy-start | bytes 376
  45.1 35.0 %all-to-all-start.1 = ((bf16[16,1,320,256]{3,2,1,0:T(8,128)(2,1)}), bf16[16,1,320,256]{3,2,1,0:T(8,128)(2,1)S(1)}, u32[]{:S(2)}, u32[]{:S(2)}) async-start(bf16[16,1,320,256]{3,2,1,0:T(8,128)(2,1)} %broadcast_in_dim.29), calls=%async_computation.1 | async-start | bytes 5242880 | tf_op jit(solution)/shard_map/all_to_all | solution.py:54
  50.2 32.3 %copy-start.14 = (s32[8]{0:T(128)}, s32[8]{0:T(128)S(1)}, u32[]{:S(2)}) copy-start(s32[8]{0:T(128)S(1)} %iota_add_fusion.2) | copy-start | bytes 100
  50.2 285.7 %copy-start.16 = (s32[31]{0:T(128)}, s32[31]{0:T(128)S(1)}, u32[]{:S(2)}) copy-start(s32[31]{0:T(128)S(1)} %get-tuple-element.10) | copy-start | bytes 376
  148.5 22.1 %all-to-all-start.5 = ((bf16[16,1,160,256]{3,2,1,0:T(8,128)(2,1)}), bf16[16,1,160,256]{3,2,1,0:T(8,128)(2,1)}, u32[]{:S(2)}, u32[]{:S(2)}) async-start(bf16[16,1,160,256]{3,2,1,0:T(8,128)(2,1)} %broadcast_in_dim.31), calls=%async_computation.5 | async-start | bytes 2621440 | tf_op jit(solution)/shard_map/all_to_all | solution.py:54
  201.2 15.2 %all-to-all-start.8 = ((bf16[16,1,80,256]{3,2,1,0:T(8,128)(2,1)}), bf16[16,1,80,256]{3,2,1,0:T(8,128)(2,1)S(1)}, u32[]{:S(2)}, u32[]{:S(2)}) async-start(bf16[16,1,80,256]{3,2,1,0:T(8,128)(2,1)} %bitcast.248), calls=%async_computation.8 | async-start | bytes 1310720 | tf_op jit(solution)/shard_map/all_to_all | solution.py:52
  204.9 27.9 %copy-start.24 = (s32[4]{0:T(128)}, s32[4]{0:T(128)S(1)}, u32[]{:S(2)}) copy-start(s32[4]{0:T(128)S(1)} %slice.128) | copy-start | bytes 52
  217.4 13.8 %all-to-all-start.9 = ((bf16[16,1,80,256]{3,2,1,0:T(8,128)(2,1)}), bf16[16,1,80,256]{3,2,1,0:T(8,128)(2,1)S(1)}, u32[]{:S(2)}, u32[]{:S(2)}) async-start(bf16[16,1,80,256]{3,2,1,0:T(8,128)(2,1)} %broadcast_in_dim.33), calls=%async_computation.9 | async-start | bytes 1310720 | tf_op jit(solution)/shard_map/all_to_all | solution.py:54
  237.4 4.8 collective-permute-start
  242.5 5.5 collective-permute-start.1
  248.1 6.1 collective-permute-start.2
  256.6 12.1 %all-to-all-start.10 = ((bf16[16,1,40,256]{3,2,1,0:T(8,128)(2,1)}), bf16[16,1,40,256]{3,2,1,0:T(8,128)(2,1)}, u32[]{:S(2)}, u32[]{:S(2)}) async-start(bf16[16,1,40,256]{3,2,1,0:T(8,128)(2,1)} %bitcast.251), calls=%async_computation.10 | async-start | bytes 655360 | tf_op jit(solution)/shard_map/all_to_all | solution.py:52
  270.4 11.9 %all-to-all-start.11 = ((bf16[16,1,40,256]{3,2,1,0:T(8,128)(2,1)}), bf16[16,1,40,256]{3,2,1,0:T(8,128)(2,1)}, u32[]{:S(2)}, u32[]{:S(2)}) async-start(bf16[16,1,40,256]{3,2,1,0:T(8,128)(2,1)} %broadcast_in_dim.34), calls=%async_computation.11 | async-start | bytes 655360 | tf_op jit(solution)/shard_map/all_to_all | solution.py:54
  285.6 5.4 collective-permute-start.3
  291.0 3.8 collective-permute-start.4
  294.8 4.9 collective-permute-start.5
  300.9 4.2 collective-permute-start.6
  305.2 5.8 collective-permute-start.7
  311.0 4.5 collective-permute-start.8
  315.6 7.2 %collective-permute-start.9 = (bf16[1,320,256]{2,1,0:T(8,128)(2,1)S(1)}, bf16[1,320,256]{2,1,0:T(8,128)(2,1)S(1)}, u32[]{:S(2)}, u32[]{:S(2)}) collective-permute-start(bf16[1,320,256]{2,1,0:T(8,128)(2,1)S(1)} %add_convert_fusion.6), channel_id=1, source_target_pairs={{0,64},{8,72},{16,80},{24,88},{32,96},{40,104},{48,112},{56,120},{... | collective-permute-start | bytes 491528 | tf_op jit(solution)/shard_map/ppermute | solution.py:61
  323.9 7.4 %collective-permute-start.10 = (bf16[1,160,256]{2,1,0:T(8,128)(2,1)S(1)}, bf16[1,160,256]{2,1,0:T(8,128)(2,1)S(1)}, u32[]{:S(2)}, u32[]{:S(2)}) collective-permute-start(bf16[1,160,256]{2,1,0:T(8,128)(2,1)S(1)} %fusion.93), channel_id=1, source_target_pairs={{0,1},{1,0},{2,3},{3,2},{4,5},{5,4},{6,7},{7,6},{8,9},{9,8},{10,11... | collective-permute-start | bytes 245768 | tf_op jit(solution)/shard_map/ppermute | solution.py:61
  331.4 3.8 collective-permute-start.11
  335.1 4.9 collective-permute-start.12
  366.8 6.0 collective-permute-start.13
  372.9 5.5 collective-permute-start.14
  378.4 6.1 collective-permute-start.15
  420.7 15.2 %all-to-all-start.16 = ((bf16[8,1,80,256]{3,2,1,0:T(8,128)(2,1)}), bf16[8,1,80,256]{3,2,1,0:T(8,128)(2,1)S(1)}, u32[]{:S(2)}, u32[]{:S(2)}) async-start(bf16[8,1,80,256]{3,2,1,0:T(8,128)(2,1)} %bitcast.255), calls=%async_computation.16 | async-start | bytes 655360 | tf_op jit(solution)/shard_map/all_to_all | solution.py:52
  436.7 11.6 %all-to-all-start.17 = ((bf16[8,1,80,256]{3,2,1,0:T(8,128)(2,1)}), bf16[8,1,80,256]{3,2,1,0:T(8,128)(2,1)S(1)}, u32[]{:S(2)}, u32[]{:S(2)}) async-start(bf16[8,1,80,256]{3,2,1,0:T(8,128)(2,1)} %broadcast_in_dim.37), calls=%async_computation.17 | async-start | bytes 655360 | tf_op jit(solution)/shard_map/all_to_all | solution.py:54
  476.9 21.3 %all-to-all-start.19 = ((bf16[16,1,160,256]{3,2,1,0:T(8,128)(2,1)}), bf16[16,1,160,256]{3,2,1,0:T(8,128)(2,1)}, u32[]{:S(2)}, u32[]{:S(2)}) async-start(bf16[16,1,160,256]{3,2,1,0:T(8,128)(2,1)} %broadcast_in_dim.38), calls=%async_computation.19 | async-start | bytes 2621440 | tf_op jit(solution)/shard_map/all_to_all | solution.py:54
  501.6 18.7 %all-to-all-start.20 = ((bf16[8,1,160,256]{3,2,1,0:T(8,128)(2,1)}), bf16[8,1,160,256]{3,2,1,0:T(8,128)(2,1)S(1)}, u32[]{:S(2)}, u32[]{:S(2)}) async-start(bf16[8,1,160,256]{3,2,1,0:T(8,128)(2,1)} %fusion.70), calls=%async_computation.20 | async-start | bytes 1310720 | tf_op jit(solution)/shard_map/all_to_all | solution.py:52
  522.7 15.4 %all-to-all-start.21 = ((bf16[8,1,160,256]{3,2,1,0:T(8,128)(2,1)}), bf16[8,1,160,256]{3,2,1,0:T(8,128)(2,1)S(1)}, u32[]{:S(2)}, u32[]{:S(2)}) async-start(bf16[8,1,160,256]{3,2,1,0:T(8,128)(2,1)} %broadcast_in_dim.39), calls=%async_computation.21 | async-start | bytes 1310720 | tf_op jit(solution)/shard_map/all_to_all | solution.py:54
  583.8 36.3 %copy-start.5 = (bf16[31,320,160]{1,2,0:T(8,128)(2,1)S(1)}, bf16[31,320,160]{1,2,0:T(8,128)(2,1)}, u32[]{:S(2)}) copy-start(bf16[31,320,160]{1,2,0:T(8,128)(2,1)} %param.7) | copy-start | bytes 9523204
  (23 other events, 179.5 us)

commit v6 on v5

--- a/solution.py
+++ b/solution.py
@@ -2,10 +2,12 @@
 import jax.numpy as jnp
 import numpy as np
 from jax import lax
-from jax.sharding import PartitionSpec as P
+from jax.sharding import Mesh, PartitionSpec as P
 
 level_starts = (0, 16, 24, 28, 30)
 level_counts = (16, 8, 4, 2, 1)
+LEAF = ("x", "y")
+COL = ("z", "core")
 
 
 def pair_offset(tree_level):
@@ -63,10 +65,28 @@
     return x
 
 
+def staged_allreduce(x, stages):
+    shape = x.shape
+    total = 1
+    for _, size in stages:
+        total *= size
+    cur = x.reshape((total, shape[0] // total) + shape[1:])
+    for axis, size in stages:
+        pieces = cur.reshape((size, cur.shape[0] // size) + cur.shape[1:])
+        got = lax.all_to_all(pieces, axis, 0, 0, tiled=False)
+        cur = jnp.sum(got.astype(jnp.float32), axis=0).astype(jnp.bfloat16)
+    for axis, size in reversed(stages):
+        spread = lax.all_to_all(jnp.broadcast_to(cur[None], (size,) + cur.shape), axis, 0, 0, tiled=False)
+        cur = spread.reshape((size * cur.shape[0],) + cur.shape[1:])
+    return cur.reshape(shape)
+
+
 def group_allreduce(x, axis, n):
-    small = 1 if axis == "leaf" else 2
+    small = 1 if axis == LEAF else 4
     if x.shape[0] <= small:
         return doubling_allreduce(x, axis, n)
+    if axis == COL and x.shape[0] >= 2 * n:
+        return staged_allreduce(x, (("core", 2), ("z", 4)))
     return a2a_allreduce(x, axis, n)
 
 
@@ -94,7 +114,7 @@
                 term = jnp.einsum("ks,sjr->kjr", onehot, products, precision=lax.Precision.HIGHEST)
                 partial_value = term if partial_value is None else partial_value + term
             reduced = reduced - group_allreduce(
-                partial_value.astype(jnp.bfloat16), "col", n_col
+                partial_value.astype(jnp.bfloat16), COL, n_col
             ).astype(jnp.float32)
         division_count = jnp.einsum(
             "kcl,klr->kcr",
@@ -103,7 +123,7 @@
             preferred_element_type=jnp.float32,
         )
         forward_value = group_allreduce(
-            division_count.astype(jnp.bfloat16), "leaf", n_leaf
+            division_count.astype(jnp.bfloat16), LEAF, n_leaf
         )
         forward_levels[tree_level] = forward_value.astype(jnp.float32)
         forward_half[tree_level] = forward_value
@@ -131,7 +151,7 @@
                 )
                 partial_value = term if partial_value is None else partial_value + term
             corrected = corrected - group_allreduce(
-                partial_value.astype(jnp.bfloat16), "leaf", n_leaf
+                partial_value.astype(jnp.bfloat16), LEAF, n_leaf
             ).astype(jnp.float32)
         division_count = jnp.einsum(
             "kcl,kcr->klr",
@@ -139,17 +159,18 @@
             corrected.astype(jnp.bfloat16),
             preferred_element_type=jnp.float32,
         )
-        solution = group_allreduce(division_count.astype(jnp.bfloat16), "col", n_col)
+        solution = group_allreduce(division_count.astype(jnp.bfloat16), COL, n_col)
         results[tree_level] = solution.astype(jnp.float32)
         solution_half[tree_level] = solution
     return jnp.concatenate(results, axis=0)
 
 
 def solution(mesh):
+    chips = Mesh(mesh.devices.reshape(4, 4, 4, 2), ("x", "y", "z", "core"))
     return jax.shard_map(
         solve,
-        mesh=mesh,
-        in_specs=(P(None, "leaf", None), P(None, "col", "leaf"), P(None, "leaf", "col"), P()),
-        out_specs=P(None, "leaf", None),
+        mesh=chips,
+        in_specs=(P(None, LEAF, None), P(None, COL, LEAF), P(None, LEAF, COL), P()),
+        out_specs=P(None, LEAF, None),
         check_vma=False,
     )

time: 679 us -> 669 us (0.985)
  blocking collectives: 309 us -> 279 us
  waiting for transfers between devices: 148 us -> 173 us
    all_to_all x0 -> x4, blocking collectives: none -> 39.2 us  [the longest x2 20.5 us: staged_allreduce(): got = lax.all_to_all(pieces, axis, 0, 0, tiled=False)]
    all_to_all x9 -> x7, blocking collectives: 202 us -> 165 us  [a2a_allreduce(): got = lax.all_to_all(pieces, axis, 0, 0, tiled=False)]
    ppermute x16 -> x22, waiting for transfers between devices: 53.8 us -> 89 us  [doubling_allreduce(): lax.ppermute(x, axis, xor_perm(n, bit)).astype(jnp.float32)]
    all_to_all x6 -> x4, blocking collectives: 107 us -> 74.2 us  [a2a_allreduce(): lax.all_to_all(jnp.broadcast_to(owned[None], (n,) + owned.shape), axis, 0...]
    ppermute x16 -> x22, starting transfers between devices: 27 us -> 39 us  [doubling_allreduce(): lax.ppermute(x, axis, xor_perm(n, bit)).astype(jnp.float32)]
    all_to_all x4 -> x3, starting transfers between devices: 23.8 us -> 15.7 us  [a2a_allreduce(): got = lax.all_to_all(pieces, axis, 0, 0, tiled=False)]
    all_to_all x4 -> x3, waiting for transfers between devices: 22.4 us -> 16.3 us  [a2a_allreduce(): got = lax.all_to_all(pieces, axis, 0, 0, tiled=False)]
    all_to_all x7 -> x6, waiting for transfers between devices: 72.2 us -> 67.3 us  [a2a_allreduce(): lax.all_to_all(jnp.broadcast_to(owned[None], (n,) + owned.shape), axis, 0...]
  transfers between devices with their start and end apart: 27 -> 31, of which waited for: 27 -> 31; matrix products, arithmetic and copies ran while one was open for 7% -> 7% of each run, Pallas kernels for 0% -> 0%
where the time goes in v6:
time: 669 us; the launch traced here: 661 us
  blocking collectives  279 us (42%)
  waiting for transfers between devices  173 us (26%)
  matrix products  94.7 us (14%)
  starting transfers between devices  80.9 us (12%)
  other arithmetic  17.4 us (3%)
  local copies, waits for them, and re-layouts  16.2 us (2%)
    all_to_all x7, blocking collectives, a2a_allreduce(): got = lax.all_to_all(pieces, axis, 0, 0, tiled=False)  165 us
    ppermute x22, waiting for transfers between devices, doubling_allreduce(): lax.ppermute(x, axis, xor_perm(n, bit)).astype(jnp.float32)  89 us
    all_to_all x4, blocking collectives, a2a_allreduce(): lax.all_to_all(jnp.broadcast_to(owned[None], (n,) + owned.shape), axis, 0...  74.2 us
    all_to_all x6, waiting for transfers between devices, a2a_allreduce(): lax.all_to_all(jnp.broadcast_to(owned[None], (n,) + owned.shape), axis, 0...  67.3 us
    ppermute x22, starting transfers between devices, doubling_allreduce(): lax.ppermute(x, axis, xor_perm(n, bit)).astype(jnp.float32)  39 us
    dot_general x10, matrix products, solve(): jnp.einsum('boj,boh->bjh', pair_slice(panel_local, tree_level, distance),...  26.5 us
    all_to_all x6, starting transfers between devices, a2a_allreduce(): lax.all_to_all(jnp.broadcast_to(owned[None], (n,) + owned.shape), axis, 0...  26.1 us
    dot_general x10, matrix products, solve(): jnp.einsum('sjv,svk->sjk', pair_slice(panel_local, source_level, distance...  21.7 us
  transfers between devices with their start and end apart: 31, of which 31 were waited for; matrix products, arithmetic and copies ran while one was open for 7% of the time, Pallas kernels for 0%

profile of v6, /device:TPU:1, one launch (start us, length us, event | category | flops | bytes accessed | tf_op | source)
XLA Modules:
  0.0 661.4 jit_solution(1196768609521874464)
XLA Ops:
  3.3 39.6 %all_to_all.120 = bf16[16,1,320,256]{3,2,1,0:T(8,128)(2,1)S(1)} all-to-all(bf16[16,1,320,256]{3,2,1,0:T(8,128)(2,1)S(1)} %convert_bitcast_fusion), channel_id=1, replica_groups=mesh['x'=4,'y'=4,'z'=4,'core'=2] {'x','y'}, dimensions={0} | all-to-all | bytes 5242880 | tf_op jit(solution)/shard_map/all_to_all | solution.py:54
  50.2 29.9 %all-to-all-done.1 = bf16[16,1,320,256]{3,2,1,0:T(8,128)(2,1)S(1)} async-done(((bf16[16,1,320,256]{3,2,1,0:T(8,128)(2,1)}), bf16[16,1,320,256]{3,2,1,0:T(8,128)(2,1)S(1)}, u32[]{:S(2)}, u32[]{:S(2)}) %all-to-all-start.1) | async-done | bytes 2621472 | tf_op jit(solution)/shard_map/all_to_all | solution.py:56
  85.1 22.2 %all_to_all.121 = bf16[8,1,160,256]{3,2,1,0:T(8,128)(2,1)S(1)} all-to-all(bf16[8,1,160,256]{3,2,1,0:T(8,128)(2,1)S(1)} %copy.15), channel_id=1, replica_groups=mesh['x'=4,'y'=4,'z'=4,'core'=2] {'z','core'}, dimensions={0} | all-to-all | bytes 1310720 | tf_op jit(solution)/shard_map/all_to_all | solution.py:54
  107.5 14.2 %all_to_all.122 = bf16[8,1,160,256]{3,2,1,0:T(8,128)(2,1)S(1)} all-to-all(bf16[8,1,160,256]{3,2,1,0:T(8,128)(2,1)S(1)} %broadcast_in_dim.30), channel_id=1, replica_groups=mesh['x'=4,'y'=4,'z'=4,'core'=2] {'z','core'}, dimensions={0} | all-to-all | bytes 1310720 | tf_op jit(solution)/shard_map/all_to_all | solution.py:56
  123.9 22.0 %all_to_all.123 = bf16[16,1,160,256]{3,2,1,0:T(8,128)(2,1)} all-to-all(bf16[16,1,160,256]{3,2,1,0:T(8,128)(2,1)S(1)} %bitcast.234), channel_id=1, replica_groups=mesh['x'=4,'y'=4,'z'=4,'core'=2] {'x','y'}, dimensions={0} | all-to-all | bytes 2621440 | tf_op jit(solution)/shard_map/all_to_all | solution.py:54
  148.5 4.9 all-to-all-start.5
  160.0 10.6 %all-to-all-done.5 = bf16[16,1,160,256]{3,2,1,0:T(8,128)(2,1)} async-done(((bf16[16,1,160,256]{3,2,1,0:T(8,128)(2,1)}), bf16[16,1,160,256]{3,2,1,0:T(8,128)(2,1)}, u32[]{:S(2)}, u32[]{:S(2)}) %all-to-all-start.5) | async-done | bytes 1310752 | tf_op jit(solution)/shard_map/all_to_all | solution.py:56
  180.0 8.6 %collective-permute-done.1 = bf16[4,160,256]{2,0,1:T(4,128)(2,1)S(1)} collective-permute-done((bf16[4,160,256]{2,0,1:T(4,128)(2,1)S(1)}, bf16[4,160,256]{2,0,1:T(4,128)(2,1)S(1)}, u32[]{:S(2)}, u32[]{:S(2)}) %collective-permute-start.1) | collective-permute-done | bytes 327712 | tf_op jit(solution)/shard_map/ppermute | solution.py:63
  189.6 8.8 %collective-permute-done.2 = bf16[4,160,256]{2,0,1:T(4,128)(2,1)S(1)} collective-permute-done((bf16[4,160,256]{2,0,1:T(4,128)(2,1)S(1)}, bf16[4,160,256]{2,0,1:T(4,128)(2,1)S(1)}, u32[]{:S(2)}, u32[]{:S(2)}) %collective-permute-start.2) | collective-permute-done | bytes 327712 | tf_op jit(solution)/shard_map/ppermute | solution.py:63
  206.5 8.6 %all-to-all-done.6 = bf16[16,1,80,256]{3,2,1,0:T(8,128)(2,1)S(1)} async-done(((bf16[16,1,80,256]{3,2,1,0:T(8,128)(2,1)}), bf16[16,1,80,256]{3,2,1,0:T(8,128)(2,1)S(1)}, u32[]{:S(2)}, u32[]{:S(2)}) %all-to-all-start.6) | async-done | bytes 655392 | tf_op jit(solution)/shard_map/all_to_all | solution.py:54
  316.4 6.1 collective-permute-done.12
  323.6 6.5 collective-permute-start.13
  341.6 11.4 %all_to_all.124 = bf16[16,1,40,256]{3,2,1,0:T(8,128)(2,1)} all-to-all(bf16[16,1,40,256]{3,2,1,0:T(8,128)(2,1)S(1)} %bitcast.245), channel_id=1, replica_groups=mesh['x'=4,'y'=4,'z'=4,'core'=2] {'x','y'}, dimensions={0} | all-to-all | bytes 655360 | tf_op jit(solution)/shard_map/all_to_all | solution.py:54
  354.1 11.0 %all_to_all.125 = bf16[16,1,40,256]{3,2,1,0:T(8,128)(2,1)S(1)} all-to-all(bf16[16,1,40,256]{3,2,1,0:T(8,128)(2,1)S(1)} %broadcast_in_dim.34), channel_id=1, replica_groups=mesh['x'=4,'y'=4,'z'=4,'core'=2] {'x','y'}, dimensions={0} | all-to-all | bytes 655360 | tf_op jit(solution)/shard_map/all_to_all | solution.py:56
  366.5 5.0 collective-permute-start.16
  372.9 5.1 collective-permute-done.17
  378.9 5.2 collective-permute-done.18
  388.9 13.4 %all_to_all.126 = bf16[16,1,80,256]{3,2,1,0:T(8,128)(2,1)} all-to-all(bf16[16,1,80,256]{3,2,1,0:T(8,128)(2,1)S(1)} %bitcast.241), channel_id=1, replica_groups=mesh['x'=4,'y'=4,'z'=4,'core'=2] {'x','y'}, dimensions={0} | all-to-all | bytes 1310720 | tf_op jit(solution)/shard_map/all_to_all | solution.py:54
  404.9 13.4 %all_to_all.127 = bf16[16,1,80,256]{3,2,1,0:T(8,128)(2,1)S(1)} all-to-all(bf16[16,1,80,256]{3,2,1,0:T(8,128)(2,1)S(1)} %broadcast_in_dim.35), channel_id=1, replica_groups=mesh['x'=4,'y'=4,'z'=4,'core'=2] {'x','y'}, dimensions={0} | all-to-all | bytes 1310720 | tf_op jit(solution)/shard_map/all_to_all | solution.py:56
  426.8 8.1 %collective-permute-done.20 = bf16[4,160,256]{2,1,0:T(8,128)(2,1)S(1)} collective-permute-done((bf16[4,160,256]{2,1,0:T(8,128)(2,1)S(1)}, bf16[4,160,256]{2,1,0:T(8,128)(2,1)S(1)}, u32[]{:S(2)}, u32[]{:S(2)}) %collective-permute-start.20) | collective-permute-done | bytes 327712 | tf_op jit(solution)/shard_map/ppermute | solution.py:63
  437.6 7.0 %collective-permute-done.21 = bf16[4,160,256]{2,1,0:T(8,128)(2,1)S(1)} collective-permute-done((bf16[4,160,256]{2,1,0:T(8,128)(2,1)S(1)}, bf16[4,160,256]{2,1,0:T(8,128)(2,1)S(1)}, u32[]{:S(2)}, u32[]{:S(2)}) %collective-permute-start.21) | collective-permute-done | bytes 327712 | tf_op jit(solution)/shard_map/ppermute | solution.py:63
  449.8 20.7 %all_to_all.128 = bf16[16,1,160,256]{3,2,1,0:T(8,128)(2,1)} all-to-all(bf16[16,1,160,256]{3,2,1,0:T(8,128)(2,1)S(1)} %bitcast.236), channel_id=1, replica_groups=mesh['x'=4,'y'=4,'z'=4,'core'=2] {'x','y'}, dimensions={0} | all-to-all | bytes 2621440 | tf_op jit(solution)/shard_map/all_to_all | solution.py:54
  477.6 16.9 %all-to-all-done.15 = bf16[16,1,160,256]{3,2,1,0:T(8,128)(2,1)} async-done(((bf16[16,1,160,256]{3,2,1,0:T(8,128)(2,1)}), bf16[16,1,160,256]{3,2,1,0:T(8,128)(2,1)}, u32[]{:S(2)}, u32[]{:S(2)}) %all-to-all-start.15) | async-done | bytes 1310752 | tf_op jit(solution)/shard_map/all_to_all | solution.py:56
  497.8 7.7 %all-to-all-start.16 = ((bf16[8,1,160,256]{3,2,1,0:T(8,128)(2,1)}), bf16[8,1,160,256]{3,2,1,0:T(8,128)(2,1)S(1)}, u32[]{:S(2)}, u32[]{:S(2)}) async-start(bf16[8,1,160,256]{3,2,1,0:T(8,128)(2,1)} %fusion.70), calls=%async_computation.16 | async-start | bytes 1310720 | tf_op jit(solution)/shard_map/all_to_all | solution.py:54
  507.1 5.2 fusion.38
  525.1 5.3 fusion.41
  542.2 36.1 %all_to_all.129 = bf16[16,1,320,256]{3,2,1,0:T(8,128)(2,1)} all-to-all(bf16[16,1,320,256]{3,2,1,0:T(8,128)(2,1)S(1)} %fusion.1), channel_id=1, replica_groups=mesh['x'=4,'y'=4,'z'=4,'core'=2] {'x','y'}, dimensions={0} | all-to-all | bytes 5242880 | tf_op jit(solution)/shard_map/all_to_all | solution.py:54
  580.7 35.6 %all_to_all.130 = bf16[16,1,320,256]{3,2,1,0:T(8,128)(2,1)S(1)} all-to-all(bf16[16,1,320,256]{3,2,1,0:T(8,128)(2,1)S(1)} %broadcast_in_dim.38), channel_id=1, replica_groups=mesh['x'=4,'y'=4,'z'=4,'core'=2] {'x','y'}, dimensions={0} | all-to-all | bytes 5242880 | tf_op jit(solution)/shard_map/all_to_all | solution.py:56
  617.2 7.5 %all_to_all.131 = bf16[2,4,2,160,256]{4,3,2,1,0:T(8,128)(2,1)S(1)} all-to-all(bf16[2,4,2,160,256]{4,3,2,1,0:T(8,128)(2,1)S(1)} %bitcast.237), channel_id=1, replica_groups=mesh['x'=4,'y'=4,'z'=4,'core'=2] {'core'}, dimensions={0} | all-to-all | bytes 2621440 | tf_op jit(solution)/shard_map/all_to_all | solution.py:76
  625.2 13.0 %all_to_all.132 = bf16[4,1,2,160,256]{4,3,2,1,0:T(8,128)(2,1)S(1)} all-to-all(bf16[4,1,2,160,256]{4,3,2,1,0:T(8,128)(2,1)S(1)} %bitcast.240), channel_id=1, replica_groups=mesh['x'=4,'y'=4,'z'=4,'core'=2] {'z'}, dimensions={0} | all-to-all | bytes 1310720 | tf_op jit(solution)/shard_map/all_to_all | solution.py:76
  638.4 12.1 %all_to_all.133 = bf16[4,1,2,160,256]{4,3,2,1,0:T(8,128)(2,1)S(1)} all-to-all(bf16[4,1,2,160,256]{4,3,2,1,0:T(8,128)(2,1)S(1)} %broadcast_in_dim.39), channel_id=1, replica_groups=mesh['x'=4,'y'=4,'z'=4,'core'=2] {'z'}, dimensions={0} | all-to-all | bytes 1310720 | tf_op jit(solution)/shard_map/all_to_all | solution.py:79
  650.7 6.5 all_to_all.134
  (227 shorter events, 232.3 us)
Async XLA Ops:
  45.1 35.0 %all-to-all-start.1 = ((bf16[16,1,320,256]{3,2,1,0:T(8,128)(2,1)}), bf16[16,1,320,256]{3,2,1,0:T(8,128)(2,1)S(1)}, u32[]{:S(2)}, u32[]{:S(2)}) async-start(bf16[16,1,320,256]{3,2,1,0:T(8,128)(2,1)} %broadcast_in_dim.29), calls=%async_computation.1 | async-start | bytes 5242880 | tf_op jit(solution)/shard_map/all_to_all | solution.py:56
  50.2 285.4 %copy-start.17 = (s32[31]{0:T(128)}, s32[31]{0:T(128)S(1)}, u32[]{:S(2)}) copy-start(s32[31]{0:T(128)S(1)} %get-tuple-element.10) | copy-start | bytes 376
  148.5 22.1 %all-to-all-start.5 = ((bf16[16,1,160,256]{3,2,1,0:T(8,128)(2,1)}), bf16[16,1,160,256]{3,2,1,0:T(8,128)(2,1)}, u32[]{:S(2)}, u32[]{:S(2)}) async-start(bf16[16,1,160,256]{3,2,1,0:T(8,128)(2,1)} %broadcast_in_dim.31), calls=%async_computation.5 | async-start | bytes 2621440 | tf_op jit(solution)/shard_map/all_to_all | solution.py:56
  174.4 5.1 collective-permute-start
  179.7 9.0 %collective-permute-start.1 = (bf16[4,160,256]{2,0,1:T(4,128)(2,1)S(1)}, bf16[4,160,256]{2,0,1:T(4,128)(2,1)S(1)}, u32[]{:S(2)}, u32[]{:S(2)}) collective-permute-start(bf16[4,160,256]{2,0,1:T(4,128)(2,1)S(1)} %add_convert_fusion.7), channel_id=1, source_target_pairs={{0,2},{1,3},{2,0},{3,1},{4,6},{5,7},{6,4},{7,5},{8,10},{9,11},{10,... | collective-permute-start | bytes 983048 | tf_op jit(solution)/shard_map/ppermute | solution.py:63
  188.8 9.6 %collective-permute-start.2 = (bf16[4,160,256]{2,0,1:T(4,128)(2,1)S(1)}, bf16[4,160,256]{2,0,1:T(4,128)(2,1)S(1)}, u32[]{:S(2)}, u32[]{:S(2)}) collective-permute-start(bf16[4,160,256]{2,0,1:T(4,128)(2,1)S(1)} %add_convert_fusion.6), channel_id=1, source_target_pairs={{0,4},{1,5},{2,6},{3,7},{4,0},{5,1},{6,2},{7,3},{8,12},{9,13},{10,... | collective-permute-start | bytes 983048 | tf_op jit(solution)/shard_map/ppermute | solution.py:63
  201.3 13.8 %all-to-all-start.6 = ((bf16[16,1,80,256]{3,2,1,0:T(8,128)(2,1)}), bf16[16,1,80,256]{3,2,1,0:T(8,128)(2,1)S(1)}, u32[]{:S(2)}, u32[]{:S(2)}) async-start(bf16[16,1,80,256]{3,2,1,0:T(8,128)(2,1)} %bitcast.238), calls=%async_computation.6 | async-start | bytes 1310720 | tf_op jit(solution)/shard_map/all_to_all | solution.py:54
  216.1 13.5 %all-to-all-start.7 = ((bf16[16,1,80,256]{3,2,1,0:T(8,128)(2,1)}), bf16[16,1,80,256]{3,2,1,0:T(8,128)(2,1)S(1)}, u32[]{:S(2)}, u32[]{:S(2)}) async-start(bf16[16,1,80,256]{3,2,1,0:T(8,128)(2,1)} %broadcast_in_dim.32), calls=%async_computation.7 | async-start | bytes 1310720 | tf_op jit(solution)/shard_map/all_to_all | solution.py:56
  235.8 5.8 collective-permute-start.3
  241.8 5.5 collective-permute-start.4
  247.4 6.1 collective-permute-start.5
  255.9 12.2 %all-to-all-start.8 = ((bf16[16,1,40,256]{3,2,1,0:T(8,128)(2,1)}), bf16[16,1,40,256]{3,2,1,0:T(8,128)(2,1)}, u32[]{:S(2)}, u32[]{:S(2)}) async-start(bf16[16,1,40,256]{3,2,1,0:T(8,128)(2,1)} %bitcast.243), calls=%async_computation.8 | async-start | bytes 655360 | tf_op jit(solution)/shard_map/all_to_all | solution.py:54
  269.9 11.9 %all-to-all-start.9 = ((bf16[16,1,40,256]{3,2,1,0:T(8,128)(2,1)}), bf16[16,1,40,256]{3,2,1,0:T(8,128)(2,1)}, u32[]{:S(2)}, u32[]{:S(2)}) async-start(bf16[16,1,40,256]{3,2,1,0:T(8,128)(2,1)} %broadcast_in_dim.33), calls=%async_computation.9 | async-start | bytes 655360 | tf_op jit(solution)/shard_map/all_to_all | solution.py:56
  285.0 5.7 collective-permute-start.6
  290.7 3.8 collective-permute-start.7
  294.5 4.9 collective-permute-start.8
  300.6 4.2 collective-permute-start.9
  304.9 5.8 collective-permute-start.10
  310.7 4.5 collective-permute-start.11
  315.3 7.2 %collective-permute-start.12 = (bf16[1,320,256]{2,1,0:T(8,128)(2,1)S(1)}, bf16[1,320,256]{2,1,0:T(8,128)(2,1)S(1)}, u32[]{:S(2)}, u32[]{:S(2)}) collective-permute-start(bf16[1,320,256]{2,1,0:T(8,128)(2,1)S(1)} %add_convert_fusion.12), channel_id=1, source_target_pairs={{0,64},{8,72},{16,80},{24,88},{32,96},{40,104},{48,112},{56,120},{... | collective-permute-start | bytes 491528 | tf_op jit(solution)/shard_map/ppermute | solution.py:63
  323.6 7.4 %collective-permute-start.13 = (bf16[1,160,256]{2,1,0:T(8,128)(2,1)S(1)}, bf16[1,160,256]{2,1,0:T(8,128)(2,1)S(1)}, u32[]{:S(2)}, u32[]{:S(2)}) collective-permute-start(bf16[1,160,256]{2,1,0:T(8,128)(2,1)S(1)} %fusion.94), channel_id=1, source_target_pairs={{0,1},{1,0},{2,3},{3,2},{4,5},{5,4},{6,7},{7,6},{8,9},{9,8},{10,11... | collective-permute-start | bytes 245768 | tf_op jit(solution)/shard_map/ppermute | solution.py:63
  331.1 3.8 collective-permute-start.14
  334.8 4.9 collective-permute-start.15
  366.5 6.0 collective-permute-start.16
  372.6 5.5 collective-permute-start.17
  378.1 6.1 collective-permute-start.18
  419.8 6.0 collective-permute-start.19
  425.9 9.0 %collective-permute-start.20 = (bf16[4,160,256]{2,1,0:T(8,128)(2,1)S(1)}, bf16[4,160,256]{2,1,0:T(8,128)(2,1)S(1)}, u32[]{:S(2)}, u32[]{:S(2)}) collective-permute-start(bf16[4,160,256]{2,1,0:T(8,128)(2,1)S(1)} %add_convert_fusion.4), channel_id=1, source_target_pairs={{0,2},{1,3},{2,0},{3,1},{4,6},{5,7},{6,4},{7,5},{8,10},{9,11},{10,... | collective-permute-start | bytes 983048 | tf_op jit(solution)/shard_map/ppermute | solution.py:63
  435.0 9.6 %collective-permute-start.21 = (bf16[4,160,256]{2,1,0:T(8,128)(2,1)S(1)}, bf16[4,160,256]{2,1,0:T(8,128)(2,1)S(1)}, u32[]{:S(2)}, u32[]{:S(2)}) collective-permute-start(bf16[4,160,256]{2,1,0:T(8,128)(2,1)S(1)} %add_convert_fusion.3), channel_id=1, source_target_pairs={{0,4},{1,5},{2,6},{3,7},{4,0},{5,1},{6,2},{7,3},{8,12},{9,13},{10,... | collective-permute-start | bytes 983048 | tf_op jit(solution)/shard_map/ppermute | solution.py:63
  473.1 21.3 %all-to-all-start.15 = ((bf16[16,1,160,256]{3,2,1,0:T(8,128)(2,1)}), bf16[16,1,160,256]{3,2,1,0:T(8,128)(2,1)}, u32[]{:S(2)}, u32[]{:S(2)}) async-start(bf16[16,1,160,256]{3,2,1,0:T(8,128)(2,1)} %broadcast_in_dim.36), calls=%async_computation.15 | async-start | bytes 2621440 | tf_op jit(solution)/shard_map/all_to_all | solution.py:56
  497.8 18.6 %all-to-all-start.16 = ((bf16[8,1,160,256]{3,2,1,0:T(8,128)(2,1)}), bf16[8,1,160,256]{3,2,1,0:T(8,128)(2,1)S(1)}, u32[]{:S(2)}, u32[]{:S(2)}) async-start(bf16[8,1,160,256]{3,2,1,0:T(8,128)(2,1)} %fusion.70), calls=%async_computation.16 | async-start | bytes 1310720 | tf_op jit(solution)/shard_map/all_to_all | solution.py:54
  518.9 15.4 %all-to-all-start.17 = ((bf16[8,1,160,256]{3,2,1,0:T(8,128)(2,1)}), bf16[8,1,160,256]{3,2,1,0:T(8,128)(2,1)S(1)}, u32[]{:S(2)}, u32[]{:S(2)}) async-start(bf16[8,1,160,256]{3,2,1,0:T(8,128)(2,1)} %broadcast_in_dim.37), calls=%async_computation.17 | async-start | bytes 1310720 | tf_op jit(solution)/shard_map/all_to_all | solution.py:56
  (29 other events, 359.1 us)

commit v7 on v6

--- a/solution.py
+++ b/solution.py
@@ -81,9 +81,25 @@
     return cur.reshape(shape)
 
 
+def col_halved_allreduce(x):
+    core = lax.axis_index("core")
+    swap = [(0, 1), (1, 0)]
+    halves = x.reshape((x.shape[0], 2, x.shape[1] // 2) + x.shape[2:])
+    keep = lax.dynamic_index_in_dim(halves, core, axis=1, keepdims=False)
+    send = lax.dynamic_index_in_dim(halves, 1 - core, axis=1, keepdims=False)
+    acc = (keep.astype(jnp.float32) + lax.ppermute(send, "core", swap).astype(jnp.float32)).astype(jnp.bfloat16)
+    acc = doubling_allreduce(acc, "z", 4)
+    other = lax.ppermute(acc, "core", swap)
+    low = jnp.where(core == 0, acc, other)
+    high = jnp.where(core == 0, other, acc)
+    return jnp.stack([low, high], axis=1).reshape(x.shape)
+
+
 def group_allreduce(x, axis, n):
     small = 1 if axis == LEAF else 4
     if x.shape[0] <= small:
+        if axis == COL:
+            return col_halved_allreduce(x)
         return doubling_allreduce(x, axis, n)
     if axis == COL and x.shape[0] >= 2 * n:
         return staged_allreduce(x, (("core", 2), ("z", 4)))

time: 669 us -> 668 us (level)
  waiting for transfers between devices: 173 us -> 162 us
    ppermute x0 -> x12, starting transfers between devices: none -> 36 us  [the longest x6 21.4 us: col_halved_allreduce(): lax.ppermute(send, 'core', swap).astype(jnp.float32)]
    ppermute x22 -> x16, starting transfers between devices: 39 us -> 9.35 us  [doubling_allreduce(): lax.ppermute(x, axis, xor_perm(n, bit)).astype(jnp.float32)]
    ppermute x22 -> x16, waiting for transfers between devices: 89 us -> 64.5 us  [doubling_allreduce(): lax.ppermute(x, axis, xor_perm(n, bit)).astype(jnp.float32)]
    ppermute x0 -> x12, waiting for transfers between devices: none -> 8.62 us  [the longest x6 5.07 us: col_halved_allreduce(): lax.ppermute(send, 'core', swap).astype(jnp.float32)]
  transfers between devices with their start and end apart: 31 -> 37, of which waited for: 31 -> 35; matrix products, arithmetic and copies ran while one was open for 7% -> 7% of each run, Pallas kernels for 0% -> 0%
where the time goes in v7:
time: 668 us; the launch traced here: 660 us
  blocking collectives  284 us (43%)
  waiting for transfers between devices  162 us (24%)
  matrix products  93.5 us (14%)
  starting transfers between devices  87 us (13%)
  other arithmetic  16.9 us (3%)
  local copies, waits for them, and re-layouts  15.7 us (2%)
    all_to_all x7, blocking collectives, a2a_allreduce(): got = lax.all_to_all(pieces, axis, 0, 0, tiled=False)  169 us
    all_to_all x4, blocking collectives, a2a_allreduce(): lax.all_to_all(jnp.broadcast_to(owned[None], (n,) + owned.shape), axis, 0...  76 us
    all_to_all x6, waiting for transfers between devices, a2a_allreduce(): lax.all_to_all(jnp.broadcast_to(owned[None], (n,) + owned.shape), axis, 0...  69.5 us
    ppermute x16, waiting for transfers between devices, doubling_allreduce(): lax.ppermute(x, axis, xor_perm(n, bit)).astype(jnp.float32)  64.5 us
    all_to_all x6, starting transfers between devices, a2a_allreduce(): lax.all_to_all(jnp.broadcast_to(owned[None], (n,) + owned.shape), axis, 0...  26.7 us
    dot_general x10, matrix products, solve(): jnp.einsum('boj,boh->bjh', pair_slice(panel_local, tree_level, distance),...  26.5 us
    dot_general x10, matrix products, solve(): jnp.einsum('sjv,svk->sjk', pair_slice(panel_local, source_level, distance...  21.6 us
    ppermute x6, starting transfers between devices, col_halved_allreduce(): lax.ppermute(send, 'core', swap).astype(jnp.float32)  21.4 us
  transfers between devices with their start and end apart: 37, of which 35 were waited for; matrix products, arithmetic and copies ran while one was open for 7% of the time, Pallas kernels for 0%

profile of v7, /device:TPU:1, one launch (start us, length us, event | category | flops | bytes accessed | tf_op | source)
XLA Modules:
  0.0 659.9 jit_solution(6399359320178770328)
XLA Ops:
  3.3 39.6 %all_to_all.120 = bf16[16,1,320,256]{3,2,1,0:T(8,128)(2,1)S(1)} all-to-all(bf16[16,1,320,256]{3,2,1,0:T(8,128)(2,1)S(1)} %convert_bitcast_fusion), channel_id=1, replica_groups=mesh['x'=4,'y'=4,'z'=4,'core'=2] {'x','y'}, dimensions={0} | all-to-all | bytes 5242880 | tf_op jit(solution)/shard_map/all_to_all | solution.py:54
  50.2 29.9 %all-to-all-done.1 = bf16[16,1,320,256]{3,2,1,0:T(8,128)(2,1)S(1)} async-done(((bf16[16,1,320,256]{3,2,1,0:T(8,128)(2,1)}), bf16[16,1,320,256]{3,2,1,0:T(8,128)(2,1)S(1)}, u32[]{:S(2)}, u32[]{:S(2)}) %all-to-all-start.1) | async-done | bytes 2621472 | tf_op jit(solution)/shard_map/all_to_all | solution.py:56
  85.1 22.2 %all_to_all.121 = bf16[8,1,160,256]{3,2,1,0:T(8,128)(2,1)S(1)} all-to-all(bf16[8,1,160,256]{3,2,1,0:T(8,128)(2,1)S(1)} %copy.85), channel_id=1, replica_groups=mesh['x'=4,'y'=4,'z'=4,'core'=2] {'z','core'}, dimensions={0} | all-to-all | bytes 1310720 | tf_op jit(solution)/shard_map/all_to_all | solution.py:54
  107.5 14.2 %all_to_all.122 = bf16[8,1,160,256]{3,2,1,0:T(8,128)(2,1)S(1)} all-to-all(bf16[8,1,160,256]{3,2,1,0:T(8,128)(2,1)S(1)} %broadcast_in_dim.30), channel_id=1, replica_groups=mesh['x'=4,'y'=4,'z'=4,'core'=2] {'z','core'}, dimensions={0} | all-to-all | bytes 1310720 | tf_op jit(solution)/shard_map/all_to_all | solution.py:56
  123.9 22.0 %all_to_all.123 = bf16[16,1,160,256]{3,2,1,0:T(8,128)(2,1)} all-to-all(bf16[16,1,160,256]{3,2,1,0:T(8,128)(2,1)S(1)} %bitcast.303), channel_id=1, replica_groups=mesh['x'=4,'y'=4,'z'=4,'core'=2] {'x','y'}, dimensions={0} | all-to-all | bytes 2621440 | tf_op jit(solution)/shard_map/all_to_all | solution.py:54
  148.5 4.6 all-to-all-start.5
  158.8 11.5 %all-to-all-done.5 = bf16[16,1,160,256]{3,2,1,0:T(8,128)(2,1)} async-done(((bf16[16,1,160,256]{3,2,1,0:T(8,128)(2,1)}), bf16[16,1,160,256]{3,2,1,0:T(8,128)(2,1)}, u32[]{:S(2)}, u32[]{:S(2)}) %all-to-all-start.5) | async-done | bytes 1310752 | tf_op jit(solution)/shard_map/all_to_all | solution.py:56
  179.4 5.1 collective-permute-done.1
  185.3 5.3 collective-permute-done.2
  200.9 10.5 %all-to-all-done.6 = bf16[16,1,80,256]{3,2,1,0:T(8,128)(2,1)S(1)} async-done(((bf16[16,1,80,256]{3,2,1,0:T(8,128)(2,1)}), bf16[16,1,80,256]{3,2,1,0:T(8,128)(2,1)S(1)}, u32[]{:S(2)}, u32[]{:S(2)}) %all-to-all-start.6) | async-done | bytes 655392 | tf_op jit(solution)/shard_map/all_to_all | solution.py:54
  276.8 4.7 all-to-all-done.9
  300.8 5.3 collective-permute-done.12
  307.4 4.8 collective-permute-done.13
  317.7 4.7 collective-permute-done.15
  341.2 11.3 %all_to_all.124 = bf16[16,1,40,256]{3,2,1,0:T(8,128)(2,1)} all-to-all(bf16[16,1,40,256]{3,2,1,0:T(8,128)(2,1)S(1)} %bitcast.323), channel_id=1, replica_groups=mesh['x'=4,'y'=4,'z'=4,'core'=2] {'x','y'}, dimensions={0} | all-to-all | bytes 655360 | tf_op jit(solution)/shard_map/all_to_all | solution.py:54
  353.6 11.5 %all_to_all.125 = bf16[16,1,40,256]{3,2,1,0:T(8,128)(2,1)S(1)} all-to-all(bf16[16,1,40,256]{3,2,1,0:T(8,128)(2,1)S(1)} %broadcast_in_dim.34), channel_id=1, replica_groups=mesh['x'=4,'y'=4,'z'=4,'core'=2] {'x','y'}, dimensions={0} | all-to-all | bytes 655360 | tf_op jit(solution)/shard_map/all_to_all | solution.py:56
  386.6 15.5 %all_to_all.126 = bf16[16,1,80,256]{3,2,1,0:T(8,128)(2,1)} all-to-all(bf16[16,1,80,256]{3,2,1,0:T(8,128)(2,1)S(1)} %bitcast.317), channel_id=1, replica_groups=mesh['x'=4,'y'=4,'z'=4,'core'=2] {'x','y'}, dimensions={0} | all-to-all | bytes 1310720 | tf_op jit(solution)/shard_map/all_to_all | solution.py:54
  404.8 14.0 %all_to_all.127 = bf16[16,1,80,256]{3,2,1,0:T(8,128)(2,1)S(1)} all-to-all(bf16[16,1,80,256]{3,2,1,0:T(8,128)(2,1)S(1)} %broadcast_in_dim.35), channel_id=1, replica_groups=mesh['x'=4,'y'=4,'z'=4,'core'=2] {'x','y'}, dimensions={0} | all-to-all | bytes 1310720 | tf_op jit(solution)/shard_map/all_to_all | solution.py:56
  424.9 5.1 collective-permute-done.25
  431.2 4.8 collective-permute-done.26
  445.4 22.4 %all_to_all.128 = bf16[16,1,160,256]{3,2,1,0:T(8,128)(2,1)} all-to-all(bf16[16,1,160,256]{3,2,1,0:T(8,128)(2,1)S(1)} %bitcast.308), channel_id=1, replica_groups=mesh['x'=4,'y'=4,'z'=4,'core'=2] {'x','y'}, dimensions={0} | all-to-all | bytes 2621440 | tf_op jit(solution)/shard_map/all_to_all | solution.py:54
  474.9 18.0 %all-to-all-done.15 = bf16[16,1,160,256]{3,2,1,0:T(8,128)(2,1)} async-done(((bf16[16,1,160,256]{3,2,1,0:T(8,128)(2,1)}), bf16[16,1,160,256]{3,2,1,0:T(8,128)(2,1)}, u32[]{:S(2)}, u32[]{:S(2)}) %all-to-all-start.15) | async-done | bytes 1310752 | tf_op jit(solution)/shard_map/all_to_all | solution.py:56
  496.3 7.0 %all-to-all-start.16 = ((bf16[8,1,160,256]{3,2,1,0:T(8,128)(2,1)}), bf16[8,1,160,256]{3,2,1,0:T(8,128)(2,1)S(1)}, u32[]{:S(2)}, u32[]{:S(2)}) async-start(bf16[8,1,160,256]{3,2,1,0:T(8,128)(2,1)} %fusion.70), calls=%async_computation.16 | async-start | bytes 1310720 | tf_op jit(solution)/shard_map/all_to_all | solution.py:54
  504.9 5.2 fusion.38
  516.8 4.6 all-to-all-start.17
  523.0 5.2 fusion.41
  540.2 35.7 %all_to_all.129 = bf16[16,1,320,256]{3,2,1,0:T(8,128)(2,1)} all-to-all(bf16[16,1,320,256]{3,2,1,0:T(8,128)(2,1)S(1)} %fusion.1), channel_id=1, replica_groups=mesh['x'=4,'y'=4,'z'=4,'core'=2] {'x','y'}, dimensions={0} | all-to-all | bytes 5242880 | tf_op jit(solution)/shard_map/all_to_all | solution.py:54
  578.2 36.3 %all_to_all.130 = bf16[16,1,320,256]{3,2,1,0:T(8,128)(2,1)S(1)} all-to-all(bf16[16,1,320,256]{3,2,1,0:T(8,128)(2,1)S(1)} %broadcast_in_dim.38), channel_id=1, replica_groups=mesh['x'=4,'y'=4,'z'=4,'core'=2] {'x','y'}, dimensions={0} | all-to-all | bytes 5242880 | tf_op jit(solution)/shard_map/all_to_all | solution.py:56
  615.5 7.5 %all_to_all.131 = bf16[2,4,2,160,256]{4,3,2,1,0:T(8,128)(2,1)S(1)} all-to-all(bf16[2,4,2,160,256]{4,3,2,1,0:T(8,128)(2,1)S(1)} %bitcast.309), channel_id=1, replica_groups=mesh['x'=4,'y'=4,'z'=4,'core'=2] {'core'}, dimensions={0} | all-to-all | bytes 2621440 | tf_op jit(solution)/shard_map/all_to_all | solution.py:76
  623.5 13.0 %all_to_all.132 = bf16[4,1,2,160,256]{4,3,2,1,0:T(8,128)(2,1)S(1)} all-to-all(bf16[4,1,2,160,256]{4,3,2,1,0:T(8,128)(2,1)S(1)} %bitcast.312), channel_id=1, replica_groups=mesh['x'=4,'y'=4,'z'=4,'core'=2] {'z'}, dimensions={0} | all-to-all | bytes 1310720 | tf_op jit(solution)/shard_map/all_to_all | solution.py:76
  636.7 12.1 %all_to_all.133 = bf16[4,1,2,160,256]{4,3,2,1,0:T(8,128)(2,1)S(1)} all-to-all(bf16[4,1,2,160,256]{4,3,2,1,0:T(8,128)(2,1)S(1)} %broadcast_in_dim.39), channel_id=1, replica_groups=mesh['x'=4,'y'=4,'z'=4,'core'=2] {'z'}, dimensions={0} | all-to-all | bytes 1310720 | tf_op jit(solution)/shard_map/all_to_all | solution.py:79
  648.9 6.5 all_to_all.134
  (259 shorter events, 238.2 us)
Async XLA Ops:
  45.1 35.0 %all-to-all-start.1 = ((bf16[16,1,320,256]{3,2,1,0:T(8,128)(2,1)}), bf16[16,1,320,256]{3,2,1,0:T(8,128)(2,1)S(1)}, u32[]{:S(2)}, u32[]{:S(2)}) async-start(bf16[16,1,320,256]{3,2,1,0:T(8,128)(2,1)} %broadcast_in_dim.29), calls=%async_computation.1 | async-start | bytes 5242880 | tf_op jit(solution)/shard_map/all_to_all | solution.py:56
  148.5 21.7 %all-to-all-start.5 = ((bf16[16,1,160,256]{3,2,1,0:T(8,128)(2,1)}), bf16[16,1,160,256]{3,2,1,0:T(8,128)(2,1)}, u32[]{:S(2)}, u32[]{:S(2)}) async-start(bf16[16,1,160,256]{3,2,1,0:T(8,128)(2,1)} %broadcast_in_dim.31), calls=%async_computation.5 | async-start | bytes 2621440 | tf_op jit(solution)/shard_map/all_to_all | solution.py:56
  174.0 4.9 collective-permute-start
  179.0 5.5 collective-permute-start.1
  184.5 6.1 collective-permute-start.2
  196.5 15.0 %all-to-all-start.6 = ((bf16[16,1,80,256]{3,2,1,0:T(8,128)(2,1)}), bf16[16,1,80,256]{3,2,1,0:T(8,128)(2,1)S(1)}, u32[]{:S(2)}, u32[]{:S(2)}) async-start(bf16[16,1,80,256]{3,2,1,0:T(8,128)(2,1)} %bitcast.310), calls=%async_computation.6 | async-start | bytes 1310720 | tf_op jit(solution)/shard_map/all_to_all | solution.py:54
  212.5 14.2 %all-to-all-start.7 = ((bf16[16,1,80,256]{3,2,1,0:T(8,128)(2,1)}), bf16[16,1,80,256]{3,2,1,0:T(8,128)(2,1)S(1)}, u32[]{:S(2)}, u32[]{:S(2)}) async-start(bf16[16,1,80,256]{3,2,1,0:T(8,128)(2,1)} %broadcast_in_dim.32), calls=%async_computation.7 | async-start | bytes 1310720 | tf_op jit(solution)/shard_map/all_to_all | solution.py:56
  233.0 5.2 collective-permute-start.4
  239.1 3.8 collective-permute-start.5
  242.9 4.9 collective-permute-start.6
  247.8 4.9 collective-permute-start.7
  254.8 12.9 %all-to-all-start.8 = ((bf16[16,1,40,256]{3,2,1,0:T(8,128)(2,1)}), bf16[16,1,40,256]{3,2,1,0:T(8,128)(2,1)}, u32[]{:S(2)}, u32[]{:S(2)}) async-start(bf16[16,1,40,256]{3,2,1,0:T(8,128)(2,1)} %bitcast.321), calls=%async_computation.8 | async-start | bytes 655360 | tf_op jit(solution)/shard_map/all_to_all | solution.py:54
  269.5 12.0 %all-to-all-start.9 = ((bf16[16,1,40,256]{3,2,1,0:T(8,128)(2,1)}), bf16[16,1,40,256]{3,2,1,0:T(8,128)(2,1)}, u32[]{:S(2)}, u32[]{:S(2)}) async-start(bf16[16,1,40,256]{3,2,1,0:T(8,128)(2,1)} %broadcast_in_dim.33), calls=%async_computation.9 | async-start | bytes 655360 | tf_op jit(solution)/shard_map/all_to_all | solution.py:56
  291.3 4.4 collective-permute-start.10
  295.8 3.6 collective-permute-start.11
  300.6 5.5 collective-permute-start.12
  306.2 6.1 collective-permute-start.13
  312.3 4.2 collective-permute-start.14
  316.6 5.8 collective-permute-start.15
  323.5 5.3 collective-permute-start.16
  331.8 4.4 collective-permute-start.18
  336.3 3.6 collective-permute-start.19
  366.5 3.9 collective-permute-start.20
  370.5 3.8 collective-permute-start.21
  374.2 4.9 collective-permute-start.22
  420.2 4.2 collective-permute-start.24
  424.5 5.5 collective-permute-start.25
  430.0 6.1 collective-permute-start.26
  436.1 4.0 collective-permute-start.27
  470.5 22.4 %all-to-all-start.15 = ((bf16[16,1,160,256]{3,2,1,0:T(8,128)(2,1)}), bf16[16,1,160,256]{3,2,1,0:T(8,128)(2,1)}, u32[]{:S(2)}, u32[]{:S(2)}) async-start(bf16[16,1,160,256]{3,2,1,0:T(8,128)(2,1)} %broadcast_in_dim.36), calls=%async_computation.15 | async-start | bytes 2621440 | tf_op jit(solution)/shard_map/all_to_all | solution.py:56
  496.3 18.0 %all-to-all-start.16 = ((bf16[8,1,160,256]{3,2,1,0:T(8,128)(2,1)}), bf16[8,1,160,256]{3,2,1,0:T(8,128)(2,1)S(1)}, u32[]{:S(2)}, u32[]{:S(2)}) async-start(bf16[8,1,160,256]{3,2,1,0:T(8,128)(2,1)} %fusion.70), calls=%async_computation.16 | async-start | bytes 1310720 | tf_op jit(solution)/shard_map/all_to_all | solution.py:54
  516.8 15.5 %all-to-all-start.17 = ((bf16[8,1,160,256]{3,2,1,0:T(8,128)(2,1)}), bf16[8,1,160,256]{3,2,1,0:T(8,128)(2,1)S(1)}, u32[]{:S(2)}, u32[]{:S(2)}) async-start(bf16[8,1,160,256]{3,2,1,0:T(8,128)(2,1)} %broadcast_in_dim.37), calls=%async_computation.17 | async-start | bytes 1310720 | tf_op jit(solution)/shard_map/all_to_all | solution.py:56
  (33 other events, 754.4 us)

commit v8 on v6

--- a/solution.py
+++ b/solution.py
@@ -111,7 +111,9 @@
                     preferred_element_type=jnp.float32,
                 )
                 onehot = level_onehot(climbed, source_level, distance)
-                term = jnp.einsum("ks,sjr->kjr", onehot, products, precision=lax.Precision.HIGHEST)
+                term = jnp.sum(
+                    jnp.where(onehot[:, :, None, None] > 0, products[None], 0.0), axis=1
+                )
                 partial_value = term if partial_value is None else partial_value + term
             reduced = reduced - group_allreduce(
                 partial_value.astype(jnp.bfloat16), COL, n_col

time: 669 us -> 664 us (level)
  matrix products: 94.7 us -> 75.6 us
  other arithmetic: 17.4 us -> 28.9 us
    all_to_all x7 -> x6, blocking collectives: 165 us -> 143 us  [a2a_allreduce(): got = lax.all_to_all(pieces, axis, 0, 0, tiled=False)]
    dot_general x10 -> x0, matrix products: 21.3 us -> none  [solve(): jnp.einsum('ks,sjr->kjr', onehot, products, precision=lax.Precision.HIGHEST)]
    all_to_all x4 -> x5, blocking collectives: 74.2 us -> 93.2 us  [a2a_allreduce(): lax.all_to_all(jnp.broadcast_to(owned[None], (n,) + owned.shape), axis, 0...]
    all_to_all x3 -> x4, waiting for transfers between devices: 16.3 us -> 32.4 us  [a2a_allreduce(): got = lax.all_to_all(pieces, axis, 0, 0, tiled=False)]
    all_to_all x6 -> x5, waiting for transfers between devices: 67.3 us -> 52.5 us  [a2a_allreduce(): lax.all_to_all(jnp.broadcast_to(owned[None], (n,) + owned.shape), axis, 0...]
    reduce_sum x0 -> x6, other arithmetic: none -> 9.61 us  [solve(): jnp.sum(jnp.where(onehot[:, :, None, None] > 0, products[None], 0.0), axi...]
    all_to_all x6 -> x5, starting transfers between devices: 26.1 us -> 21.4 us  [a2a_allreduce(): lax.all_to_all(jnp.broadcast_to(owned[None], (n,) + owned.shape), axis, 0...]
    all_to_all x3 -> x4, starting transfers between devices: 15.7 us -> 20.5 us  [a2a_allreduce(): got = lax.all_to_all(pieces, axis, 0, 0, tiled=False)]
  transfers between devices with their start and end apart: 31 -> 31, of which waited for: 31 -> 31; matrix products, arithmetic and copies ran while one was open for 7% -> 6% of each run, Pallas kernels for 0% -> 0%
where the time goes in v8:
time: 664 us; the launch traced here: 655 us
  blocking collectives  276 us (42%)
  waiting for transfers between devices  176 us (27%)
  starting transfers between devices  81.2 us (12%)
  matrix products  75.6 us (11%)
  other arithmetic  28.9 us (4%)
  local copies, waits for them, and re-layouts  15.7 us (2%)
    all_to_all x6, blocking collectives, a2a_allreduce(): got = lax.all_to_all(pieces, axis, 0, 0, tiled=False)  143 us
    all_to_all x5, blocking collectives, a2a_allreduce(): lax.all_to_all(jnp.broadcast_to(owned[None], (n,) + owned.shape), axis, 0...  93.2 us
    ppermute x22, waiting for transfers between devices, doubling_allreduce(): lax.ppermute(x, axis, xor_perm(n, bit)).astype(jnp.float32)  91.3 us
    all_to_all x5, waiting for transfers between devices, a2a_allreduce(): lax.all_to_all(jnp.broadcast_to(owned[None], (n,) + owned.shape), axis, 0...  52.5 us
    ppermute x22, starting transfers between devices, doubling_allreduce(): lax.ppermute(x, axis, xor_perm(n, bit)).astype(jnp.float32)  39.4 us
    all_to_all x4, waiting for transfers between devices, a2a_allreduce(): got = lax.all_to_all(pieces, axis, 0, 0, tiled=False)  32.4 us
    dot_general x10, matrix products, solve(): jnp.einsum('boj,boh->bjh', pair_slice(panel_local, tree_level, distance),...  26.5 us
    dot_general x10, matrix products, solve(): jnp.einsum('sjv,svk->sjk', pair_slice(panel_local, source_level, distance...  23 us
  transfers between devices with their start and end apart: 31, of which 31 were waited for; matrix products, arithmetic and copies ran while one was open for 6% of the time, Pallas kernels for 0%

profile of v8, /device:TPU:1, one launch (start us, length us, event | category | flops | bytes accessed | tf_op | source)
XLA Modules:
  0.0 654.5 jit_solution(16139444263776895238)
XLA Ops:
  3.3 39.6 %all_to_all.120 = bf16[16,1,320,256]{3,2,1,0:T(8,128)(2,1)S(1)} all-to-all(bf16[16,1,320,256]{3,2,1,0:T(8,128)(2,1)S(1)} %convert_bitcast_fusion), channel_id=1, replica_groups=mesh['x'=4,'y'=4,'z'=4,'core'=2] {'x','y'}, dimensions={0} | all-to-all | bytes 5242880 | tf_op jit(solution)/shard_map/all_to_all | solution.py:54
  50.8 29.3 %all-to-all-done.1 = bf16[16,1,320,256]{3,2,1,0:T(8,128)(2,1)S(1)} async-done(((bf16[16,1,320,256]{3,2,1,0:T(8,128)(2,1)}), bf16[16,1,320,256]{3,2,1,0:T(8,128)(2,1)S(1)}, u32[]{:S(2)}, u32[]{:S(2)}) %all-to-all-start.1) | async-done | bytes 2621472 | tf_op jit(solution)/shard_map/all_to_all | solution.py:56
  86.1 22.2 %all_to_all.121 = bf16[8,1,160,256]{3,2,1,0:T(8,128)(2,1)S(1)} all-to-all(bf16[8,1,160,256]{3,2,1,0:T(8,128)(2,1)S(1)} %bitcast.193), channel_id=1, replica_groups=mesh['x'=4,'y'=4,'z'=4,'core'=2] {'z','core'}, dimensions={0} | all-to-all | bytes 1310720 | tf_op jit(solution)/shard_map/all_to_all | solution.py:54
  108.5 14.2 %all_to_all.122 = bf16[8,1,160,256]{3,2,1,0:T(8,128)(2,1)S(1)} all-to-all(bf16[8,1,160,256]{3,2,1,0:T(8,128)(2,1)S(1)} %broadcast_in_dim.201), channel_id=1, replica_groups=mesh['x'=4,'y'=4,'z'=4,'core'=2] {'z','core'}, dimensions={0} | all-to-all | bytes 1310720 | tf_op jit(solution)/shard_map/all_to_all | solution.py:56
  131.8 16.8 %all-to-all-done.4 = bf16[16,1,160,256]{3,2,1,0:T(8,128)(2,1)} async-done(((bf16[16,1,160,256]{3,2,1,0:T(8,128)(2,1)}), bf16[16,1,160,256]{3,2,1,0:T(8,128)(2,1)}, u32[]{:S(2)}, u32[]{:S(2)}) %all-to-all-start.4) | async-done | bytes 1310752 | tf_op jit(solution)/shard_map/all_to_all | solution.py:54
  160.5 12.7 %all-to-all-done.5 = bf16[16,1,160,256]{3,2,1,0:T(8,128)(2,1)} async-done(((bf16[16,1,160,256]{3,2,1,0:T(8,128)(2,1)}), bf16[16,1,160,256]{3,2,1,0:T(8,128)(2,1)}, u32[]{:S(2)}, u32[]{:S(2)}) %all-to-all-start.5) | async-done | bytes 1310752 | tf_op jit(solution)/shard_map/all_to_all | solution.py:56
  182.7 8.0 %collective-permute-done.1 = bf16[4,160,256]{2,1,0:T(8,128)(2,1)} collective-permute-done((bf16[4,160,256]{2,1,0:T(8,128)(2,1)S(1)}, bf16[4,160,256]{2,1,0:T(8,128)(2,1)}, u32[]{:S(2)}, u32[]{:S(2)}) %collective-permute-start.1) | collective-permute-done | bytes 327712 | tf_op jit(solution)/shard_map/ppermute | solution.py:63
  193.3 8.0 %collective-permute-done.2 = bf16[4,160,256]{2,1,0:T(8,128)(2,1)S(1)} collective-permute-done((bf16[4,160,256]{2,1,0:T(8,128)(2,1)S(1)}, bf16[4,160,256]{2,1,0:T(8,128)(2,1)S(1)}, u32[]{:S(2)}, u32[]{:S(2)}) %collective-permute-start.2) | collective-permute-done | bytes 327712 | tf_op jit(solution)/shard_map/ppermute | solution.py:63
  211.4 6.2 all-to-all-done.6
  239.9 5.1 collective-permute-done.4
  259.8 5.2 all-to-all-done.8
  312.4 6.1 collective-permute-done.12
  319.7 6.5 collective-permute-start.13
  337.7 11.4 %all_to_all.123 = bf16[16,1,40,256]{3,2,1,0:T(8,128)(2,1)} all-to-all(bf16[16,1,40,256]{3,2,1,0:T(8,128)(2,1)S(1)} %bitcast.197), channel_id=1, replica_groups=mesh['x'=4,'y'=4,'z'=4,'core'=2] {'x','y'}, dimensions={0} | all-to-all | bytes 655360 | tf_op jit(solution)/shard_map/all_to_all | solution.py:54
  350.1 11.0 %all_to_all.124 = bf16[16,1,40,256]{3,2,1,0:T(8,128)(2,1)S(1)} all-to-all(bf16[16,1,40,256]{3,2,1,0:T(8,128)(2,1)S(1)} %broadcast_in_dim.327), channel_id=1, replica_groups=mesh['x'=4,'y'=4,'z'=4,'core'=2] {'x','y'}, dimensions={0} | all-to-all | bytes 655360 | tf_op jit(solution)/shard_map/all_to_all | solution.py:56
  369.0 5.1 collective-permute-done.17
  374.9 5.3 collective-permute-done.18
  385.1 13.4 %all_to_all.125 = bf16[16,1,80,256]{3,2,1,0:T(8,128)(2,1)} all-to-all(bf16[16,1,80,256]{3,2,1,0:T(8,128)(2,1)S(1)} %bitcast.194), channel_id=1, replica_groups=mesh['x'=4,'y'=4,'z'=4,'core'=2] {'x','y'}, dimensions={0} | all-to-all | bytes 1310720 | tf_op jit(solution)/shard_map/all_to_all | solution.py:54
  401.1 13.0 %all_to_all.126 = bf16[16,1,80,256]{3,2,1,0:T(8,128)(2,1)S(1)} all-to-all(bf16[16,1,80,256]{3,2,1,0:T(8,128)(2,1)S(1)} %broadcast_in_dim.328), channel_id=1, replica_groups=mesh['x'=4,'y'=4,'z'=4,'core'=2] {'x','y'}, dimensions={0} | all-to-all | bytes 1310720 | tf_op jit(solution)/shard_map/all_to_all | solution.py:56
  422.4 8.2 %collective-permute-done.20 = bf16[4,160,256]{2,1,0:T(8,128)(2,1)S(1)} collective-permute-done((bf16[4,160,256]{2,1,0:T(8,128)(2,1)S(1)}, bf16[4,160,256]{2,1,0:T(8,128)(2,1)S(1)}, u32[]{:S(2)}, u32[]{:S(2)}) %collective-permute-start.20) | collective-permute-done | bytes 327712 | tf_op jit(solution)/shard_map/ppermute | solution.py:63
  433.4 7.0 %collective-permute-done.21 = bf16[4,160,256]{2,1,0:T(8,128)(2,1)S(1)} collective-permute-done((bf16[4,160,256]{2,1,0:T(8,128)(2,1)S(1)}, bf16[4,160,256]{2,1,0:T(8,128)(2,1)S(1)}, u32[]{:S(2)}, u32[]{:S(2)}) %collective-permute-start.21) | collective-permute-done | bytes 327712 | tf_op jit(solution)/shard_map/ppermute | solution.py:63
  445.5 20.7 %all_to_all.127 = bf16[16,1,160,256]{3,2,1,0:T(8,128)(2,1)} all-to-all(bf16[16,1,160,256]{3,2,1,0:T(8,128)(2,1)S(1)} %bitcast.188), channel_id=1, replica_groups=mesh['x'=4,'y'=4,'z'=4,'core'=2] {'x','y'}, dimensions={0} | all-to-all | bytes 2621440 | tf_op jit(solution)/shard_map/all_to_all | solution.py:54
  467.9 19.4 %all_to_all.128 = bf16[16,1,160,256]{3,2,1,0:T(8,128)(2,1)S(1)} all-to-all(bf16[16,1,160,256]{3,2,1,0:T(8,128)(2,1)S(1)} %broadcast_in_dim.329), channel_id=1, replica_groups=mesh['x'=4,'y'=4,'z'=4,'core'=2] {'x','y'}, dimensions={0} | all-to-all | bytes 2621440 | tf_op jit(solution)/shard_map/all_to_all | solution.py:56
  490.3 8.3 %all-to-all-start.16 = ((bf16[8,1,160,256]{3,2,1,0:T(8,128)(2,1)}), bf16[8,1,160,256]{3,2,1,0:T(8,128)(2,1)S(1)}, u32[]{:S(2)}, u32[]{:S(2)}) async-start(bf16[8,1,160,256]{3,2,1,0:T(8,128)(2,1)} %fusion.53), calls=%async_computation.16 | async-start | bytes 1310720 | tf_op jit(solution)/shard_map/all_to_all | solution.py:54
  500.2 5.2 fusion.29
  517.9 5.2 fusion.32
  535.1 36.1 %all_to_all.129 = bf16[16,1,320,256]{3,2,1,0:T(8,128)(2,1)} all-to-all(bf16[16,1,320,256]{3,2,1,0:T(8,128)(2,1)S(1)} %fusion.1), channel_id=1, replica_groups=mesh['x'=4,'y'=4,'z'=4,'core'=2] {'x','y'}, dimensions={0} | all-to-all | bytes 5242880 | tf_op jit(solution)/shard_map/all_to_all | solution.py:54
  573.5 35.6 %all_to_all.130 = bf16[16,1,320,256]{3,2,1,0:T(8,128)(2,1)S(1)} all-to-all(bf16[16,1,320,256]{3,2,1,0:T(8,128)(2,1)S(1)} %broadcast_in_dim.331), channel_id=1, replica_groups=mesh['x'=4,'y'=4,'z'=4,'core'=2] {'x','y'}, dimensions={0} | all-to-all | bytes 5242880 | tf_op jit(solution)/shard_map/all_to_all | solution.py:56
  610.1 7.5 %all_to_all.131 = bf16[2,4,2,160,256]{4,3,2,1,0:T(8,128)(2,1)S(1)} all-to-all(bf16[2,4,2,160,256]{4,3,2,1,0:T(8,128)(2,1)S(1)} %bitcast.189), channel_id=1, replica_groups=mesh['x'=4,'y'=4,'z'=4,'core'=2] {'core'}, dimensions={0} | all-to-all | bytes 2621440 | tf_op jit(solution)/shard_map/all_to_all | solution.py:76
  618.1 13.0 %all_to_all.132 = bf16[4,1,2,160,256]{4,3,2,1,0:T(8,128)(2,1)S(1)} all-to-all(bf16[4,1,2,160,256]{4,3,2,1,0:T(8,128)(2,1)S(1)} %bitcast.191), channel_id=1, replica_groups=mesh['x'=4,'y'=4,'z'=4,'core'=2] {'z'}, dimensions={0} | all-to-all | bytes 1310720 | tf_op jit(solution)/shard_map/all_to_all | solution.py:76
  631.3 12.1 %all_to_all.133 = bf16[4,1,2,160,256]{4,3,2,1,0:T(8,128)(2,1)S(1)} all-to-all(bf16[4,1,2,160,256]{4,3,2,1,0:T(8,128)(2,1)S(1)} %broadcast_in_dim.332), channel_id=1, replica_groups=mesh['x'=4,'y'=4,'z'=4,'core'=2] {'z'}, dimensions={0} | all-to-all | bytes 1310720 | tf_op jit(solution)/shard_map/all_to_all | solution.py:79
  643.5 6.5 all_to_all.134
  (230 shorter events, 229.3 us)
Async XLA Ops:
  45.1 35.0 %all-to-all-start.1 = ((bf16[16,1,320,256]{3,2,1,0:T(8,128)(2,1)}), bf16[16,1,320,256]{3,2,1,0:T(8,128)(2,1)S(1)}, u32[]{:S(2)}, u32[]{:S(2)}) async-start(bf16[16,1,320,256]{3,2,1,0:T(8,128)(2,1)} %broadcast_in_dim.197), calls=%async_computation.1 | async-start | bytes 5242880 | tf_op jit(solution)/shard_map/all_to_all | solution.py:56
  50.2 106.0 %copy-start.19 = (s32[31]{0:T(128)}, s32[31]{0:T(128)S(1)}, u32[]{:S(2)}) copy-start(s32[31]{0:T(128)S(1)} %get-tuple-element.18) | copy-start | bytes 376
  126.0 22.6 %all-to-all-start.4 = ((bf16[16,1,160,256]{3,2,1,0:T(8,128)(2,1)}), bf16[16,1,160,256]{3,2,1,0:T(8,128)(2,1)}, u32[]{:S(2)}, u32[]{:S(2)}) async-start(bf16[16,1,160,256]{3,2,1,0:T(8,128)(2,1)} %bitcast.185), calls=%async_computation.4 | async-start | bytes 2621440 | tf_op jit(solution)/shard_map/all_to_all | solution.py:54
  151.3 21.8 %all-to-all-start.5 = ((bf16[16,1,160,256]{3,2,1,0:T(8,128)(2,1)}), bf16[16,1,160,256]{3,2,1,0:T(8,128)(2,1)}, u32[]{:S(2)}, u32[]{:S(2)}) async-start(bf16[16,1,160,256]{3,2,1,0:T(8,128)(2,1)} %broadcast_in_dim.202), calls=%async_computation.5 | async-start | bytes 2621440 | tf_op jit(solution)/shard_map/all_to_all | solution.py:56
  176.0 5.5 collective-permute-start
  181.6 9.1 %collective-permute-start.1 = (bf16[4,160,256]{2,1,0:T(8,128)(2,1)S(1)}, bf16[4,160,256]{2,1,0:T(8,128)(2,1)}, u32[]{:S(2)}, u32[]{:S(2)}) collective-permute-start(bf16[4,160,256]{2,1,0:T(8,128)(2,1)S(1)} %add_convert_fusion.7), channel_id=1, source_target_pairs={{0,2},{1,3},{2,0},{3,1},{4,6},{5,7},{6,4},{7,5},{8,10},{9,11},{10,... | collective-permute-start | bytes 983048 | tf_op jit(solution)/shard_map/ppermute | solution.py:63
  191.8 9.6 %collective-permute-start.2 = (bf16[4,160,256]{2,1,0:T(8,128)(2,1)S(1)}, bf16[4,160,256]{2,1,0:T(8,128)(2,1)S(1)}, u32[]{:S(2)}, u32[]{:S(2)}) collective-permute-start(bf16[4,160,256]{2,1,0:T(8,128)(2,1)S(1)} %add_convert_fusion.6), channel_id=1, source_target_pairs={{0,4},{1,5},{2,6},{3,7},{4,0},{5,1},{6,2},{7,3},{8,12},{9,13},{10,... | collective-permute-start | bytes 983048 | tf_op jit(solution)/shard_map/ppermute | solution.py:63
  203.9 13.7 %all-to-all-start.6 = ((bf16[16,1,80,256]{3,2,1,0:T(8,128)(2,1)}), bf16[16,1,80,256]{3,2,1,0:T(8,128)(2,1)S(1)}, u32[]{:S(2)}, u32[]{:S(2)}) async-start(bf16[16,1,80,256]{3,2,1,0:T(8,128)(2,1)} %bitcast.192), calls=%async_computation.6 | async-start | bytes 1310720 | tf_op jit(solution)/shard_map/all_to_all | solution.py:54
  218.6 13.4 %all-to-all-start.7 = ((bf16[16,1,80,256]{3,2,1,0:T(8,128)(2,1)}), bf16[16,1,80,256]{3,2,1,0:T(8,128)(2,1)S(1)}, u32[]{:S(2)}, u32[]{:S(2)}) async-start(bf16[16,1,80,256]{3,2,1,0:T(8,128)(2,1)} %broadcast_in_dim.209), calls=%async_computation.7 | async-start | bytes 1310720 | tf_op jit(solution)/shard_map/all_to_all | solution.py:56
  233.7 5.7 collective-permute-start.3
  239.5 5.5 collective-permute-start.4
  245.0 6.1 collective-permute-start.5
  253.2 11.9 %all-to-all-start.8 = ((bf16[16,1,40,256]{3,2,1,0:T(8,128)(2,1)}), bf16[16,1,40,256]{3,2,1,0:T(8,128)(2,1)}, u32[]{:S(2)}, u32[]{:S(2)}) async-start(bf16[16,1,40,256]{3,2,1,0:T(8,128)(2,1)} %bitcast.198), calls=%async_computation.8 | async-start | bytes 655360 | tf_op jit(solution)/shard_map/all_to_all | solution.py:54
  266.8 11.9 %all-to-all-start.9 = ((bf16[16,1,40,256]{3,2,1,0:T(8,128)(2,1)}), bf16[16,1,40,256]{3,2,1,0:T(8,128)(2,1)}, u32[]{:S(2)}, u32[]{:S(2)}) async-start(bf16[16,1,40,256]{3,2,1,0:T(8,128)(2,1)} %broadcast_in_dim.318), calls=%async_computation.9 | async-start | bytes 655360 | tf_op jit(solution)/shard_map/all_to_all | solution.py:56
  281.2 5.4 collective-permute-start.6
  286.6 3.8 collective-permute-start.7
  290.4 5.1 collective-permute-start.8
  296.7 4.2 collective-permute-start.9
  301.0 5.8 collective-permute-start.10
  306.8 4.5 collective-permute-start.11
  311.4 7.2 %collective-permute-start.12 = (bf16[1,320,256]{2,1,0:T(8,128)(2,1)S(1)}, bf16[1,320,256]{2,1,0:T(8,128)(2,1)S(1)}, u32[]{:S(2)}, u32[]{:S(2)}) collective-permute-start(bf16[1,320,256]{2,1,0:T(8,128)(2,1)S(1)} %add_convert_fusion.13), channel_id=1, source_target_pairs={{0,64},{8,72},{16,80},{24,88},{32,96},{40,104},{48,112},{56,120},{... | collective-permute-start | bytes 491528 | tf_op jit(solution)/shard_map/ppermute | solution.py:63
  319.7 7.4 %collective-permute-start.13 = (bf16[1,160,256]{2,1,0:T(8,128)(2,1)S(1)}, bf16[1,160,256]{2,1,0:T(8,128)(2,1)S(1)}, u32[]{:S(2)}, u32[]{:S(2)}) collective-permute-start(bf16[1,160,256]{2,1,0:T(8,128)(2,1)S(1)} %fusion.61), channel_id=1, source_target_pairs={{0,1},{1,0},{2,3},{3,2},{4,5},{5,4},{6,7},{7,6},{8,9},{9,8},{10,11... | collective-permute-start | bytes 245768 | tf_op jit(solution)/shard_map/ppermute | solution.py:63
  327.1 3.8 collective-permute-start.14
  330.9 4.9 collective-permute-start.15
  362.6 6.0 collective-permute-start.16
  368.6 5.5 collective-permute-start.17
  374.2 6.1 collective-permute-start.18
  415.5 6.0 collective-permute-start.19
  421.6 9.0 %collective-permute-start.20 = (bf16[4,160,256]{2,1,0:T(8,128)(2,1)S(1)}, bf16[4,160,256]{2,1,0:T(8,128)(2,1)S(1)}, u32[]{:S(2)}, u32[]{:S(2)}) collective-permute-start(bf16[4,160,256]{2,1,0:T(8,128)(2,1)S(1)} %add_convert_fusion.4), channel_id=1, source_target_pairs={{0,2},{1,3},{2,0},{3,1},{4,6},{5,7},{6,4},{7,5},{8,10},{9,11},{10,... | collective-permute-start | bytes 983048 | tf_op jit(solution)/shard_map/ppermute | solution.py:63
  430.7 9.6 %collective-permute-start.21 = (bf16[4,160,256]{2,1,0:T(8,128)(2,1)S(1)}, bf16[4,160,256]{2,1,0:T(8,128)(2,1)S(1)}, u32[]{:S(2)}, u32[]{:S(2)}) collective-permute-start(bf16[4,160,256]{2,1,0:T(8,128)(2,1)S(1)} %add_convert_fusion.3), channel_id=1, source_target_pairs={{0,4},{1,5},{2,6},{3,7},{4,0},{5,1},{6,2},{7,3},{8,12},{9,13},{10,... | collective-permute-start | bytes 983048 | tf_op jit(solution)/shard_map/ppermute | solution.py:63
  490.3 19.2 %all-to-all-start.16 = ((bf16[8,1,160,256]{3,2,1,0:T(8,128)(2,1)}), bf16[8,1,160,256]{3,2,1,0:T(8,128)(2,1)S(1)}, u32[]{:S(2)}, u32[]{:S(2)}) async-start(bf16[8,1,160,256]{3,2,1,0:T(8,128)(2,1)} %fusion.53), calls=%async_computation.16 | async-start | bytes 1310720 | tf_op jit(solution)/shard_map/all_to_all | solution.py:54
  511.9 15.2 %all-to-all-start.17 = ((bf16[8,1,160,256]{3,2,1,0:T(8,128)(2,1)}), bf16[8,1,160,256]{3,2,1,0:T(8,128)(2,1)S(1)}, u32[]{:S(2)}, u32[]{:S(2)}) async-start(bf16[8,1,160,256]{3,2,1,0:T(8,128)(2,1)} %broadcast_in_dim.330), calls=%async_computation.17 | async-start | bytes 1310720 | tf_op jit(solution)/shard_map/all_to_all | solution.py:56
  (30 other events, 352.5 us)

commit v9 on v8

--- a/solution.py
+++ b/solution.py
@@ -139,11 +139,13 @@
             partial_value = None
             for distance in range(1, 5 - tree_level):
                 onehot = level_onehot(climbed, tree_level, distance)
-                upper_node = jnp.einsum(
-                    "ks,kjr->sjr",
-                    onehot,
-                    solution_half[tree_level + distance].astype(jnp.float32),
-                    precision=lax.Precision.HIGHEST,
+                upper_node = jnp.sum(
+                    jnp.where(
+                        onehot[:, :, None, None] > 0,
+                        solution_half[tree_level + distance].astype(jnp.float32)[:, None],
+                        0.0,
+                    ),
+                    axis=0,
                 ).astype(jnp.bfloat16)
                 term = jnp.einsum(
                     "boj,boh->bjh",

time: 664 us -> 673 us (1.014)
  other arithmetic: 28.9 us -> 36.9 us
  matrix products: 75.6 us -> 68.6 us
where the time goes in v9:
time: 673 us; the launch traced here: 661 us
  blocking collectives  276 us (41%)
  waiting for transfers between devices  179 us (27%)
  starting transfers between devices  82.6 us (12%)
  matrix products  68.6 us (10%)
  other arithmetic  36.9 us (5%)
  local copies, waits for them, and re-layouts  16.9 us (3%)
    all_to_all x6, blocking collectives, a2a_allreduce(): got = lax.all_to_all(pieces, axis, 0, 0, tiled=False)  143 us
    all_to_all x5, blocking collectives, a2a_allreduce(): lax.all_to_all(jnp.broadcast_to(owned[None], (n,) + owned.shape), axis, 0...  93.2 us
    ppermute x22, waiting for transfers between devices, doubling_allreduce(): lax.ppermute(x, axis, xor_perm(n, bit)).astype(jnp.float32)  92.4 us
    all_to_all x5, waiting for transfers between devices, a2a_allreduce(): lax.all_to_all(jnp.broadcast_to(owned[None], (n,) + owned.shape), axis, 0...  54.1 us
    ppermute x22, starting transfers between devices, doubling_allreduce(): lax.ppermute(x, axis, xor_perm(n, bit)).astype(jnp.float32)  39.3 us
    all_to_all x4, waiting for transfers between devices, a2a_allreduce(): got = lax.all_to_all(pieces, axis, 0, 0, tiled=False)  33 us
    dot_general x10, matrix products, solve(): jnp.einsum('boj,boh->bjh', pair_slice(panel_local, tree_level, distance),...  25.4 us
    dot_general x10, matrix products, solve(): jnp.einsum('sjv,svk->sjk', pair_slice(panel_local, source_level, distance...  22.9 us
  transfers between devices with their start and end apart: 31, of which 31 were waited for; matrix products, arithmetic and copies ran while one was open for 6% of the time, Pallas kernels for 0%

profile of v9, /device:TPU:1, one launch (start us, length us, event | category | flops | bytes accessed | tf_op | source)
XLA Modules:
  0.0 661.5 jit_solution(7700251673336511358)
XLA Ops:
  3.3 39.6 %all_to_all.120 = bf16[16,1,320,256]{3,2,1,0:T(8,128)(2,1)S(1)} all-to-all(bf16[16,1,320,256]{3,2,1,0:T(8,128)(2,1)S(1)} %convert_bitcast_fusion), channel_id=1, replica_groups=mesh['x'=4,'y'=4,'z'=4,'core'=2] {'x','y'}, dimensions={0} | all-to-all | bytes 5242880 | tf_op jit(solution)/shard_map/all_to_all | solution.py:54
  50.3 29.8 %all-to-all-done.1 = bf16[16,1,320,256]{3,2,1,0:T(8,128)(2,1)S(1)} async-done(((bf16[16,1,320,256]{3,2,1,0:T(8,128)(2,1)}), bf16[16,1,320,256]{3,2,1,0:T(8,128)(2,1)S(1)}, u32[]{:S(2)}, u32[]{:S(2)}) %all-to-all-start.1) | async-done | bytes 2621472 | tf_op jit(solution)/shard_map/all_to_all | solution.py:56
  86.1 22.2 %all_to_all.121 = bf16[8,1,160,256]{3,2,1,0:T(8,128)(2,1)S(1)} all-to-all(bf16[8,1,160,256]{3,2,1,0:T(8,128)(2,1)S(1)} %bitcast.182), channel_id=1, replica_groups=mesh['x'=4,'y'=4,'z'=4,'core'=2] {'z','core'}, dimensions={0} | all-to-all | bytes 1310720 | tf_op jit(solution)/shard_map/all_to_all | solution.py:54
  108.5 14.2 %all_to_all.122 = bf16[8,1,160,256]{3,2,1,0:T(8,128)(2,1)S(1)} all-to-all(bf16[8,1,160,256]{3,2,1,0:T(8,128)(2,1)S(1)} %broadcast_in_dim.503), channel_id=1, replica_groups=mesh['x'=4,'y'=4,'z'=4,'core'=2] {'z','core'}, dimensions={0} | all-to-all | bytes 1310720 | tf_op jit(solution)/shard_map/all_to_all | solution.py:56
  131.3 17.4 %all-to-all-done.4 = bf16[16,1,160,256]{3,2,1,0:T(8,128)(2,1)} async-done(((bf16[16,1,160,256]{3,2,1,0:T(8,128)(2,1)}), bf16[16,1,160,256]{3,2,1,0:T(8,128)(2,1)}, u32[]{:S(2)}, u32[]{:S(2)}) %all-to-all-start.4) | async-done | bytes 1310752 | tf_op jit(solution)/shard_map/all_to_all | solution.py:54
  160.0 13.0 %all-to-all-done.5 = bf16[16,1,160,256]{3,2,1,0:T(8,128)(2,1)} async-done(((bf16[16,1,160,256]{3,2,1,0:T(8,128)(2,1)}), bf16[16,1,160,256]{3,2,1,0:T(8,128)(2,1)}, u32[]{:S(2)}, u32[]{:S(2)}) %all-to-all-start.5) | async-done | bytes 1310752 | tf_op jit(solution)/shard_map/all_to_all | solution.py:56
  183.9 8.5 %collective-permute-done.1 = bf16[4,160,256]{2,1,0:T(8,128)(2,1)S(1)} collective-permute-done((bf16[4,160,256]{2,1,0:T(8,128)(2,1)S(1)}, bf16[4,160,256]{2,1,0:T(8,128)(2,1)S(1)}, u32[]{:S(2)}, u32[]{:S(2)}) %collective-permute-start.1) | collective-permute-done | bytes 327712 | tf_op jit(solution)/shard_map/ppermute | solution.py:63
  194.0 8.0 %collective-permute-done.2 = bf16[4,160,256]{2,1,0:T(8,128)(2,1)S(1)} collective-permute-done((bf16[4,160,256]{2,1,0:T(8,128)(2,1)S(1)}, bf16[4,160,256]{2,1,0:T(8,128)(2,1)S(1)}, u32[]{:S(2)}, u32[]{:S(2)}) %collective-permute-start.2) | collective-permute-done | bytes 327712 | tf_op jit(solution)/shard_map/ppermute | solution.py:63
  212.2 6.0 all-to-all-done.6
  240.7 5.1 collective-permute-done.4
  246.6 5.2 collective-permute-done.5
  260.6 5.2 all-to-all-done.8
  313.0 6.1 collective-permute-done.12
  320.2 6.5 collective-permute-start.13
  337.7 11.4 %all_to_all.123 = bf16[16,1,40,256]{3,2,1,0:T(8,128)(2,1)} all-to-all(bf16[16,1,40,256]{3,2,1,0:T(8,128)(2,1)S(1)} %bitcast.186), channel_id=1, replica_groups=mesh['x'=4,'y'=4,'z'=4,'core'=2] {'x','y'}, dimensions={0} | all-to-all | bytes 655360 | tf_op jit(solution)/shard_map/all_to_all | solution.py:54
  350.1 11.0 %all_to_all.124 = bf16[16,1,40,256]{3,2,1,0:T(8,128)(2,1)S(1)} all-to-all(bf16[16,1,40,256]{3,2,1,0:T(8,128)(2,1)S(1)} %broadcast_in_dim.534), channel_id=1, replica_groups=mesh['x'=4,'y'=4,'z'=4,'core'=2] {'x','y'}, dimensions={0} | all-to-all | bytes 655360 | tf_op jit(solution)/shard_map/all_to_all | solution.py:56
  368.9 5.1 collective-permute-done.17
  375.0 5.2 collective-permute-done.18
  384.8 13.4 %all_to_all.125 = bf16[16,1,80,256]{3,2,1,0:T(8,128)(2,1)} all-to-all(bf16[16,1,80,256]{3,2,1,0:T(8,128)(2,1)S(1)} %bitcast.181), channel_id=1, replica_groups=mesh['x'=4,'y'=4,'z'=4,'core'=2] {'x','y'}, dimensions={0} | all-to-all | bytes 1310720 | tf_op jit(solution)/shard_map/all_to_all | solution.py:54
  400.8 13.0 %all_to_all.126 = bf16[16,1,80,256]{3,2,1,0:T(8,128)(2,1)S(1)} all-to-all(bf16[16,1,80,256]{3,2,1,0:T(8,128)(2,1)S(1)} %broadcast_in_dim.539), channel_id=1, replica_groups=mesh['x'=4,'y'=4,'z'=4,'core'=2] {'x','y'}, dimensions={0} | all-to-all | bytes 1310720 | tf_op jit(solution)/shard_map/all_to_all | solution.py:56
  422.0 8.3 %collective-permute-done.20 = bf16[4,160,256]{2,1,0:T(8,128)(2,1)S(1)} collective-permute-done((bf16[4,160,256]{2,1,0:T(8,128)(2,1)S(1)}, bf16[4,160,256]{2,1,0:T(8,128)(2,1)S(1)}, u32[]{:S(2)}, u32[]{:S(2)}) %collective-permute-start.20) | collective-permute-done | bytes 327712 | tf_op jit(solution)/shard_map/ppermute | solution.py:63
  433.1 6.9 %collective-permute-done.21 = bf16[4,160,256]{2,1,0:T(8,128)(2,1)S(1)} collective-permute-done((bf16[4,160,256]{2,1,0:T(8,128)(2,1)S(1)}, bf16[4,160,256]{2,1,0:T(8,128)(2,1)S(1)}, u32[]{:S(2)}, u32[]{:S(2)}) %collective-permute-start.21) | collective-permute-done | bytes 327712 | tf_op jit(solution)/shard_map/ppermute | solution.py:63
  445.2 20.7 %all_to_all.127 = bf16[16,1,160,256]{3,2,1,0:T(8,128)(2,1)} all-to-all(bf16[16,1,160,256]{3,2,1,0:T(8,128)(2,1)S(1)} %bitcast.176), channel_id=1, replica_groups=mesh['x'=4,'y'=4,'z'=4,'core'=2] {'x','y'}, dimensions={0} | all-to-all | bytes 2621440 | tf_op jit(solution)/shard_map/all_to_all | solution.py:54
  469.1 19.4 %all_to_all.128 = bf16[16,1,160,256]{3,2,1,0:T(8,128)(2,1)S(1)} all-to-all(bf16[16,1,160,256]{3,2,1,0:T(8,128)(2,1)S(1)} %broadcast_in_dim.545), channel_id=1, replica_groups=mesh['x'=4,'y'=4,'z'=4,'core'=2] {'x','y'}, dimensions={0} | all-to-all | bytes 2621440 | tf_op jit(solution)/shard_map/all_to_all | solution.py:56
  491.5 8.6 %all-to-all-start.16 = ((bf16[8,1,160,256]{3,2,1,0:T(8,128)(2,1)}), bf16[8,1,160,256]{3,2,1,0:T(8,128)(2,1)}, u32[]{:S(2)}, u32[]{:S(2)}) async-start(bf16[8,1,160,256]{3,2,1,0:T(8,128)(2,1)} %fusion.54), calls=%async_computation.16 | async-start | bytes 1310720 | tf_op jit(solution)/shard_map/all_to_all | solution.py:54
  514.8 5.3 all-to-all-start.17
  541.4 36.1 %all_to_all.129 = bf16[16,1,320,256]{3,2,1,0:T(8,128)(2,1)} all-to-all(bf16[16,1,320,256]{3,2,1,0:T(8,128)(2,1)S(1)} %fusion.1), channel_id=1, replica_groups=mesh['x'=4,'y'=4,'z'=4,'core'=2] {'x','y'}, dimensions={0} | all-to-all | bytes 5242880 | tf_op jit(solution)/shard_map/all_to_all | solution.py:54
  579.8 35.5 %all_to_all.130 = bf16[16,1,320,256]{3,2,1,0:T(8,128)(2,1)S(1)} all-to-all(bf16[16,1,320,256]{3,2,1,0:T(8,128)(2,1)S(1)} %broadcast_in_dim.555), channel_id=1, replica_groups=mesh['x'=4,'y'=4,'z'=4,'core'=2] {'x','y'}, dimensions={0} | all-to-all | bytes 5242880 | tf_op jit(solution)/shard_map/all_to_all | solution.py:56
  616.3 7.5 %all_to_all.131 = bf16[2,4,2,160,256]{4,3,2,1,0:T(8,128)(2,1)S(1)} all-to-all(bf16[2,4,2,160,256]{4,3,2,1,0:T(8,128)(2,1)S(1)} %bitcast.177), channel_id=1, replica_groups=mesh['x'=4,'y'=4,'z'=4,'core'=2] {'core'}, dimensions={0} | all-to-all | bytes 2621440 | tf_op jit(solution)/shard_map/all_to_all | solution.py:76
  624.3 13.0 %all_to_all.132 = bf16[4,1,2,160,256]{4,3,2,1,0:T(8,128)(2,1)S(1)} all-to-all(bf16[4,1,2,160,256]{4,3,2,1,0:T(8,128)(2,1)S(1)} %bitcast.179), channel_id=1, replica_groups=mesh['x'=4,'y'=4,'z'=4,'core'=2] {'z'}, dimensions={0} | all-to-all | bytes 1310720 | tf_op jit(solution)/shard_map/all_to_all | solution.py:76
  637.5 12.1 %all_to_all.133 = bf16[4,1,2,160,256]{4,3,2,1,0:T(8,128)(2,1)S(1)} all-to-all(bf16[4,1,2,160,256]{4,3,2,1,0:T(8,128)(2,1)S(1)} %broadcast_in_dim.556), channel_id=1, replica_groups=mesh['x'=4,'y'=4,'z'=4,'core'=2] {'z'}, dimensions={0} | all-to-all | bytes 1310720 | tf_op jit(solution)/shard_map/all_to_all | solution.py:79
  649.8 6.5 all_to_all.134
  (238 shorter events, 234.1 us)
Async XLA Ops:
  45.1 35.0 %all-to-all-start.1 = ((bf16[16,1,320,256]{3,2,1,0:T(8,128)(2,1)}), bf16[16,1,320,256]{3,2,1,0:T(8,128)(2,1)S(1)}, u32[]{:S(2)}, u32[]{:S(2)}) async-start(bf16[16,1,320,256]{3,2,1,0:T(8,128)(2,1)} %broadcast_in_dim.499), calls=%async_computation.1 | async-start | bytes 5242880 | tf_op jit(solution)/shard_map/all_to_all | solution.py:56
  126.0 22.6 %all-to-all-start.4 = ((bf16[16,1,160,256]{3,2,1,0:T(8,128)(2,1)}), bf16[16,1,160,256]{3,2,1,0:T(8,128)(2,1)}, u32[]{:S(2)}, u32[]{:S(2)}) async-start(bf16[16,1,160,256]{3,2,1,0:T(8,128)(2,1)} %bitcast.173), calls=%async_computation.4 | async-start | bytes 2621440 | tf_op jit(solution)/shard_map/all_to_all | solution.py:54
  151.3 21.7 %all-to-all-start.5 = ((bf16[16,1,160,256]{3,2,1,0:T(8,128)(2,1)}), bf16[16,1,160,256]{3,2,1,0:T(8,128)(2,1)}, u32[]{:S(2)}, u32[]{:S(2)}) async-start(bf16[16,1,160,256]{3,2,1,0:T(8,128)(2,1)} %broadcast_in_dim.504), calls=%async_computation.5 | async-start | bytes 2621440 | tf_op jit(solution)/shard_map/all_to_all | solution.py:56
  156.3 78.0 %copy-start.19 = (pred[2,4]{1,0:T(4,128)(4,1)}, pred[2,4]{1,0:T(4,128)(4,1)S(1)}, u32[]{:S(2)}) copy-start(pred[2,4]{1,0:T(4,128)(4,1)S(1)} %fusion.113) | copy-start | bytes 28
  176.5 5.8 collective-permute-start
  183.4 9.0 %collective-permute-start.1 = (bf16[4,160,256]{2,1,0:T(8,128)(2,1)S(1)}, bf16[4,160,256]{2,1,0:T(8,128)(2,1)S(1)}, u32[]{:S(2)}, u32[]{:S(2)}) collective-permute-start(bf16[4,160,256]{2,1,0:T(8,128)(2,1)S(1)} %add_convert_fusion.7), channel_id=1, source_target_pairs={{0,2},{1,3},{2,0},{3,1},{4,6},{5,7},{6,4},{7,5},{8,10},{9,11},{10,... | collective-permute-start | bytes 983048 | tf_op jit(solution)/shard_map/ppermute | solution.py:63
  192.5 9.6 %collective-permute-start.2 = (bf16[4,160,256]{2,1,0:T(8,128)(2,1)S(1)}, bf16[4,160,256]{2,1,0:T(8,128)(2,1)S(1)}, u32[]{:S(2)}, u32[]{:S(2)}) collective-permute-start(bf16[4,160,256]{2,1,0:T(8,128)(2,1)S(1)} %add_convert_fusion.6), channel_id=1, source_target_pairs={{0,4},{1,5},{2,6},{3,7},{4,0},{5,1},{6,2},{7,3},{8,12},{9,13},{10,... | collective-permute-start | bytes 983048 | tf_op jit(solution)/shard_map/ppermute | solution.py:63
  204.6 13.5 %all-to-all-start.6 = ((bf16[16,1,80,256]{3,2,1,0:T(8,128)(2,1)}), bf16[16,1,80,256]{3,2,1,0:T(8,128)(2,1)S(1)}, u32[]{:S(2)}, u32[]{:S(2)}) async-start(bf16[16,1,80,256]{3,2,1,0:T(8,128)(2,1)} %bitcast.180), calls=%async_computation.6 | async-start | bytes 1310720 | tf_op jit(solution)/shard_map/all_to_all | solution.py:54
  219.1 13.8 %all-to-all-start.7 = ((bf16[16,1,80,256]{3,2,1,0:T(8,128)(2,1)}), bf16[16,1,80,256]{3,2,1,0:T(8,128)(2,1)S(1)}, u32[]{:S(2)}, u32[]{:S(2)}) async-start(bf16[16,1,80,256]{3,2,1,0:T(8,128)(2,1)} %broadcast_in_dim.511), calls=%async_computation.7 | async-start | bytes 1310720 | tf_op jit(solution)/shard_map/all_to_all | solution.py:56
  234.6 5.6 collective-permute-start.3
  240.2 5.5 collective-permute-start.4
  245.8 6.1 collective-permute-start.5
  253.9 11.9 %all-to-all-start.8 = ((bf16[16,1,40,256]{3,2,1,0:T(8,128)(2,1)}), bf16[16,1,40,256]{3,2,1,0:T(8,128)(2,1)}, u32[]{:S(2)}, u32[]{:S(2)}) async-start(bf16[16,1,40,256]{3,2,1,0:T(8,128)(2,1)} %bitcast.185), calls=%async_computation.8 | async-start | bytes 655360 | tf_op jit(solution)/shard_map/all_to_all | solution.py:54
  267.6 11.9 %all-to-all-start.9 = ((bf16[16,1,40,256]{3,2,1,0:T(8,128)(2,1)}), bf16[16,1,40,256]{3,2,1,0:T(8,128)(2,1)}, u32[]{:S(2)}, u32[]{:S(2)}) async-start(bf16[16,1,40,256]{3,2,1,0:T(8,128)(2,1)} %broadcast_in_dim.521), calls=%async_computation.9 | async-start | bytes 655360 | tf_op jit(solution)/shard_map/all_to_all | solution.py:56
  281.9 5.4 collective-permute-start.6
  287.3 3.8 collective-permute-start.7
  291.1 4.9 collective-permute-start.8
  297.2 4.2 collective-permute-start.9
  301.5 5.8 collective-permute-start.10
  307.3 4.5 collective-permute-start.11
  311.9 7.2 %collective-permute-start.12 = (bf16[1,320,256]{2,1,0:T(8,128)(2,1)S(1)}, bf16[1,320,256]{2,1,0:T(8,128)(2,1)S(1)}, u32[]{:S(2)}, u32[]{:S(2)}) collective-permute-start(bf16[1,320,256]{2,1,0:T(8,128)(2,1)S(1)} %add_convert_fusion.13), channel_id=1, source_target_pairs={{0,64},{8,72},{16,80},{24,88},{32,96},{40,104},{48,112},{56,120},{... | collective-permute-start | bytes 491528 | tf_op jit(solution)/shard_map/ppermute | solution.py:63
  320.2 7.4 %collective-permute-start.13 = (bf16[1,160,256]{2,1,0:T(8,128)(2,1)S(1)}, bf16[1,160,256]{2,1,0:T(8,128)(2,1)S(1)}, u32[]{:S(2)}, u32[]{:S(2)}) collective-permute-start(bf16[1,160,256]{2,1,0:T(8,128)(2,1)S(1)} %fusion.62), channel_id=1, source_target_pairs={{0,1},{1,0},{2,3},{3,2},{4,5},{5,4},{6,7},{7,6},{8,9},{9,8},{10,11... | collective-permute-start | bytes 245768 | tf_op jit(solution)/shard_map/ppermute | solution.py:63
  327.7 3.8 collective-permute-start.14
  331.4 4.9 collective-permute-start.15
  362.5 6.0 collective-permute-start.16
  368.6 5.5 collective-permute-start.17
  374.1 6.1 collective-permute-start.18
  415.2 6.0 collective-permute-start.19
  421.3 9.0 %collective-permute-start.20 = (bf16[4,160,256]{2,1,0:T(8,128)(2,1)S(1)}, bf16[4,160,256]{2,1,0:T(8,128)(2,1)S(1)}, u32[]{:S(2)}, u32[]{:S(2)}) collective-permute-start(bf16[4,160,256]{2,1,0:T(8,128)(2,1)S(1)} %add_convert_fusion.4), channel_id=1, source_target_pairs={{0,2},{1,3},{2,0},{3,1},{4,6},{5,7},{6,4},{7,5},{8,10},{9,11},{10,... | collective-permute-start | bytes 983048 | tf_op jit(solution)/shard_map/ppermute | solution.py:63
  430.4 9.6 %collective-permute-start.21 = (bf16[4,160,256]{2,1,0:T(8,128)(2,1)S(1)}, bf16[4,160,256]{2,1,0:T(8,128)(2,1)S(1)}, u32[]{:S(2)}, u32[]{:S(2)}) collective-permute-start(bf16[4,160,256]{2,1,0:T(8,128)(2,1)S(1)} %add_convert_fusion.3), channel_id=1, source_target_pairs={{0,4},{1,5},{2,6},{3,7},{4,0},{5,1},{6,2},{7,3},{8,12},{9,13},{10,... | collective-permute-start | bytes 983048 | tf_op jit(solution)/shard_map/ppermute | solution.py:63
  491.5 19.7 %all-to-all-start.16 = ((bf16[8,1,160,256]{3,2,1,0:T(8,128)(2,1)}), bf16[8,1,160,256]{3,2,1,0:T(8,128)(2,1)}, u32[]{:S(2)}, u32[]{:S(2)}) async-start(bf16[8,1,160,256]{3,2,1,0:T(8,128)(2,1)} %fusion.54), calls=%async_computation.16 | async-start | bytes 1310720 | tf_op jit(solution)/shard_map/all_to_all | solution.py:54
  514.8 16.2 %all-to-all-start.17 = ((bf16[8,1,160,256]{3,2,1,0:T(8,128)(2,1)}), bf16[8,1,160,256]{3,2,1,0:T(8,128)(2,1)}, u32[]{:S(2)}, u32[]{:S(2)}) async-start(bf16[8,1,160,256]{3,2,1,0:T(8,128)(2,1)} %broadcast_in_dim.546), calls=%async_computation.17 | async-start | bytes 1310720 | tf_op jit(solution)/shard_map/all_to_all | solution.py:56
  (34 other events, 497.2 us)

commit v10 on v8

--- a/solution.py
+++ b/solution.py
@@ -141,9 +141,9 @@
                 onehot = level_onehot(climbed, tree_level, distance)
                 upper_node = jnp.einsum(
                     "ks,kjr->sjr",
-                    onehot,
-                    solution_half[tree_level + distance].astype(jnp.float32),
-                    precision=lax.Precision.HIGHEST,
+                    onehot.astype(jnp.bfloat16),
+                    solution_half[tree_level + distance],
+                    preferred_element_type=jnp.float32,
                 ).astype(jnp.bfloat16)
                 term = jnp.einsum(
                     "boj,boh->bjh",

time: 664 us -> 664 us (level)
  no operation moved by 1% of the time
where the time goes in v10:
time: 664 us; the launch traced here: 654 us
  blocking collectives  276 us (42%)
  waiting for transfers between devices  176 us (27%)
  starting transfers between devices  81.2 us (12%)
  matrix products  75.6 us (11%)
  other arithmetic  28.9 us (4%)
  local copies, waits for them, and re-layouts  15.7 us (2%)
    all_to_all x6, blocking collectives, a2a_allreduce(): got = lax.all_to_all(pieces, axis, 0, 0, tiled=False)  143 us
    all_to_all x5, blocking collectives, a2a_allreduce(): lax.all_to_all(jnp.broadcast_to(owned[None], (n,) + owned.shape), axis, 0...  93.2 us
    ppermute x22, waiting for transfers between devices, doubling_allreduce(): lax.ppermute(x, axis, xor_perm(n, bit)).astype(jnp.float32)  91.3 us
    all_to_all x5, waiting for transfers between devices, a2a_allreduce(): lax.all_to_all(jnp.broadcast_to(owned[None], (n,) + owned.shape), axis, 0...  52.5 us
    ppermute x22, starting transfers between devices, doubling_allreduce(): lax.ppermute(x, axis, xor_perm(n, bit)).astype(jnp.float32)  39.4 us
    all_to_all x4, waiting for transfers between devices, a2a_allreduce(): got = lax.all_to_all(pieces, axis, 0, 0, tiled=False)  32.4 us
    dot_general x10, matrix products, solve(): jnp.einsum('boj,boh->bjh', pair_slice(panel_local, tree_level, distance),...  26.5 us
    dot_general x10, matrix products, solve(): jnp.einsum('sjv,svk->sjk', pair_slice(panel_local, source_level, distance...  23 us
  transfers between devices with their start and end apart: 31, of which 31 were waited for; matrix products, arithmetic and copies ran while one was open for 6% of the time, Pallas kernels for 0%

profile of v10, /device:TPU:1, one launch (start us, length us, event | category | flops | bytes accessed | tf_op | source)
XLA Modules:
  0.0 654.5 jit_solution(2540967313522973625)
XLA Ops:
  3.3 39.6 %all_to_all.120 = bf16[16,1,320,256]{3,2,1,0:T(8,128)(2,1)S(1)} all-to-all(bf16[16,1,320,256]{3,2,1,0:T(8,128)(2,1)S(1)} %convert_bitcast_fusion), channel_id=1, replica_groups=mesh['x'=4,'y'=4,'z'=4,'core'=2] {'x','y'}, dimensions={0} | all-to-all | bytes 5242880 | tf_op jit(solution)/shard_map/all_to_all | solution.py:54
  50.8 29.3 %all-to-all-done.1 = bf16[16,1,320,256]{3,2,1,0:T(8,128)(2,1)S(1)} async-done(((bf16[16,1,320,256]{3,2,1,0:T(8,128)(2,1)}), bf16[16,1,320,256]{3,2,1,0:T(8,128)(2,1)S(1)}, u32[]{:S(2)}, u32[]{:S(2)}) %all-to-all-start.1) | async-done | bytes 2621472 | tf_op jit(solution)/shard_map/all_to_all | solution.py:56
  86.1 22.2 %all_to_all.121 = bf16[8,1,160,256]{3,2,1,0:T(8,128)(2,1)S(1)} all-to-all(bf16[8,1,160,256]{3,2,1,0:T(8,128)(2,1)S(1)} %bitcast.193), channel_id=1, replica_groups=mesh['x'=4,'y'=4,'z'=4,'core'=2] {'z','core'}, dimensions={0} | all-to-all | bytes 1310720 | tf_op jit(solution)/shard_map/all_to_all | solution.py:54
  108.5 14.2 %all_to_all.122 = bf16[8,1,160,256]{3,2,1,0:T(8,128)(2,1)S(1)} all-to-all(bf16[8,1,160,256]{3,2,1,0:T(8,128)(2,1)S(1)} %broadcast_in_dim.201), channel_id=1, replica_groups=mesh['x'=4,'y'=4,'z'=4,'core'=2] {'z','core'}, dimensions={0} | all-to-all | bytes 1310720 | tf_op jit(solution)/shard_map/all_to_all | solution.py:56
  131.8 16.8 %all-to-all-done.4 = bf16[16,1,160,256]{3,2,1,0:T(8,128)(2,1)} async-done(((bf16[16,1,160,256]{3,2,1,0:T(8,128)(2,1)}), bf16[16,1,160,256]{3,2,1,0:T(8,128)(2,1)}, u32[]{:S(2)}, u32[]{:S(2)}) %all-to-all-start.4) | async-done | bytes 1310752 | tf_op jit(solution)/shard_map/all_to_all | solution.py:54
  160.5 12.7 %all-to-all-done.5 = bf16[16,1,160,256]{3,2,1,0:T(8,128)(2,1)} async-done(((bf16[16,1,160,256]{3,2,1,0:T(8,128)(2,1)}), bf16[16,1,160,256]{3,2,1,0:T(8,128)(2,1)}, u32[]{:S(2)}, u32[]{:S(2)}) %all-to-all-start.5) | async-done | bytes 1310752 | tf_op jit(solution)/shard_map/all_to_all | solution.py:56
  182.7 8.0 %collective-permute-done.1 = bf16[4,160,256]{2,1,0:T(8,128)(2,1)} collective-permute-done((bf16[4,160,256]{2,1,0:T(8,128)(2,1)S(1)}, bf16[4,160,256]{2,1,0:T(8,128)(2,1)}, u32[]{:S(2)}, u32[]{:S(2)}) %collective-permute-start.1) | collective-permute-done | bytes 327712 | tf_op jit(solution)/shard_map/ppermute | solution.py:63
  193.3 8.0 %collective-permute-done.2 = bf16[4,160,256]{2,1,0:T(8,128)(2,1)S(1)} collective-permute-done((bf16[4,160,256]{2,1,0:T(8,128)(2,1)S(1)}, bf16[4,160,256]{2,1,0:T(8,128)(2,1)S(1)}, u32[]{:S(2)}, u32[]{:S(2)}) %collective-permute-start.2) | collective-permute-done | bytes 327712 | tf_op jit(solution)/shard_map/ppermute | solution.py:63
  211.4 6.2 all-to-all-done.6
  239.9 5.1 collective-permute-done.4
  259.8 5.2 all-to-all-done.8
  312.4 6.1 collective-permute-done.12
  319.7 6.5 collective-permute-start.13
  337.7 11.4 %all_to_all.123 = bf16[16,1,40,256]{3,2,1,0:T(8,128)(2,1)} all-to-all(bf16[16,1,40,256]{3,2,1,0:T(8,128)(2,1)S(1)} %bitcast.197), channel_id=1, replica_groups=mesh['x'=4,'y'=4,'z'=4,'core'=2] {'x','y'}, dimensions={0} | all-to-all | bytes 655360 | tf_op jit(solution)/shard_map/all_to_all | solution.py:54
  350.1 11.0 %all_to_all.124 = bf16[16,1,40,256]{3,2,1,0:T(8,128)(2,1)S(1)} all-to-all(bf16[16,1,40,256]{3,2,1,0:T(8,128)(2,1)S(1)} %broadcast_in_dim.327), channel_id=1, replica_groups=mesh['x'=4,'y'=4,'z'=4,'core'=2] {'x','y'}, dimensions={0} | all-to-all | bytes 655360 | tf_op jit(solution)/shard_map/all_to_all | solution.py:56
  369.0 5.1 collective-permute-done.17
  374.9 5.3 collective-permute-done.18
  385.1 13.4 %all_to_all.125 = bf16[16,1,80,256]{3,2,1,0:T(8,128)(2,1)} all-to-all(bf16[16,1,80,256]{3,2,1,0:T(8,128)(2,1)S(1)} %bitcast.194), channel_id=1, replica_groups=mesh['x'=4,'y'=4,'z'=4,'core'=2] {'x','y'}, dimensions={0} | all-to-all | bytes 1310720 | tf_op jit(solution)/shard_map/all_to_all | solution.py:54
  401.1 13.0 %all_to_all.126 = bf16[16,1,80,256]{3,2,1,0:T(8,128)(2,1)S(1)} all-to-all(bf16[16,1,80,256]{3,2,1,0:T(8,128)(2,1)S(1)} %broadcast_in_dim.328), channel_id=1, replica_groups=mesh['x'=4,'y'=4,'z'=4,'core'=2] {'x','y'}, dimensions={0} | all-to-all | bytes 1310720 | tf_op jit(solution)/shard_map/all_to_all | solution.py:56
  422.4 8.2 %collective-permute-done.20 = bf16[4,160,256]{2,1,0:T(8,128)(2,1)S(1)} collective-permute-done((bf16[4,160,256]{2,1,0:T(8,128)(2,1)S(1)}, bf16[4,160,256]{2,1,0:T(8,128)(2,1)S(1)}, u32[]{:S(2)}, u32[]{:S(2)}) %collective-permute-start.20) | collective-permute-done | bytes 327712 | tf_op jit(solution)/shard_map/ppermute | solution.py:63
  433.4 7.0 %collective-permute-done.21 = bf16[4,160,256]{2,1,0:T(8,128)(2,1)S(1)} collective-permute-done((bf16[4,160,256]{2,1,0:T(8,128)(2,1)S(1)}, bf16[4,160,256]{2,1,0:T(8,128)(2,1)S(1)}, u32[]{:S(2)}, u32[]{:S(2)}) %collective-permute-start.21) | collective-permute-done | bytes 327712 | tf_op jit(solution)/shard_map/ppermute | solution.py:63
  445.5 20.7 %all_to_all.127 = bf16[16,1,160,256]{3,2,1,0:T(8,128)(2,1)} all-to-all(bf16[16,1,160,256]{3,2,1,0:T(8,128)(2,1)S(1)} %bitcast.188), channel_id=1, replica_groups=mesh['x'=4,'y'=4,'z'=4,'core'=2] {'x','y'}, dimensions={0} | all-to-all | bytes 2621440 | tf_op jit(solution)/shard_map/all_to_all | solution.py:54
  467.8 19.4 %all_to_all.128 = bf16[16,1,160,256]{3,2,1,0:T(8,128)(2,1)S(1)} all-to-all(bf16[16,1,160,256]{3,2,1,0:T(8,128)(2,1)S(1)} %broadcast_in_dim.329), channel_id=1, replica_groups=mesh['x'=4,'y'=4,'z'=4,'core'=2] {'x','y'}, dimensions={0} | all-to-all | bytes 2621440 | tf_op jit(solution)/shard_map/all_to_all | solution.py:56
  490.3 8.3 %all-to-all-start.16 = ((bf16[8,1,160,256]{3,2,1,0:T(8,128)(2,1)}), bf16[8,1,160,256]{3,2,1,0:T(8,128)(2,1)S(1)}, u32[]{:S(2)}, u32[]{:S(2)}) async-start(bf16[8,1,160,256]{3,2,1,0:T(8,128)(2,1)} %fusion.53), calls=%async_computation.16 | async-start | bytes 1310720 | tf_op jit(solution)/shard_map/all_to_all | solution.py:54
  500.1 5.2 fusion.29
  517.9 5.2 fusion.32
  535.0 36.1 %all_to_all.129 = bf16[16,1,320,256]{3,2,1,0:T(8,128)(2,1)} all-to-all(bf16[16,1,320,256]{3,2,1,0:T(8,128)(2,1)S(1)} %fusion.1), channel_id=1, replica_groups=mesh['x'=4,'y'=4,'z'=4,'core'=2] {'x','y'}, dimensions={0} | all-to-all | bytes 5242880 | tf_op jit(solution)/shard_map/all_to_all | solution.py:54
  573.5 35.6 %all_to_all.130 = bf16[16,1,320,256]{3,2,1,0:T(8,128)(2,1)S(1)} all-to-all(bf16[16,1,320,256]{3,2,1,0:T(8,128)(2,1)S(1)} %broadcast_in_dim.331), channel_id=1, replica_groups=mesh['x'=4,'y'=4,'z'=4,'core'=2] {'x','y'}, dimensions={0} | all-to-all | bytes 5242880 | tf_op jit(solution)/shard_map/all_to_all | solution.py:56
  610.0 7.5 %all_to_all.131 = bf16[2,4,2,160,256]{4,3,2,1,0:T(8,128)(2,1)S(1)} all-to-all(bf16[2,4,2,160,256]{4,3,2,1,0:T(8,128)(2,1)S(1)} %bitcast.189), channel_id=1, replica_groups=mesh['x'=4,'y'=4,'z'=4,'core'=2] {'core'}, dimensions={0} | all-to-all | bytes 2621440 | tf_op jit(solution)/shard_map/all_to_all | solution.py:76
  618.0 13.0 %all_to_all.132 = bf16[4,1,2,160,256]{4,3,2,1,0:T(8,128)(2,1)S(1)} all-to-all(bf16[4,1,2,160,256]{4,3,2,1,0:T(8,128)(2,1)S(1)} %bitcast.191), channel_id=1, replica_groups=mesh['x'=4,'y'=4,'z'=4,'core'=2] {'z'}, dimensions={0} | all-to-all | bytes 1310720 | tf_op jit(solution)/shard_map/all_to_all | solution.py:76
  631.2 12.1 %all_to_all.133 = bf16[4,1,2,160,256]{4,3,2,1,0:T(8,128)(2,1)S(1)} all-to-all(bf16[4,1,2,160,256]{4,3,2,1,0:T(8,128)(2,1)S(1)} %broadcast_in_dim.332), channel_id=1, replica_groups=mesh['x'=4,'y'=4,'z'=4,'core'=2] {'z'}, dimensions={0} | all-to-all | bytes 1310720 | tf_op jit(solution)/shard_map/all_to_all | solution.py:79
  643.5 6.5 all_to_all.134
  (230 shorter events, 229.3 us)
Async XLA Ops:
  45.1 35.0 %all-to-all-start.1 = ((bf16[16,1,320,256]{3,2,1,0:T(8,128)(2,1)}), bf16[16,1,320,256]{3,2,1,0:T(8,128)(2,1)S(1)}, u32[]{:S(2)}, u32[]{:S(2)}) async-start(bf16[16,1,320,256]{3,2,1,0:T(8,128)(2,1)} %broadcast_in_dim.197), calls=%async_computation.1 | async-start | bytes 5242880 | tf_op jit(solution)/shard_map/all_to_all | solution.py:56
  50.2 106.0 %copy-start.19 = (s32[31]{0:T(128)}, s32[31]{0:T(128)S(1)}, u32[]{:S(2)}) copy-start(s32[31]{0:T(128)S(1)} %get-tuple-element.18) | copy-start | bytes 376
  126.0 22.6 %all-to-all-start.4 = ((bf16[16,1,160,256]{3,2,1,0:T(8,128)(2,1)}), bf16[16,1,160,256]{3,2,1,0:T(8,128)(2,1)}, u32[]{:S(2)}, u32[]{:S(2)}) async-start(bf16[16,1,160,256]{3,2,1,0:T(8,128)(2,1)} %bitcast.185), calls=%async_computation.4 | async-start | bytes 2621440 | tf_op jit(solution)/shard_map/all_to_all | solution.py:54
  151.3 21.8 %all-to-all-start.5 = ((bf16[16,1,160,256]{3,2,1,0:T(8,128)(2,1)}), bf16[16,1,160,256]{3,2,1,0:T(8,128)(2,1)}, u32[]{:S(2)}, u32[]{:S(2)}) async-start(bf16[16,1,160,256]{3,2,1,0:T(8,128)(2,1)} %broadcast_in_dim.202), calls=%async_computation.5 | async-start | bytes 2621440 | tf_op jit(solution)/shard_map/all_to_all | solution.py:56
  176.0 5.5 collective-permute-start
  181.6 9.1 %collective-permute-start.1 = (bf16[4,160,256]{2,1,0:T(8,128)(2,1)S(1)}, bf16[4,160,256]{2,1,0:T(8,128)(2,1)}, u32[]{:S(2)}, u32[]{:S(2)}) collective-permute-start(bf16[4,160,256]{2,1,0:T(8,128)(2,1)S(1)} %add_convert_fusion.7), channel_id=1, source_target_pairs={{0,2},{1,3},{2,0},{3,1},{4,6},{5,7},{6,4},{7,5},{8,10},{9,11},{10,... | collective-permute-start | bytes 983048 | tf_op jit(solution)/shard_map/ppermute | solution.py:63
  191.8 9.6 %collective-permute-start.2 = (bf16[4,160,256]{2,1,0:T(8,128)(2,1)S(1)}, bf16[4,160,256]{2,1,0:T(8,128)(2,1)S(1)}, u32[]{:S(2)}, u32[]{:S(2)}) collective-permute-start(bf16[4,160,256]{2,1,0:T(8,128)(2,1)S(1)} %add_convert_fusion.6), channel_id=1, source_target_pairs={{0,4},{1,5},{2,6},{3,7},{4,0},{5,1},{6,2},{7,3},{8,12},{9,13},{10,... | collective-permute-start | bytes 983048 | tf_op jit(solution)/shard_map/ppermute | solution.py:63
  203.9 13.7 %all-to-all-start.6 = ((bf16[16,1,80,256]{3,2,1,0:T(8,128)(2,1)}), bf16[16,1,80,256]{3,2,1,0:T(8,128)(2,1)S(1)}, u32[]{:S(2)}, u32[]{:S(2)}) async-start(bf16[16,1,80,256]{3,2,1,0:T(8,128)(2,1)} %bitcast.192), calls=%async_computation.6 | async-start | bytes 1310720 | tf_op jit(solution)/shard_map/all_to_all | solution.py:54
  218.6 13.4 %all-to-all-start.7 = ((bf16[16,1,80,256]{3,2,1,0:T(8,128)(2,1)}), bf16[16,1,80,256]{3,2,1,0:T(8,128)(2,1)S(1)}, u32[]{:S(2)}, u32[]{:S(2)}) async-start(bf16[16,1,80,256]{3,2,1,0:T(8,128)(2,1)} %broadcast_in_dim.209), calls=%async_computation.7 | async-start | bytes 1310720 | tf_op jit(solution)/shard_map/all_to_all | solution.py:56
  233.7 5.7 collective-permute-start.3
  239.5 5.5 collective-permute-start.4
  245.0 6.1 collective-permute-start.5
  253.2 11.9 %all-to-all-start.8 = ((bf16[16,1,40,256]{3,2,1,0:T(8,128)(2,1)}), bf16[16,1,40,256]{3,2,1,0:T(8,128)(2,1)}, u32[]{:S(2)}, u32[]{:S(2)}) async-start(bf16[16,1,40,256]{3,2,1,0:T(8,128)(2,1)} %bitcast.198), calls=%async_computation.8 | async-start | bytes 655360 | tf_op jit(solution)/shard_map/all_to_all | solution.py:54
  266.8 11.9 %all-to-all-start.9 = ((bf16[16,1,40,256]{3,2,1,0:T(8,128)(2,1)}), bf16[16,1,40,256]{3,2,1,0:T(8,128)(2,1)}, u32[]{:S(2)}, u32[]{:S(2)}) async-start(bf16[16,1,40,256]{3,2,1,0:T(8,128)(2,1)} %broadcast_in_dim.318), calls=%async_computation.9 | async-start | bytes 655360 | tf_op jit(solution)/shard_map/all_to_all | solution.py:56
  281.2 5.4 collective-permute-start.6
  286.6 3.8 collective-permute-start.7
  290.4 5.1 collective-permute-start.8
  296.7 4.2 collective-permute-start.9
  301.0 5.8 collective-permute-start.10
  306.8 4.5 collective-permute-start.11
  311.4 7.2 %collective-permute-start.12 = (bf16[1,320,256]{2,1,0:T(8,128)(2,1)S(1)}, bf16[1,320,256]{2,1,0:T(8,128)(2,1)S(1)}, u32[]{:S(2)}, u32[]{:S(2)}) collective-permute-start(bf16[1,320,256]{2,1,0:T(8,128)(2,1)S(1)} %add_convert_fusion.13), channel_id=1, source_target_pairs={{0,64},{8,72},{16,80},{24,88},{32,96},{40,104},{48,112},{56,120},{... | collective-permute-start | bytes 491528 | tf_op jit(solution)/shard_map/ppermute | solution.py:63
  319.7 7.4 %collective-permute-start.13 = (bf16[1,160,256]{2,1,0:T(8,128)(2,1)S(1)}, bf16[1,160,256]{2,1,0:T(8,128)(2,1)S(1)}, u32[]{:S(2)}, u32[]{:S(2)}) collective-permute-start(bf16[1,160,256]{2,1,0:T(8,128)(2,1)S(1)} %fusion.61), channel_id=1, source_target_pairs={{0,1},{1,0},{2,3},{3,2},{4,5},{5,4},{6,7},{7,6},{8,9},{9,8},{10,11... | collective-permute-start | bytes 245768 | tf_op jit(solution)/shard_map/ppermute | solution.py:63
  327.1 3.8 collective-permute-start.14
  330.9 4.9 collective-permute-start.15
  362.6 6.0 collective-permute-start.16
  368.6 5.5 collective-permute-start.17
  374.2 6.1 collective-permute-start.18
  415.5 6.0 collective-permute-start.19
  421.6 9.0 %collective-permute-start.20 = (bf16[4,160,256]{2,1,0:T(8,128)(2,1)S(1)}, bf16[4,160,256]{2,1,0:T(8,128)(2,1)S(1)}, u32[]{:S(2)}, u32[]{:S(2)}) collective-permute-start(bf16[4,160,256]{2,1,0:T(8,128)(2,1)S(1)} %add_convert_fusion.4), channel_id=1, source_target_pairs={{0,2},{1,3},{2,0},{3,1},{4,6},{5,7},{6,4},{7,5},{8,10},{9,11},{10,... | collective-permute-start | bytes 983048 | tf_op jit(solution)/shard_map/ppermute | solution.py:63
  430.7 9.6 %collective-permute-start.21 = (bf16[4,160,256]{2,1,0:T(8,128)(2,1)S(1)}, bf16[4,160,256]{2,1,0:T(8,128)(2,1)S(1)}, u32[]{:S(2)}, u32[]{:S(2)}) collective-permute-start(bf16[4,160,256]{2,1,0:T(8,128)(2,1)S(1)} %add_convert_fusion.3), channel_id=1, source_target_pairs={{0,4},{1,5},{2,6},{3,7},{4,0},{5,1},{6,2},{7,3},{8,12},{9,13},{10,... | collective-permute-start | bytes 983048 | tf_op jit(solution)/shard_map/ppermute | solution.py:63
  490.3 19.1 %all-to-all-start.16 = ((bf16[8,1,160,256]{3,2,1,0:T(8,128)(2,1)}), bf16[8,1,160,256]{3,2,1,0:T(8,128)(2,1)S(1)}, u32[]{:S(2)}, u32[]{:S(2)}) async-start(bf16[8,1,160,256]{3,2,1,0:T(8,128)(2,1)} %fusion.53), calls=%async_computation.16 | async-start | bytes 1310720 | tf_op jit(solution)/shard_map/all_to_all | solution.py:54
  511.9 15.2 %all-to-all-start.17 = ((bf16[8,1,160,256]{3,2,1,0:T(8,128)(2,1)}), bf16[8,1,160,256]{3,2,1,0:T(8,128)(2,1)S(1)}, u32[]{:S(2)}, u32[]{:S(2)}) async-start(bf16[8,1,160,256]{3,2,1,0:T(8,128)(2,1)} %broadcast_in_dim.330), calls=%async_computation.17 | async-start | bytes 1310720 | tf_op jit(solution)/shard_map/all_to_all | solution.py:56
  (30 other events, 352.4 us)

commit v11 on v10

--- a/solution.py
+++ b/solution.py
@@ -52,8 +52,13 @@
         rows = shape[1] * k // n
         pieces = x.reshape((n, 1, rows) + shape[2:])
     got = lax.all_to_all(pieces, axis, 0, 0, tiled=False)
-    owned = jnp.sum(got.astype(jnp.float32), axis=0).astype(jnp.bfloat16)
-    spread = lax.all_to_all(jnp.broadcast_to(owned[None], (n,) + owned.shape), axis, 0, 0, tiled=False)
+    if got.size * n <= (1 << 22):
+        copies = jnp.broadcast_to(got.astype(jnp.float32)[None], (n,) + got.shape)
+        sent = jnp.sum(copies, axis=1).astype(jnp.bfloat16)
+    else:
+        owned = jnp.sum(got.astype(jnp.float32), axis=0).astype(jnp.bfloat16)
+        sent = jnp.broadcast_to(owned[None], (n,) + owned.shape)
+    spread = lax.all_to_all(sent, axis, 0, 0, tiled=False)
     return spread.reshape(shape)
 
 

time: 664 us -> 664 us (level)
  no operation moved by 1% of the time
where the time goes in v11:
time: 664 us; the launch traced here: 654 us
  blocking collectives  276 us (42%)
  waiting for transfers between devices  176 us (27%)
  starting transfers between devices  81.2 us (12%)
  matrix products  75.6 us (11%)
  other arithmetic  28.9 us (4%)
  local copies, waits for them, and re-layouts  15.7 us (2%)
    all_to_all x6, blocking collectives, a2a_allreduce(): got = lax.all_to_all(pieces, axis, 0, 0, tiled=False)  143 us
    all_to_all x5, blocking collectives, a2a_allreduce(): spread = lax.all_to_all(sent, axis, 0, 0, tiled=False)  93.2 us
    ppermute x22, waiting for transfers between devices, doubling_allreduce(): lax.ppermute(x, axis, xor_perm(n, bit)).astype(jnp.float32)  91.3 us
    all_to_all x5, waiting for transfers between devices, a2a_allreduce(): spread = lax.all_to_all(sent, axis, 0, 0, tiled=False)  52.5 us
    ppermute x22, starting transfers between devices, doubling_allreduce(): lax.ppermute(x, axis, xor_perm(n, bit)).astype(jnp.float32)  39.4 us
    all_to_all x4, waiting for transfers between devices, a2a_allreduce(): got = lax.all_to_all(pieces, axis, 0, 0, tiled=False)  32.4 us
    dot_general x10, matrix products, solve(): jnp.einsum('boj,boh->bjh', pair_slice(panel_local, tree_level, distance),...  26.5 us
    dot_general x10, matrix products, solve(): jnp.einsum('sjv,svk->sjk', pair_slice(panel_local, source_level, distance...  23 us
  transfers between devices with their start and end apart: 31, of which 31 were waited for; matrix products, arithmetic and copies ran while one was open for 6% of the time, Pallas kernels for 0%

profile of v11, /device:TPU:1, one launch (start us, length us, event | category | flops | bytes accessed | tf_op | source)
XLA Modules:
  0.0 654.5 jit_solution(2540967313522973625)
XLA Ops:
  3.3 39.6 %all_to_all.120 = bf16[16,1,320,256]{3,2,1,0:T(8,128)(2,1)S(1)} all-to-all(bf16[16,1,320,256]{3,2,1,0:T(8,128)(2,1)S(1)} %convert_bitcast_fusion), channel_id=1, replica_groups=mesh['x'=4,'y'=4,'z'=4,'core'=2] {'x','y'}, dimensions={0} | all-to-all | bytes 5242880 | tf_op jit(solution)/shard_map/all_to_all | solution.py:54
  50.8 29.3 %all-to-all-done.1 = bf16[16,1,320,256]{3,2,1,0:T(8,128)(2,1)S(1)} async-done(((bf16[16,1,320,256]{3,2,1,0:T(8,128)(2,1)}), bf16[16,1,320,256]{3,2,1,0:T(8,128)(2,1)S(1)}, u32[]{:S(2)}, u32[]{:S(2)}) %all-to-all-start.1) | async-done | bytes 2621472 | tf_op jit(solution)/shard_map/all_to_all | solution.py:61
  86.1 22.2 %all_to_all.121 = bf16[8,1,160,256]{3,2,1,0:T(8,128)(2,1)S(1)} all-to-all(bf16[8,1,160,256]{3,2,1,0:T(8,128)(2,1)S(1)} %bitcast.193), channel_id=1, replica_groups=mesh['x'=4,'y'=4,'z'=4,'core'=2] {'z','core'}, dimensions={0} | all-to-all | bytes 1310720 | tf_op jit(solution)/shard_map/all_to_all | solution.py:54
  108.5 14.2 %all_to_all.122 = bf16[8,1,160,256]{3,2,1,0:T(8,128)(2,1)S(1)} all-to-all(bf16[8,1,160,256]{3,2,1,0:T(8,128)(2,1)S(1)} %reduce_sum.245), channel_id=1, replica_groups=mesh['x'=4,'y'=4,'z'=4,'core'=2] {'z','core'}, dimensions={0} | all-to-all | bytes 1310720 | tf_op jit(solution)/shard_map/all_to_all | solution.py:61
  131.8 16.8 %all-to-all-done.4 = bf16[16,1,160,256]{3,2,1,0:T(8,128)(2,1)} async-done(((bf16[16,1,160,256]{3,2,1,0:T(8,128)(2,1)}), bf16[16,1,160,256]{3,2,1,0:T(8,128)(2,1)}, u32[]{:S(2)}, u32[]{:S(2)}) %all-to-all-start.4) | async-done | bytes 1310752 | tf_op jit(solution)/shard_map/all_to_all | solution.py:54
  160.5 12.7 %all-to-all-done.5 = bf16[16,1,160,256]{3,2,1,0:T(8,128)(2,1)} async-done(((bf16[16,1,160,256]{3,2,1,0:T(8,128)(2,1)}), bf16[16,1,160,256]{3,2,1,0:T(8,128)(2,1)}, u32[]{:S(2)}, u32[]{:S(2)}) %all-to-all-start.5) | async-done | bytes 1310752 | tf_op jit(solution)/shard_map/all_to_all | solution.py:61
  182.7 8.0 %collective-permute-done.1 = bf16[4,160,256]{2,1,0:T(8,128)(2,1)} collective-permute-done((bf16[4,160,256]{2,1,0:T(8,128)(2,1)S(1)}, bf16[4,160,256]{2,1,0:T(8,128)(2,1)}, u32[]{:S(2)}, u32[]{:S(2)}) %collective-permute-start.1) | collective-permute-done | bytes 327712 | tf_op jit(solution)/shard_map/ppermute | solution.py:68
  193.3 8.0 %collective-permute-done.2 = bf16[4,160,256]{2,1,0:T(8,128)(2,1)S(1)} collective-permute-done((bf16[4,160,256]{2,1,0:T(8,128)(2,1)S(1)}, bf16[4,160,256]{2,1,0:T(8,128)(2,1)S(1)}, u32[]{:S(2)}, u32[]{:S(2)}) %collective-permute-start.2) | collective-permute-done | bytes 327712 | tf_op jit(solution)/shard_map/ppermute | solution.py:68
  211.4 6.2 all-to-all-done.6
  239.9 5.1 collective-permute-done.4
  259.8 5.2 all-to-all-done.8
  312.4 6.1 collective-permute-done.12
  319.7 6.5 collective-permute-start.13
  337.7 11.4 %all_to_all.123 = bf16[16,1,40,256]{3,2,1,0:T(8,128)(2,1)} all-to-all(bf16[16,1,40,256]{3,2,1,0:T(8,128)(2,1)S(1)} %bitcast.197), channel_id=1, replica_groups=mesh['x'=4,'y'=4,'z'=4,'core'=2] {'x','y'}, dimensions={0} | all-to-all | bytes 655360 | tf_op jit(solution)/shard_map/all_to_all | solution.py:54
  350.1 11.0 %all_to_all.124 = bf16[16,1,40,256]{3,2,1,0:T(8,128)(2,1)S(1)} all-to-all(bf16[16,1,40,256]{3,2,1,0:T(8,128)(2,1)S(1)} %reduce_sum.260), channel_id=1, replica_groups=mesh['x'=4,'y'=4,'z'=4,'core'=2] {'x','y'}, dimensions={0} | all-to-all | bytes 655360 | tf_op jit(solution)/shard_map/all_to_all | solution.py:61
  369.0 5.1 collective-permute-done.17
  374.9 5.3 collective-permute-done.18
  385.1 13.4 %all_to_all.125 = bf16[16,1,80,256]{3,2,1,0:T(8,128)(2,1)} all-to-all(bf16[16,1,80,256]{3,2,1,0:T(8,128)(2,1)S(1)} %bitcast.194), channel_id=1, replica_groups=mesh['x'=4,'y'=4,'z'=4,'core'=2] {'x','y'}, dimensions={0} | all-to-all | bytes 1310720 | tf_op jit(solution)/shard_map/all_to_all | solution.py:54
  401.1 13.0 %all_to_all.126 = bf16[16,1,80,256]{3,2,1,0:T(8,128)(2,1)S(1)} all-to-all(bf16[16,1,80,256]{3,2,1,0:T(8,128)(2,1)S(1)} %broadcast_in_dim.317), channel_id=1, replica_groups=mesh['x'=4,'y'=4,'z'=4,'core'=2] {'x','y'}, dimensions={0} | all-to-all | bytes 1310720 | tf_op jit(solution)/shard_map/all_to_all | solution.py:61
  422.4 8.2 %collective-permute-done.20 = bf16[4,160,256]{2,1,0:T(8,128)(2,1)S(1)} collective-permute-done((bf16[4,160,256]{2,1,0:T(8,128)(2,1)S(1)}, bf16[4,160,256]{2,1,0:T(8,128)(2,1)S(1)}, u32[]{:S(2)}, u32[]{:S(2)}) %collective-permute-start.20) | collective-permute-done | bytes 327712 | tf_op jit(solution)/shard_map/ppermute | solution.py:68
  433.4 7.0 %collective-permute-done.21 = bf16[4,160,256]{2,1,0:T(8,128)(2,1)S(1)} collective-permute-done((bf16[4,160,256]{2,1,0:T(8,128)(2,1)S(1)}, bf16[4,160,256]{2,1,0:T(8,128)(2,1)S(1)}, u32[]{:S(2)}, u32[]{:S(2)}) %collective-permute-start.21) | collective-permute-done | bytes 327712 | tf_op jit(solution)/shard_map/ppermute | solution.py:68
  445.5 20.7 %all_to_all.127 = bf16[16,1,160,256]{3,2,1,0:T(8,128)(2,1)} all-to-all(bf16[16,1,160,256]{3,2,1,0:T(8,128)(2,1)S(1)} %bitcast.188), channel_id=1, replica_groups=mesh['x'=4,'y'=4,'z'=4,'core'=2] {'x','y'}, dimensions={0} | all-to-all | bytes 2621440 | tf_op jit(solution)/shard_map/all_to_all | solution.py:54
  467.8 19.4 %all_to_all.128 = bf16[16,1,160,256]{3,2,1,0:T(8,128)(2,1)S(1)} all-to-all(bf16[16,1,160,256]{3,2,1,0:T(8,128)(2,1)S(1)} %broadcast_in_dim.318), channel_id=1, replica_groups=mesh['x'=4,'y'=4,'z'=4,'core'=2] {'x','y'}, dimensions={0} | all-to-all | bytes 2621440 | tf_op jit(solution)/shard_map/all_to_all | solution.py:61
  490.3 8.3 %all-to-all-start.16 = ((bf16[8,1,160,256]{3,2,1,0:T(8,128)(2,1)}), bf16[8,1,160,256]{3,2,1,0:T(8,128)(2,1)S(1)}, u32[]{:S(2)}, u32[]{:S(2)}) async-start(bf16[8,1,160,256]{3,2,1,0:T(8,128)(2,1)} %fusion.53), calls=%async_computation.16 | async-start | bytes 1310720 | tf_op jit(solution)/shard_map/all_to_all | solution.py:54
  500.1 5.2 fusion.29
  517.9 5.2 fusion.32
  535.0 36.1 %all_to_all.129 = bf16[16,1,320,256]{3,2,1,0:T(8,128)(2,1)} all-to-all(bf16[16,1,320,256]{3,2,1,0:T(8,128)(2,1)S(1)} %fusion.1), channel_id=1, replica_groups=mesh['x'=4,'y'=4,'z'=4,'core'=2] {'x','y'}, dimensions={0} | all-to-all | bytes 5242880 | tf_op jit(solution)/shard_map/all_to_all | solution.py:54
  573.5 35.6 %all_to_all.130 = bf16[16,1,320,256]{3,2,1,0:T(8,128)(2,1)S(1)} all-to-all(bf16[16,1,320,256]{3,2,1,0:T(8,128)(2,1)S(1)} %broadcast_in_dim.319), channel_id=1, replica_groups=mesh['x'=4,'y'=4,'z'=4,'core'=2] {'x','y'}, dimensions={0} | all-to-all | bytes 5242880 | tf_op jit(solution)/shard_map/all_to_all | solution.py:61
  610.0 7.5 %all_to_all.131 = bf16[2,4,2,160,256]{4,3,2,1,0:T(8,128)(2,1)S(1)} all-to-all(bf16[2,4,2,160,256]{4,3,2,1,0:T(8,128)(2,1)S(1)} %bitcast.189), channel_id=1, replica_groups=mesh['x'=4,'y'=4,'z'=4,'core'=2] {'core'}, dimensions={0} | all-to-all | bytes 2621440 | tf_op jit(solution)/shard_map/all_to_all | solution.py:81
  618.0 13.0 %all_to_all.132 = bf16[4,1,2,160,256]{4,3,2,1,0:T(8,128)(2,1)S(1)} all-to-all(bf16[4,1,2,160,256]{4,3,2,1,0:T(8,128)(2,1)S(1)} %bitcast.191), channel_id=1, replica_groups=mesh['x'=4,'y'=4,'z'=4,'core'=2] {'z'}, dimensions={0} | all-to-all | bytes 1310720 | tf_op jit(solution)/shard_map/all_to_all | solution.py:81
  631.2 12.1 %all_to_all.133 = bf16[4,1,2,160,256]{4,3,2,1,0:T(8,128)(2,1)S(1)} all-to-all(bf16[4,1,2,160,256]{4,3,2,1,0:T(8,128)(2,1)S(1)} %broadcast_in_dim.320), channel_id=1, replica_groups=mesh['x'=4,'y'=4,'z'=4,'core'=2] {'z'}, dimensions={0} | all-to-all | bytes 1310720 | tf_op jit(solution)/shard_map/all_to_all | solution.py:84
  643.5 6.5 all_to_all.134
  (230 shorter events, 229.3 us)
Async XLA Ops:
  45.1 35.0 %all-to-all-start.1 = ((bf16[16,1,320,256]{3,2,1,0:T(8,128)(2,1)}), bf16[16,1,320,256]{3,2,1,0:T(8,128)(2,1)S(1)}, u32[]{:S(2)}, u32[]{:S(2)}) async-start(bf16[16,1,320,256]{3,2,1,0:T(8,128)(2,1)} %broadcast_in_dim.189), calls=%async_computation.1 | async-start | bytes 5242880 | tf_op jit(solution)/shard_map/all_to_all | solution.py:61
  50.2 106.0 %copy-start.19 = (s32[31]{0:T(128)}, s32[31]{0:T(128)S(1)}, u32[]{:S(2)}) copy-start(s32[31]{0:T(128)S(1)} %get-tuple-element.18) | copy-start | bytes 376
  126.0 22.6 %all-to-all-start.4 = ((bf16[16,1,160,256]{3,2,1,0:T(8,128)(2,1)}), bf16[16,1,160,256]{3,2,1,0:T(8,128)(2,1)}, u32[]{:S(2)}, u32[]{:S(2)}) async-start(bf16[16,1,160,256]{3,2,1,0:T(8,128)(2,1)} %bitcast.185), calls=%async_computation.4 | async-start | bytes 2621440 | tf_op jit(solution)/shard_map/all_to_all | solution.py:54
  151.3 21.8 %all-to-all-start.5 = ((bf16[16,1,160,256]{3,2,1,0:T(8,128)(2,1)}), bf16[16,1,160,256]{3,2,1,0:T(8,128)(2,1)}, u32[]{:S(2)}, u32[]{:S(2)}) async-start(bf16[16,1,160,256]{3,2,1,0:T(8,128)(2,1)} %broadcast_in_dim.193), calls=%async_computation.5 | async-start | bytes 2621440 | tf_op jit(solution)/shard_map/all_to_all | solution.py:61
  176.0 5.5 collective-permute-start
  181.6 9.1 %collective-permute-start.1 = (bf16[4,160,256]{2,1,0:T(8,128)(2,1)S(1)}, bf16[4,160,256]{2,1,0:T(8,128)(2,1)}, u32[]{:S(2)}, u32[]{:S(2)}) collective-permute-start(bf16[4,160,256]{2,1,0:T(8,128)(2,1)S(1)} %add_convert_fusion.7), channel_id=1, source_target_pairs={{0,2},{1,3},{2,0},{3,1},{4,6},{5,7},{6,4},{7,5},{8,10},{9,11},{10,... | collective-permute-start | bytes 983048 | tf_op jit(solution)/shard_map/ppermute | solution.py:68
  191.8 9.6 %collective-permute-start.2 = (bf16[4,160,256]{2,1,0:T(8,128)(2,1)S(1)}, bf16[4,160,256]{2,1,0:T(8,128)(2,1)S(1)}, u32[]{:S(2)}, u32[]{:S(2)}) collective-permute-start(bf16[4,160,256]{2,1,0:T(8,128)(2,1)S(1)} %add_convert_fusion.6), channel_id=1, source_target_pairs={{0,4},{1,5},{2,6},{3,7},{4,0},{5,1},{6,2},{7,3},{8,12},{9,13},{10,... | collective-permute-start | bytes 983048 | tf_op jit(solution)/shard_map/ppermute | solution.py:68
  203.9 13.7 %all-to-all-start.6 = ((bf16[16,1,80,256]{3,2,1,0:T(8,128)(2,1)}), bf16[16,1,80,256]{3,2,1,0:T(8,128)(2,1)S(1)}, u32[]{:S(2)}, u32[]{:S(2)}) async-start(bf16[16,1,80,256]{3,2,1,0:T(8,128)(2,1)} %bitcast.192), calls=%async_computation.6 | async-start | bytes 1310720 | tf_op jit(solution)/shard_map/all_to_all | solution.py:54
  218.6 13.4 %all-to-all-start.7 = ((bf16[16,1,80,256]{3,2,1,0:T(8,128)(2,1)}), bf16[16,1,80,256]{3,2,1,0:T(8,128)(2,1)S(1)}, u32[]{:S(2)}, u32[]{:S(2)}) async-start(bf16[16,1,80,256]{3,2,1,0:T(8,128)(2,1)} %broadcast_in_dim.200), calls=%async_computation.7 | async-start | bytes 1310720 | tf_op jit(solution)/shard_map/all_to_all | solution.py:61
  233.7 5.7 collective-permute-start.3
  239.5 5.5 collective-permute-start.4
  245.0 6.1 collective-permute-start.5
  253.2 11.9 %all-to-all-start.8 = ((bf16[16,1,40,256]{3,2,1,0:T(8,128)(2,1)}), bf16[16,1,40,256]{3,2,1,0:T(8,128)(2,1)}, u32[]{:S(2)}, u32[]{:S(2)}) async-start(bf16[16,1,40,256]{3,2,1,0:T(8,128)(2,1)} %bitcast.198), calls=%async_computation.8 | async-start | bytes 655360 | tf_op jit(solution)/shard_map/all_to_all | solution.py:54
  266.8 11.9 %all-to-all-start.9 = ((bf16[16,1,40,256]{3,2,1,0:T(8,128)(2,1)}), bf16[16,1,40,256]{3,2,1,0:T(8,128)(2,1)}, u32[]{:S(2)}, u32[]{:S(2)}) async-start(bf16[16,1,40,256]{3,2,1,0:T(8,128)(2,1)} %reduce_sum.254), calls=%async_computation.9 | async-start | bytes 655360 | tf_op jit(solution)/shard_map/all_to_all | solution.py:61
  281.2 5.4 collective-permute-start.6
  286.6 3.8 collective-permute-start.7
  290.4 5.1 collective-permute-start.8
  296.7 4.2 collective-permute-start.9
  301.0 5.8 collective-permute-start.10
  306.8 4.5 collective-permute-start.11
  311.4 7.2 %collective-permute-start.12 = (bf16[1,320,256]{2,1,0:T(8,128)(2,1)S(1)}, bf16[1,320,256]{2,1,0:T(8,128)(2,1)S(1)}, u32[]{:S(2)}, u32[]{:S(2)}) collective-permute-start(bf16[1,320,256]{2,1,0:T(8,128)(2,1)S(1)} %add_convert_fusion.13), channel_id=1, source_target_pairs={{0,64},{8,72},{16,80},{24,88},{32,96},{40,104},{48,112},{56,120},{... | collective-permute-start | bytes 491528 | tf_op jit(solution)/shard_map/ppermute | solution.py:68
  319.7 7.4 %collective-permute-start.13 = (bf16[1,160,256]{2,1,0:T(8,128)(2,1)S(1)}, bf16[1,160,256]{2,1,0:T(8,128)(2,1)S(1)}, u32[]{:S(2)}, u32[]{:S(2)}) collective-permute-start(bf16[1,160,256]{2,1,0:T(8,128)(2,1)S(1)} %fusion.61), channel_id=1, source_target_pairs={{0,1},{1,0},{2,3},{3,2},{4,5},{5,4},{6,7},{7,6},{8,9},{9,8},{10,11... | collective-permute-start | bytes 245768 | tf_op jit(solution)/shard_map/ppermute | solution.py:68
  327.1 3.8 collective-permute-start.14
  330.9 4.9 collective-permute-start.15
  362.6 6.0 collective-permute-start.16
  368.6 5.5 collective-permute-start.17
  374.2 6.1 collective-permute-start.18
  415.5 6.0 collective-permute-start.19
  421.6 9.0 %collective-permute-start.20 = (bf16[4,160,256]{2,1,0:T(8,128)(2,1)S(1)}, bf16[4,160,256]{2,1,0:T(8,128)(2,1)S(1)}, u32[]{:S(2)}, u32[]{:S(2)}) collective-permute-start(bf16[4,160,256]{2,1,0:T(8,128)(2,1)S(1)} %add_convert_fusion.4), channel_id=1, source_target_pairs={{0,2},{1,3},{2,0},{3,1},{4,6},{5,7},{6,4},{7,5},{8,10},{9,11},{10,... | collective-permute-start | bytes 983048 | tf_op jit(solution)/shard_map/ppermute | solution.py:68
  430.7 9.6 %collective-permute-start.21 = (bf16[4,160,256]{2,1,0:T(8,128)(2,1)S(1)}, bf16[4,160,256]{2,1,0:T(8,128)(2,1)S(1)}, u32[]{:S(2)}, u32[]{:S(2)}) collective-permute-start(bf16[4,160,256]{2,1,0:T(8,128)(2,1)S(1)} %add_convert_fusion.3), channel_id=1, source_target_pairs={{0,4},{1,5},{2,6},{3,7},{4,0},{5,1},{6,2},{7,3},{8,12},{9,13},{10,... | collective-permute-start | bytes 983048 | tf_op jit(solution)/shard_map/ppermute | solution.py:68
  490.3 19.1 %all-to-all-start.16 = ((bf16[8,1,160,256]{3,2,1,0:T(8,128)(2,1)}), bf16[8,1,160,256]{3,2,1,0:T(8,128)(2,1)S(1)}, u32[]{:S(2)}, u32[]{:S(2)}) async-start(bf16[8,1,160,256]{3,2,1,0:T(8,128)(2,1)} %fusion.53), calls=%async_computation.16 | async-start | bytes 1310720 | tf_op jit(solution)/shard_map/all_to_all | solution.py:54
  511.9 15.2 %all-to-all-start.17 = ((bf16[8,1,160,256]{3,2,1,0:T(8,128)(2,1)}), bf16[8,1,160,256]{3,2,1,0:T(8,128)(2,1)S(1)}, u32[]{:S(2)}, u32[]{:S(2)}) async-start(bf16[8,1,160,256]{3,2,1,0:T(8,128)(2,1)} %reduce_sum.264), calls=%async_computation.17 | async-start | bytes 1310720 | tf_op jit(solution)/shard_map/all_to_all | solution.py:61
  (30 other events, 352.4 us)

commit v12 on v11

--- a/solution.py
+++ b/solution.py
@@ -135,7 +135,7 @@
         forward_levels[tree_level] = forward_value.astype(jnp.float32)
         forward_half[tree_level] = forward_value
     solution_half = [None] * 5
-    results = [None] * 5
+    results = jnp.zeros(right_side.shape, jnp.float32)
     for tree_level in (4, 3, 2, 1, 0):
         start_node = level_starts[tree_level]
         node_count = level_counts[tree_level]
@@ -167,9 +167,9 @@
             preferred_element_type=jnp.float32,
         )
         solution = group_allreduce(division_count.astype(jnp.bfloat16), COL, n_col)
-        results[tree_level] = solution.astype(jnp.float32)
+        results = lax.dynamic_update_slice_in_dim(results, solution.astype(jnp.float32), start_node, axis=0)
         solution_half[tree_level] = solution
-    return jnp.concatenate(results, axis=0)
+    return results
 
 
 def solution(mesh):

time: 664 us -> 660 us (level)
  blocking collectives: 276 us -> 264 us
  waiting for transfers between devices: 176 us -> 184 us
    all_to_all x2 -> x1, blocking collectives: 18.7 us -> 6.54 us  [staged_allreduce(): lax.all_to_all(jnp.broadcast_to(cur[None], (size,) + cur.shape), axis, 0,...]
    all_to_all x0 -> x1, waiting for transfers between devices: none -> 8.5 us  [staged_allreduce(): lax.all_to_all(jnp.broadcast_to(cur[None], (size,) + cur.shape), axis, 0,...]
  transfers between devices with their start and end apart: 31 -> 32, of which waited for: 31 -> 32; matrix products, arithmetic and copies ran while one was open for 6% -> 7% of each run, Pallas kernels for 0% -> 0%
where the time goes in v12:
time: 660 us; the launch traced here: 651 us
  blocking collectives  264 us (40%)
  waiting for transfers between devices  184 us (28%)
  starting transfers between devices  84.6 us (13%)
  matrix products  75.3 us (11%)
  other arithmetic  29.1 us (4%)
  local copies, waits for them, and re-layouts  13.2 us (2%)
    all_to_all x6, blocking collectives, a2a_allreduce(): got = lax.all_to_all(pieces, axis, 0, 0, tiled=False)  143 us
    all_to_all x5, blocking collectives, a2a_allreduce(): spread = lax.all_to_all(sent, axis, 0, 0, tiled=False)  93.2 us
    ppermute x22, waiting for transfers between devices, doubling_allreduce(): lax.ppermute(x, axis, xor_perm(n, bit)).astype(jnp.float32)  90.8 us
    all_to_all x5, waiting for transfers between devices, a2a_allreduce(): spread = lax.all_to_all(sent, axis, 0, 0, tiled=False)  52.5 us
    ppermute x22, starting transfers between devices, doubling_allreduce(): lax.ppermute(x, axis, xor_perm(n, bit)).astype(jnp.float32)  39.3 us
    all_to_all x4, waiting for transfers between devices, a2a_allreduce(): got = lax.all_to_all(pieces, axis, 0, 0, tiled=False)  32.4 us
    dot_general x10, matrix products, solve(): jnp.einsum('boj,boh->bjh', pair_slice(panel_local, tree_level, distance),...  26.8 us
    dot_general x10, matrix products, solve(): jnp.einsum('sjv,svk->sjk', pair_slice(panel_local, source_level, distance...  22.9 us
  transfers between devices with their start and end apart: 32, of which 32 were waited for; matrix products, arithmetic and copies ran while one was open for 7% of the time, Pallas kernels for 0%

profile of v12, /device:TPU:1, one launch (start us, length us, event | category | flops | bytes accessed | tf_op | source)
XLA Modules:
  0.0 651.2 jit_solution(1243162462029668530)
XLA Ops:
  3.3 39.6 %all_to_all.120 = bf16[16,1,320,256]{3,2,1,0:T(8,128)(2,1)S(1)} all-to-all(bf16[16,1,320,256]{3,2,1,0:T(8,128)(2,1)S(1)} %convert_bitcast_fusion), channel_id=1, replica_groups=mesh['x'=4,'y'=4,'z'=4,'core'=2] {'x','y'}, dimensions={0} | all-to-all | bytes 5242880 | tf_op jit(solution)/shard_map/all_to_all | solution.py:54
  50.8 29.3 %all-to-all-done.1 = bf16[16,1,320,256]{3,2,1,0:T(8,128)(2,1)S(1)} async-done(((bf16[16,1,320,256]{3,2,1,0:T(8,128)(2,1)}), bf16[16,1,320,256]{3,2,1,0:T(8,128)(2,1)S(1)}, u32[]{:S(2)}, u32[]{:S(2)}) %all-to-all-start.1) | async-done | bytes 2621472 | tf_op jit(solution)/shard_map/all_to_all | solution.py:61
  86.1 22.2 %all_to_all.121 = bf16[8,1,160,256]{3,2,1,0:T(8,128)(2,1)S(1)} all-to-all(bf16[8,1,160,256]{3,2,1,0:T(8,128)(2,1)S(1)} %bitcast.193), channel_id=1, replica_groups=mesh['x'=4,'y'=4,'z'=4,'core'=2] {'z','core'}, dimensions={0} | all-to-all | bytes 1310720 | tf_op jit(solution)/shard_map/all_to_all | solution.py:54
  108.5 14.2 %all_to_all.122 = bf16[8,1,160,256]{3,2,1,0:T(8,128)(2,1)S(1)} all-to-all(bf16[8,1,160,256]{3,2,1,0:T(8,128)(2,1)S(1)} %reduce_sum.246), channel_id=1, replica_groups=mesh['x'=4,'y'=4,'z'=4,'core'=2] {'z','core'}, dimensions={0} | all-to-all | bytes 1310720 | tf_op jit(solution)/shard_map/all_to_all | solution.py:61
  131.8 16.8 %all-to-all-done.4 = bf16[16,1,160,256]{3,2,1,0:T(8,128)(2,1)} async-done(((bf16[16,1,160,256]{3,2,1,0:T(8,128)(2,1)}), bf16[16,1,160,256]{3,2,1,0:T(8,128)(2,1)}, u32[]{:S(2)}, u32[]{:S(2)}) %all-to-all-start.4) | async-done | bytes 1310752 | tf_op jit(solution)/shard_map/all_to_all | solution.py:54
  160.4 12.7 %all-to-all-done.5 = bf16[16,1,160,256]{3,2,1,0:T(8,128)(2,1)} async-done(((bf16[16,1,160,256]{3,2,1,0:T(8,128)(2,1)}), bf16[16,1,160,256]{3,2,1,0:T(8,128)(2,1)}, u32[]{:S(2)}, u32[]{:S(2)}) %all-to-all-start.5) | async-done | bytes 1310752 | tf_op jit(solution)/shard_map/all_to_all | solution.py:61
  182.7 8.0 %collective-permute-done.1 = bf16[4,160,256]{2,1,0:T(8,128)(2,1)} collective-permute-done((bf16[4,160,256]{2,1,0:T(8,128)(2,1)S(1)}, bf16[4,160,256]{2,1,0:T(8,128)(2,1)}, u32[]{:S(2)}, u32[]{:S(2)}) %collective-permute-start.1) | collective-permute-done | bytes 327712 | tf_op jit(solution)/shard_map/ppermute | solution.py:68
  193.4 8.0 %collective-permute-done.2 = bf16[4,160,256]{2,1,0:T(8,128)(2,1)S(1)} collective-permute-done((bf16[4,160,256]{2,1,0:T(8,128)(2,1)S(1)}, bf16[4,160,256]{2,1,0:T(8,128)(2,1)S(1)}, u32[]{:S(2)}, u32[]{:S(2)}) %collective-permute-start.2) | collective-permute-done | bytes 327712 | tf_op jit(solution)/shard_map/ppermute | solution.py:68
  211.4 6.2 all-to-all-done.6
  239.9 5.1 collective-permute-done.4
  259.8 5.2 all-to-all-done.8
  312.4 6.1 collective-permute-done.12
  319.7 6.5 collective-permute-start.13
  337.1 11.4 %all_to_all.123 = bf16[16,1,40,256]{3,2,1,0:T(8,128)(2,1)} all-to-all(bf16[16,1,40,256]{3,2,1,0:T(8,128)(2,1)S(1)} %bitcast.196), channel_id=1, replica_groups=mesh['x'=4,'y'=4,'z'=4,'core'=2] {'x','y'}, dimensions={0} | all-to-all | bytes 655360 | tf_op jit(solution)/shard_map/all_to_all | solution.py:54
  349.5 11.0 %all_to_all.124 = bf16[16,1,40,256]{3,2,1,0:T(8,128)(2,1)S(1)} all-to-all(bf16[16,1,40,256]{3,2,1,0:T(8,128)(2,1)S(1)} %reduce_sum.260), channel_id=1, replica_groups=mesh['x'=4,'y'=4,'z'=4,'core'=2] {'x','y'}, dimensions={0} | all-to-all | bytes 655360 | tf_op jit(solution)/shard_map/all_to_all | solution.py:61
  361.9 5.0 collective-permute-start.16
  368.4 5.1 collective-permute-done.17
  384.1 13.4 %all_to_all.125 = bf16[16,1,80,256]{3,2,1,0:T(8,128)(2,1)} all-to-all(bf16[16,1,80,256]{3,2,1,0:T(8,128)(2,1)S(1)} %bitcast.194), channel_id=1, replica_groups=mesh['x'=4,'y'=4,'z'=4,'core'=2] {'x','y'}, dimensions={0} | all-to-all | bytes 1310720 | tf_op jit(solution)/shard_map/all_to_all | solution.py:54
  398.7 13.0 %all_to_all.126 = bf16[16,1,80,256]{3,2,1,0:T(8,128)(2,1)S(1)} all-to-all(bf16[16,1,80,256]{3,2,1,0:T(8,128)(2,1)S(1)} %broadcast_in_dim.318), channel_id=1, replica_groups=mesh['x'=4,'y'=4,'z'=4,'core'=2] {'x','y'}, dimensions={0} | all-to-all | bytes 1310720 | tf_op jit(solution)/shard_map/all_to_all | solution.py:61
  420.1 8.2 %collective-permute-done.20 = bf16[4,160,256]{2,1,0:T(8,128)(2,1)S(1)} collective-permute-done((bf16[4,160,256]{2,1,0:T(8,128)(2,1)S(1)}, bf16[4,160,256]{2,1,0:T(8,128)(2,1)S(1)}, u32[]{:S(2)}, u32[]{:S(2)}) %collective-permute-start.20) | collective-permute-done | bytes 327712 | tf_op jit(solution)/shard_map/ppermute | solution.py:68
  431.0 7.0 %collective-permute-done.21 = bf16[4,160,256]{2,1,0:T(8,128)(2,1)S(1)} collective-permute-done((bf16[4,160,256]{2,1,0:T(8,128)(2,1)S(1)}, bf16[4,160,256]{2,1,0:T(8,128)(2,1)S(1)}, u32[]{:S(2)}, u32[]{:S(2)}) %collective-permute-start.21) | collective-permute-done | bytes 327712 | tf_op jit(solution)/shard_map/ppermute | solution.py:68
  444.0 20.7 %all_to_all.127 = bf16[16,1,160,256]{3,2,1,0:T(8,128)(2,1)} all-to-all(bf16[16,1,160,256]{3,2,1,0:T(8,128)(2,1)S(1)} %bitcast.187), channel_id=1, replica_groups=mesh['x'=4,'y'=4,'z'=4,'core'=2] {'x','y'}, dimensions={0} | all-to-all | bytes 2621440 | tf_op jit(solution)/shard_map/all_to_all | solution.py:54
  466.3 19.4 %all_to_all.128 = bf16[16,1,160,256]{3,2,1,0:T(8,128)(2,1)S(1)} all-to-all(bf16[16,1,160,256]{3,2,1,0:T(8,128)(2,1)S(1)} %broadcast_in_dim.319), channel_id=1, replica_groups=mesh['x'=4,'y'=4,'z'=4,'core'=2] {'x','y'}, dimensions={0} | all-to-all | bytes 2621440 | tf_op jit(solution)/shard_map/all_to_all | solution.py:61
  488.8 8.3 %all-to-all-start.16 = ((bf16[8,1,160,256]{3,2,1,0:T(8,128)(2,1)}), bf16[8,1,160,256]{3,2,1,0:T(8,128)(2,1)S(1)}, u32[]{:S(2)}, u32[]{:S(2)}) async-start(bf16[8,1,160,256]{3,2,1,0:T(8,128)(2,1)} %fusion.53), calls=%async_computation.16 | async-start | bytes 1310720 | tf_op jit(solution)/shard_map/all_to_all | solution.py:54
  498.7 5.2 fusion.27
  514.9 5.2 fusion.30
  532.1 36.1 %all_to_all.129 = bf16[16,1,320,256]{3,2,1,0:T(8,128)(2,1)} all-to-all(bf16[16,1,320,256]{3,2,1,0:T(8,128)(2,1)S(1)} %fusion.1), channel_id=1, replica_groups=mesh['x'=4,'y'=4,'z'=4,'core'=2] {'x','y'}, dimensions={0} | all-to-all | bytes 5242880 | tf_op jit(solution)/shard_map/all_to_all | solution.py:54
  570.5 35.6 %all_to_all.130 = bf16[16,1,320,256]{3,2,1,0:T(8,128)(2,1)S(1)} all-to-all(bf16[16,1,320,256]{3,2,1,0:T(8,128)(2,1)S(1)} %broadcast_in_dim.320), channel_id=1, replica_groups=mesh['x'=4,'y'=4,'z'=4,'core'=2] {'x','y'}, dimensions={0} | all-to-all | bytes 5242880 | tf_op jit(solution)/shard_map/all_to_all | solution.py:61
  607.1 7.5 %all_to_all.131 = bf16[2,4,2,160,256]{4,3,2,1,0:T(8,128)(2,1)S(1)} all-to-all(bf16[2,4,2,160,256]{4,3,2,1,0:T(8,128)(2,1)S(1)} %bitcast.188), channel_id=1, replica_groups=mesh['x'=4,'y'=4,'z'=4,'core'=2] {'core'}, dimensions={0} | all-to-all | bytes 2621440 | tf_op jit(solution)/shard_map/all_to_all | solution.py:81
  615.1 13.0 %all_to_all.132 = bf16[4,1,2,160,256]{4,3,2,1,0:T(8,128)(2,1)S(1)} all-to-all(bf16[4,1,2,160,256]{4,3,2,1,0:T(8,128)(2,1)S(1)} %bitcast.190), channel_id=1, replica_groups=mesh['x'=4,'y'=4,'z'=4,'core'=2] {'z'}, dimensions={0} | all-to-all | bytes 1310720 | tf_op jit(solution)/shard_map/all_to_all | solution.py:81
  633.8 8.5 %all-to-all-done.22 = bf16[4,1,2,160,256]{4,3,2,1,0:T(8,128)(2,1)S(1)} async-done(((bf16[4,1,2,160,256]{4,3,2,1,0:T(8,128)(2,1)}), bf16[4,1,2,160,256]{4,3,2,1,0:T(8,128)(2,1)S(1)}, u32[]{:S(2)}, u32[]{:S(2)}) %all-to-all-start.22) | async-done | bytes 655392 | tf_op jit(solution)/shard_map/all_to_all | solution.py:84
  642.5 6.5 %all_to_all.133 = bf16[2,4,2,160,256]{4,3,2,1,0:T(8,128)(2,1)S(1)} all-to-all(bf16[2,4,2,160,256]{4,3,2,1,0:T(8,128)(2,1)S(1)} %broadcast_in_dim.323), channel_id=1, replica_groups=mesh['x'=4,'y'=4,'z'=4,'core'=2] {'core'}, dimensions={0} | all-to-all | bytes 2621440 | tf_op jit(solution)/shard_map/all_to_all | solution.py:84
  (224 shorter events, 229.9 us)
Async XLA Ops:
  45.1 35.0 %all-to-all-start.1 = ((bf16[16,1,320,256]{3,2,1,0:T(8,128)(2,1)}), bf16[16,1,320,256]{3,2,1,0:T(8,128)(2,1)S(1)}, u32[]{:S(2)}, u32[]{:S(2)}) async-start(bf16[16,1,320,256]{3,2,1,0:T(8,128)(2,1)} %broadcast_in_dim.190), calls=%async_computation.1 | async-start | bytes 5242880 | tf_op jit(solution)/shard_map/all_to_all | solution.py:61
  126.0 22.6 %all-to-all-start.4 = ((bf16[16,1,160,256]{3,2,1,0:T(8,128)(2,1)}), bf16[16,1,160,256]{3,2,1,0:T(8,128)(2,1)}, u32[]{:S(2)}, u32[]{:S(2)}) async-start(bf16[16,1,160,256]{3,2,1,0:T(8,128)(2,1)} %bitcast.184), calls=%async_computation.4 | async-start | bytes 2621440 | tf_op jit(solution)/shard_map/all_to_all | solution.py:54
  151.3 21.8 %all-to-all-start.5 = ((bf16[16,1,160,256]{3,2,1,0:T(8,128)(2,1)}), bf16[16,1,160,256]{3,2,1,0:T(8,128)(2,1)}, u32[]{:S(2)}, u32[]{:S(2)}) async-start(bf16[16,1,160,256]{3,2,1,0:T(8,128)(2,1)} %broadcast_in_dim.196), calls=%async_computation.5 | async-start | bytes 2621440 | tf_op jit(solution)/shard_map/all_to_all | solution.py:61
  176.0 5.5 collective-permute-start
  181.6 9.1 %collective-permute-start.1 = (bf16[4,160,256]{2,1,0:T(8,128)(2,1)S(1)}, bf16[4,160,256]{2,1,0:T(8,128)(2,1)}, u32[]{:S(2)}, u32[]{:S(2)}) collective-permute-start(bf16[4,160,256]{2,1,0:T(8,128)(2,1)S(1)} %add_convert_fusion.7), channel_id=1, source_target_pairs={{0,2},{1,3},{2,0},{3,1},{4,6},{5,7},{6,4},{7,5},{8,10},{9,11},{10,... | collective-permute-start | bytes 983048 | tf_op jit(solution)/shard_map/ppermute | solution.py:68
  191.8 9.6 %collective-permute-start.2 = (bf16[4,160,256]{2,1,0:T(8,128)(2,1)S(1)}, bf16[4,160,256]{2,1,0:T(8,128)(2,1)S(1)}, u32[]{:S(2)}, u32[]{:S(2)}) collective-permute-start(bf16[4,160,256]{2,1,0:T(8,128)(2,1)S(1)} %add_convert_fusion.6), channel_id=1, source_target_pairs={{0,4},{1,5},{2,6},{3,7},{4,0},{5,1},{6,2},{7,3},{8,12},{9,13},{10,... | collective-permute-start | bytes 983048 | tf_op jit(solution)/shard_map/ppermute | solution.py:68
  203.9 13.8 %all-to-all-start.6 = ((bf16[16,1,80,256]{3,2,1,0:T(8,128)(2,1)}), bf16[16,1,80,256]{3,2,1,0:T(8,128)(2,1)S(1)}, u32[]{:S(2)}, u32[]{:S(2)}) async-start(bf16[16,1,80,256]{3,2,1,0:T(8,128)(2,1)} %bitcast.192), calls=%async_computation.6 | async-start | bytes 1310720 | tf_op jit(solution)/shard_map/all_to_all | solution.py:54
  218.6 13.4 %all-to-all-start.7 = ((bf16[16,1,80,256]{3,2,1,0:T(8,128)(2,1)}), bf16[16,1,80,256]{3,2,1,0:T(8,128)(2,1)S(1)}, u32[]{:S(2)}, u32[]{:S(2)}) async-start(bf16[16,1,80,256]{3,2,1,0:T(8,128)(2,1)} %broadcast_in_dim.205), calls=%async_computation.7 | async-start | bytes 1310720 | tf_op jit(solution)/shard_map/all_to_all | solution.py:61
  233.7 5.7 collective-permute-start.3
  239.5 5.5 collective-permute-start.4
  245.0 6.1 collective-permute-start.5
  253.2 11.9 %all-to-all-start.8 = ((bf16[16,1,40,256]{3,2,1,0:T(8,128)(2,1)}), bf16[16,1,40,256]{3,2,1,0:T(8,128)(2,1)}, u32[]{:S(2)}, u32[]{:S(2)}) async-start(bf16[16,1,40,256]{3,2,1,0:T(8,128)(2,1)} %bitcast.197), calls=%async_computation.8 | async-start | bytes 655360 | tf_op jit(solution)/shard_map/all_to_all | solution.py:54
  266.8 11.9 %all-to-all-start.9 = ((bf16[16,1,40,256]{3,2,1,0:T(8,128)(2,1)}), bf16[16,1,40,256]{3,2,1,0:T(8,128)(2,1)}, u32[]{:S(2)}, u32[]{:S(2)}) async-start(bf16[16,1,40,256]{3,2,1,0:T(8,128)(2,1)} %reduce_sum.257), calls=%async_computation.9 | async-start | bytes 655360 | tf_op jit(solution)/shard_map/all_to_all | solution.py:61
  281.1 5.4 collective-permute-start.6
  286.6 3.8 collective-permute-start.7
  290.3 5.1 collective-permute-start.8
  296.7 4.2 collective-permute-start.9
  301.0 5.8 collective-permute-start.10
  306.8 4.5 collective-permute-start.11
  311.4 7.2 %collective-permute-start.12 = (bf16[1,320,256]{2,1,0:T(8,128)(2,1)S(1)}, bf16[1,320,256]{2,1,0:T(8,128)(2,1)S(1)}, u32[]{:S(2)}, u32[]{:S(2)}) collective-permute-start(bf16[1,320,256]{2,1,0:T(8,128)(2,1)S(1)} %add_convert_fusion.13), channel_id=1, source_target_pairs={{0,64},{8,72},{16,80},{24,88},{32,96},{40,104},{48,112},{56,120},{... | collective-permute-start | bytes 491528 | tf_op jit(solution)/shard_map/ppermute | solution.py:68
  319.7 7.4 %collective-permute-start.13 = (bf16[1,160,256]{2,1,0:T(8,128)(2,1)S(1)}, bf16[1,160,256]{2,1,0:T(8,128)(2,1)S(1)}, u32[]{:S(2)}, u32[]{:S(2)}) collective-permute-start(bf16[1,160,256]{2,1,0:T(8,128)(2,1)S(1)} %fusion.61), channel_id=1, source_target_pairs={{0,1},{1,0},{2,3},{3,2},{4,5},{5,4},{6,7},{7,6},{8,9},{9,8},{10,11... | collective-permute-start | bytes 245768 | tf_op jit(solution)/shard_map/ppermute | solution.py:68
  327.1 3.8 collective-permute-start.14
  330.9 4.9 collective-permute-start.15
  361.9 6.0 collective-permute-start.16
  368.0 5.5 collective-permute-start.17
  373.5 6.1 collective-permute-start.18
  413.2 6.0 collective-permute-start.19
  419.3 9.0 %collective-permute-start.20 = (bf16[4,160,256]{2,1,0:T(8,128)(2,1)S(1)}, bf16[4,160,256]{2,1,0:T(8,128)(2,1)S(1)}, u32[]{:S(2)}, u32[]{:S(2)}) collective-permute-start(bf16[4,160,256]{2,1,0:T(8,128)(2,1)S(1)} %add_convert_fusion.4), channel_id=1, source_target_pairs={{0,2},{1,3},{2,0},{3,1},{4,6},{5,7},{6,4},{7,5},{8,10},{9,11},{10,... | collective-permute-start | bytes 983048 | tf_op jit(solution)/shard_map/ppermute | solution.py:68
  428.4 9.6 %collective-permute-start.21 = (bf16[4,160,256]{2,1,0:T(8,128)(2,1)S(1)}, bf16[4,160,256]{2,1,0:T(8,128)(2,1)S(1)}, u32[]{:S(2)}, u32[]{:S(2)}) collective-permute-start(bf16[4,160,256]{2,1,0:T(8,128)(2,1)S(1)} %add_convert_fusion.3), channel_id=1, source_target_pairs={{0,4},{1,5},{2,6},{3,7},{4,0},{5,1},{6,2},{7,3},{8,12},{9,13},{10,... | collective-permute-start | bytes 983048 | tf_op jit(solution)/shard_map/ppermute | solution.py:68
  488.8 19.2 %all-to-all-start.16 = ((bf16[8,1,160,256]{3,2,1,0:T(8,128)(2,1)}), bf16[8,1,160,256]{3,2,1,0:T(8,128)(2,1)S(1)}, u32[]{:S(2)}, u32[]{:S(2)}) async-start(bf16[8,1,160,256]{3,2,1,0:T(8,128)(2,1)} %fusion.53), calls=%async_computation.16 | async-start | bytes 1310720 | tf_op jit(solution)/shard_map/all_to_all | solution.py:54
  508.9 15.2 %all-to-all-start.17 = ((bf16[8,1,160,256]{3,2,1,0:T(8,128)(2,1)}), bf16[8,1,160,256]{3,2,1,0:T(8,128)(2,1)S(1)}, u32[]{:S(2)}, u32[]{:S(2)}) async-start(bf16[8,1,160,256]{3,2,1,0:T(8,128)(2,1)} %reduce_sum.264), calls=%async_computation.17 | async-start | bytes 1310720 | tf_op jit(solution)/shard_map/all_to_all | solution.py:61
  629.1 13.2 %all-to-all-start.22 = ((bf16[4,1,2,160,256]{4,3,2,1,0:T(8,128)(2,1)}), bf16[4,1,2,160,256]{4,3,2,1,0:T(8,128)(2,1)S(1)}, u32[]{:S(2)}, u32[]{:S(2)}) async-start(bf16[4,1,2,160,256]{4,3,2,1,0:T(8,128)(2,1)} %broadcast_in_dim.321), calls=%async_computation.22 | async-start | bytes 1310720 | tf_op jit(solution)/shard_map/all_to_all | solution.py:84
  (29 other events, 456.1 us)
